TPU v7x, 32 devices: a whole 2x2x4 slice. The times are simulated.
32 devices in a mesh: depth: 8 (over z, x), tile: 4 (over y, core).
Axes of the slice: x: 2, y: 2, z: 4, core: 2. Of those that a mesh axis runs over, the one named last changes fastest.
Arguments:
- hologram: bfloat16 [2, 256, 4096], P(None, 'tile'), may hold values from -6 to 6
- kernel: bfloat16 [32, 2, 64], P('depth'), may hold values from -0.5 to 0.5
- depth_prior: float32 [32, 256], P('depth', 'tile'), may hold values from -6 to 320
Outputs:
- plane_stack: float32 [32, 256, 4096], P('depth', 'tile')
- joined_intensity: float32 [256, 4096], P('tile', 'depth')
- mean_depth: float32 [256, 4096], P('tile', 'depth')
All inputs are finite; a program needn't handle non-finite values.
Results may differ from a plain program's by a relative error of at most 0.0031.
Values may be sent and summed in bfloat16 or wider, within the bound.
No kernel may reach another device: no remote copies, remote signals or barrier semaphores. Data moves between devices by JAX's collectives and lax.ppermute only.
A program may use at most 128 MiB of HBM per device.

v0:
```python
import functools

import jax
import jax.numpy as jnp
from jax import lax
from jax.experimental import pallas as pl
from jax.experimental.pallas import tpu as pltpu
from jax.sharding import PartitionSpec as P

TAPS = 64
LANE = 128
SPAN = 2 * LANE


def propagate_kernel(taps_ref, window_ref, out_ref, *, n_out, n_in, block_count):
    def skew(taps):
        return pltpu.roll(jnp.broadcast_to(taps, (LANE, SPAN)), 0, 1, stride=1, stride_axis=0)

    skew_re = skew(taps_ref[0, 0:1, :])
    skew_im = skew(taps_ref[0, 1:2, :])
    rows_re = skew_re[:n_out, :n_in]
    rows_im = skew_im[:n_out, :n_in]
    rows_matrix = jnp.concatenate(
        [
            jnp.concatenate([rows_re, -rows_im], axis=1),
            jnp.concatenate([rows_im, rows_re], axis=1),
        ],
        axis=0,
    ).astype(jnp.bfloat16)
    across = jnp.dot(rows_matrix, window_ref[...], preferred_element_type=jnp.float32)
    across = across.astype(jnp.bfloat16)
    across_re = across[:n_out]
    across_im = across[n_out:]

    def stacked(signal, first):
        return jnp.concatenate(
            [signal[:, LANE * b : LANE * (b + 1)] for b in range(first, first + block_count)], axis=0
        )

    blocks = jnp.concatenate(
        [stacked(across_re, 0), stacked(across_re, 1), stacked(across_im, 0), stacked(across_im, 1)],
        axis=1,
    )
    near_re = skew_re[:, :LANE].T
    far_re = skew_re[:, LANE:].T
    near_im = skew_im[:, :LANE].T
    far_im = skew_im[:, LANE:].T
    cols_matrix = jnp.concatenate(
        [
            jnp.concatenate([near_re, near_im], axis=1),
            jnp.concatenate([far_re, far_im], axis=1),
            jnp.concatenate([-near_im, near_re], axis=1),
            jnp.concatenate([-far_im, far_re], axis=1),
        ],
        axis=0,
    ).astype(jnp.bfloat16)
    field = jnp.dot(blocks, cols_matrix, preferred_element_type=jnp.float32)
    intensity = field[:, :LANE] * field[:, :LANE] + field[:, LANE:] * field[:, LANE:]
    for b in range(block_count):
        out_ref[0, :, LANE * b : LANE * (b + 1)] = intensity[n_out * b : n_out * (b + 1)]


def propagate(taps, window, n_out):
    planes = taps.shape[0]
    _, n_in, width = window.shape
    block_count = width // LANE - 1
    stacked = window.reshape(2 * n_in, width)
    body = functools.partial(
        propagate_kernel, n_out=n_out, n_in=n_in, block_count=block_count
    )
    flops = 2 * planes * (2 * n_out * 2 * n_in * width + block_count * n_out * 4 * LANE * SPAN)
    return pl.pallas_call(
        body,
        grid=(planes,),
        in_specs=[
            pl.BlockSpec((1, 2, SPAN), lambda p: (p, 0, 0)),
            pl.BlockSpec((2 * n_in, width), lambda p: (0, 0)),
        ],
        out_specs=pl.BlockSpec((1, n_out, block_count * LANE), lambda p: (p, 0, 0)),
        out_shape=jax.ShapeDtypeStruct((planes, n_out, block_count * LANE), jnp.float32),
        cost_estimate=pl.CostEstimate(
            flops=flops,
            transcendentals=0,
            bytes_accessed=stacked.size * 2 + planes * n_out * block_count * LANE * 4,
        ),
    )(taps, stacked)


def gather_depth(block):
    count = lax.axis_size("depth")
    have = 1
    while have < count:
        need = min(have, count - have)
        moved = lax.ppermute(
            block[: need * (block.shape[0] // have)],
            "depth",
            [((j + have) % count, j) for j in range(count)],
        )
        block = jnp.concatenate([block, moved], axis=0)
        have += need
    return block


def sharpness(rimmed):
    vertical = rimmed[:, :-2] + 2.0 * rimmed[:, 1:-1] + rimmed[:, 2:]
    grad_x = vertical[:, :, 2:] - vertical[:, :, :-2]
    horizontal = rimmed[:, :, :-2] + 2.0 * rimmed[:, :, 1:-1] + rimmed[:, :, 2:]
    grad_y = horizontal[:, 2:] - horizontal[:, :-2]
    return grad_x * grad_x + grad_y * grad_y


def local(hologram, kernel, depth_prior):
    _, rows, col_total = hologram.shape
    local_planes = kernel.shape[0]
    depth_count = lax.axis_size("depth")
    tile_count = lax.axis_size("tile")
    depth_at = lax.axis_index("depth")
    tile_at = lax.axis_index("tile")
    planes_total = local_planes * depth_count
    own_cols = col_total // depth_count
    row_total = rows * tile_count
    half_taps = TAPS // 2

    taps = jnp.pad(kernel.astype(jnp.float32), ((0, 0), (0, 0), (0, SPAN - TAPS)))
    packed = jnp.concatenate([taps.reshape(local_planes, 2 * SPAN), depth_prior], axis=1)
    packed_all = gather_depth(packed)
    taps_all = packed_all[:, : 2 * SPAN].reshape(planes_total, 2, SPAN)
    prior_all = packed_all[:, 2 * SPAN :]
    owner = (depth_at + jnp.arange(planes_total) // local_planes) % depth_count
    plane_at = owner * local_planes + jnp.arange(planes_total) % local_planes

    halo = 48
    above = lax.ppermute(
        hologram[:, rows - halo :], "tile", [(i, i + 1) for i in range(tile_count - 1)]
    )
    below = lax.ppermute(hologram[:, :halo], "tile", [(i + 1, i) for i in range(tile_count - 1)])
    extended = jnp.concatenate([above, hologram, below], axis=1)

    window = extended[:, halo - half_taps : halo - half_taps + LANE]
    window = jnp.pad(window, ((0, 0), (0, 0), (half_taps, LANE - half_taps)))
    plane_stack = propagate(taps, window, rows)

    lead_rows = 8
    n_out = rows + 2 * lead_rows
    first = halo - half_taps - lead_rows
    window = extended[:, first : first + n_out + TAPS - 1]
    lead = LANE // 2 + half_taps
    width = own_cols + 2 * LANE
    window = jnp.pad(
        window, ((0, 0), (0, SPAN - window.shape[1]), (lead, width - lead))
    )
    window = lax.dynamic_slice_in_dim(window, depth_at * own_cols, width, axis=2)
    field = propagate(taps_all, window, n_out)
    start = LANE // 2 - 1
    rimmed = field[:, lead_rows - 1 : lead_rows + rows + 1, start : start + own_cols + 2]
    row_at = tile_at * rows - 1 + jnp.arange(rows + 2)
    col_at = depth_at * own_cols - 1 + jnp.arange(own_cols + 2)
    inside = ((row_at >= 0) & (row_at < row_total))[:, None] & (
        (col_at >= 0) & (col_at < col_total)
    )[None, :]
    rimmed = jnp.where(inside[None], rimmed, 0.0)
    score = prior_all[:, :, None] + jnp.log(1.0 + sharpness(rimmed))
    intensity = rimmed[:, 1:-1, 1:-1]
    peak = jnp.max(score, axis=0)
    fresh = jnp.exp(score - peak[None])
    depth_values = (plane_at.astype(jnp.float32) + 0.5) / planes_total
    weight_sum = jnp.sum(fresh, axis=0)
    weighted = jnp.sum(fresh * intensity, axis=0)
    placed = jnp.sum(fresh * depth_values[:, None, None], axis=0)
    return (plane_stack, weighted / weight_sum, placed / weight_sum)


def solution(mesh):
    in_specs = (P(None, "tile", None), P("depth", None, None), P("depth", "tile"))
    out_specs = (P("depth", "tile", None), P("tile", "depth"), P("tile", "depth"))
    return jax.shard_map(local, mesh=mesh, in_specs=in_specs, out_specs=out_specs, check_vma=False)
```

profile of v0, /device:TPU:4, one launch (start us, length us, event | category | flops | bytes accessed | tf_op | source)
XLA Modules:
  0.0 85.7 jit_solution(11652209544497803149)
XLA Ops:
  0.6 1.3 %fusion.13 = (f32[1,4,2,256]{3,2,1,0:T(2,128)S(1)}, f32[4,2,256]{2,1,0:T(2,128)}) fusion(bf16[4,2,64]{2,1,0:T(2,128)(2,1)} %param.4), kind=kLoop, calls=%fused_computation.44 | loop fusion | flops 2048 | bytes 17408
  1.9 0.7 constant_dynamic-update-slice_fusion.3
  2.6 4.5 %collective-permute-start.2 = (f32[4,576]{1,0:T(4,128)S(1)}, f32[4,576]{1,0:T(4,128)S(1)}, u32[]{:S(2)}, u32[]{:S(2)}) collective-permute-start(f32[4,576]{1,0:T(4,128)S(1)} %constant_dynamic-update-slice_fusion.3), channel_id=1, source_target_pairs={{4,0},{8,4},{12,8},{16,12},{20,16},{24,20},{28,24},{0,28},{5,1},{9... | collective-permute-start | bytes 27656 | tf_op jit(solution)/shard_map/ppermute | solution.py:94
  7.1 2.4 %fusion.23 = (bf16[2,48,4096]{2,1,0:T(8,128)(2,1)}, bf16[2,48,4096]{2,1,0:T(8,128)(2,1)S(1)}) fusion(bf16[2,64,4096]{2,1,0:T(8,128)(2,1)} %param.3), kind=kLoop, calls=%fused_computation.56 | loop fusion | bytes 3145728 | tf_op jit(solution)/shard_map/slice | solution.py:136
  9.5 1.9 %collective-permute-start = (bf16[2,48,4096]{2,1,0:T(8,128)(2,1)S(1)}, bf16[2,48,4096]{2,1,0:T(8,128)(2,1)}, u32[]{:S(2)}, u32[]{:S(2)}) collective-permute-start(bf16[2,48,4096]{2,1,0:T(8,128)(2,1)S(1)} %get-tuple-element.9), channel_id=1, source_target_pairs={{0,1},{1,2},{2,3},{4,5},{5,6},{6,7},{8,9},{9,10},{10,11},{12,13},{... | collective-permute-start | bytes 2359304 | tf_op jit(solution)/shard_map/ppermute | solution.py:133
  11.4 3.6 %collective-permute-start.1 = (bf16[2,48,4096]{2,1,0:T(8,128)(2,1)}, bf16[2,48,4096]{2,1,0:T(8,128)(2,1)S(1)}, u32[]{:S(2)}, u32[]{:S(2)}) collective-permute-start(bf16[2,48,4096]{2,1,0:T(8,128)(2,1)} %get-tuple-element.8), channel_id=1, source_target_pairs={{1,0},{2,1},{3,2},{5,4},{6,5},{7,6},{9,8},{10,9},{11,10},{13,12},{... | collective-permute-start | bytes 2359304 | tf_op jit(solution)/shard_map/ppermute | solution.py:136
  15.2 0.5 collective-permute-start.3
  15.8 3.2 %collective-permute-done.3 = f32[8,576]{1,0:T(8,128)S(1)} collective-permute-done((f32[8,576]{1,0:T(8,128)S(1)}, f32[8,576]{1,0:T(8,128)S(1)}, u32[]{:S(2)}, u32[]{:S(2)}) %collective-permute-start.3) | collective-permute-done | bytes 18464 | tf_op jit(solution)/shard_map/ppermute | solution.py:94
  19.1 4.9 %collective-permute-done.4 = f32[16,576]{1,0:T(8,128)S(1)} collective-permute-done((f32[16,576]{1,0:T(8,128)S(1)}, f32[16,576]{1,0:T(8,128)S(1)}, u32[]{:S(2)}, u32[]{:S(2)}) %collective-permute-start.4) | collective-permute-done | bytes 36896 | tf_op jit(solution)/shard_map/ppermute | solution.py:94
  24.0 0.7 reshape.102.taps_ref
  24.7 1.2 %constant_dynamic-update-slice_fusion.2 = bf16[2,160,4096]{2,1,0:T(8,128)(2,1)S(1)} fusion(bf16[2,48,4096]{2,1,0:T(8,128)(2,1)} %collective-permute-done), kind=kLoop, calls=%fused_computation.30 | loop fusion | bytes 1572864
  25.9 1.3 %constant_dynamic-update-slice_fusion.1 = bf16[2,160,4096]{2,1,0:T(8,128)(2,1)S(1)} fusion(bf16[2,160,4096]{2,1,0:T(8,128)(2,1)S(1)} %constant_dynamic-update-slice_fusion.2, bf16[2,64,4096]{2,1,0:T(8,128)(2,1)} %param.3), kind=kLoop, calls=%fused_computation.29 | loop fusion | bytes 2097152
  27.2 0.2 slice.73
  27.5 1.4 %pad_dynamic-slice_fusion = bf16[2,256,768]{2,1,0:T(8,128)(2,1)} fusion(s32[]{:T(128)S(6)} %select_n.35, bf16[2,143,4096]{2,1,0:T(8,128)(2,1)S(1)} %slice.73), kind=kLoop, calls=%fused_computation.4 | loop fusion | bytes 3129348 | tf_op jit(solution)/shard_map/dynamic_slice | solution.py:152
  28.8 23.2 %shard_map.59 = f32[32,80,640]{2,1,0:T(8,128)} custom-call(f32[32,2,256]{2,1,0:T(2,128)} %reshape.102.taps_ref, bf16[512,768]{1,0:T(8,128)(2,1)} %bitcast.8), custom_call_target="tpu_custom_call" | custom-call | flops 7381975040 | bytes 7340032 | tf_op jit(solution)/shard_map/pallas_call | solution.py:72
  52.0 4.9 %slice_select_fusion = f32[32,66,514]{2,1,0:T(8,128)S(1)} fusion(f32[32,80,640]{2,1,0:T(8,128)} %shard_map.59, pred[66,514]{1,0:T(8,128)(4,1)S(1)} %broadcast_and_fusion), kind=kLoop, calls=%fused_computation | loop fusion | flops 1085568 | bytes 8718468 | tf_op jit(solution)/shard_map/jit(_where)/select_n | solution.py:161
  56.9 4.1 %slice_add_fusion = f32[32,64,514]{2,1,0:T(8,128)} fusion(f32[32,66,514]{2,1,0:T(8,128)S(1)} %slice_select_fusion), kind=kLoop, calls=%fused_computation.1 | loop fusion | flops 3158016 | bytes 16842752 | tf_op jit(solution)/shard_map/add | solution.py:105
  61.1 4.7 %slice_add_fusion.1 = f32[32,66,512]{2,1,0:T(8,128)} fusion(f32[32,66,514]{2,1,0:T(8,128)S(1)} %slice_select_fusion), kind=kLoop, calls=%fused_computation.5 | loop fusion | flops 3244032 | bytes 17301504 | tf_op jit(solution)/shard_map/add | solution.py:107
  65.8 0.2 slice.72
  66.0 2.2 %pad.16 = bf16[2,128,4224]{2,1,0:T(8,128)(2,1)} pad(bf16[2,128,4096]{2,1,0:T(8,128)(2,1)S(1)} %slice.72, bf16[]{:T(256)} %constant.63.clone.1), padding=0_0x0_0x32_96 | pad | bytes 4259842 | tf_op jit(solution)/shard_map/jit(_pad)/pad | solution.py:140
  68.2 7.0 %shard_map.58 = f32[4,64,4096]{2,1,0:T(8,128)} custom-call(f32[4,2,256]{2,1,0:T(2,128)} %get-tuple-element.13.taps_ref, bf16[256,4224]{1,0:T(8,128)(2,1)} %bitcast.7), custom_call_target="tpu_custom_call" | custom-call | flops 3254779904 | bytes 6356992 | tf_op jit(solution)/shard_map/pallas_call | solution.py:72
  75.2 7.7 %fusion.21 = (f32[64,512]{1,0:T(8,128)S(1)}, f32[32,64,512]{2,1,0:T(8,128)S(1)}) fusion(f32[32,66,512]{2,1,0:T(8,128)} %slice_add_fusion.1, f32[32,64,514]{2,1,0:T(8,128)} %slice_add_fusion, f32[32,64]{1,0:T(8,128)S(1)} %pad_maximum_fusion.5), kind=kLoop, calls=%fused_computation.55 | loop fusion | flops 8355840 | bytes 21110784 | tf_op jit(solution)/shard_map/reduce_max | solution.py:164
  82.9 2.1 %multiply_reduce_fusion = (f32[64,512]{1,0:T(8,128)S(1)}, f32[64,512]{1,0:T(8,128)S(1)}, f32[64,512]{1,0:T(8,128)S(1)}) fusion(f32[32,64,512]{2,1,0:T(8,128)S(1)} %get-tuple-element.7, f32[32]{0:T(128)S(1)} %fusion.17, f32[64,512]{1,0:T(8,128)S(1)} %get-tuple-element.6, f32[32,66,514]{2,1,0:T(8,128)S(1)} %bitcast.6), kind=kLoop, calls=%fused_computation.18 | loop fusion | flops 6193152 | bytes 8913024 | tf_op jit(solution)/shard_map/reduce_sum | solution.py:169
  85.0 0.7 fusion.24
  (22 shorter events, 0.5 us)
Async XLA Ops:
  2.6 12.5 %collective-permute-start.2 = (f32[4,576]{1,0:T(4,128)S(1)}, f32[4,576]{1,0:T(4,128)S(1)}, u32[]{:S(2)}, u32[]{:S(2)}) collective-permute-start(f32[4,576]{1,0:T(4,128)S(1)} %constant_dynamic-update-slice_fusion.3), channel_id=1, source_target_pairs={{4,0},{8,4},{12,8},{16,12},{20,16},{24,20},{28,24},{0,28},{5,1},{9... | collective-permute-start | bytes 27656 | tf_op jit(solution)/shard_map/ppermute | solution.py:94
  9.5 15.2 %collective-permute-start = (bf16[2,48,4096]{2,1,0:T(8,128)(2,1)S(1)}, bf16[2,48,4096]{2,1,0:T(8,128)(2,1)}, u32[]{:S(2)}, u32[]{:S(2)}) collective-permute-start(bf16[2,48,4096]{2,1,0:T(8,128)(2,1)S(1)} %get-tuple-element.9), channel_id=1, source_target_pairs={{0,1},{1,2},{2,3},{4,5},{5,6},{6,7},{8,9},{9,10},{10,11},{12,13},{... | collective-permute-start | bytes 2359304 | tf_op jit(solution)/shard_map/ppermute | solution.py:133
  11.4 15.7 %collective-permute-start.1 = (bf16[2,48,4096]{2,1,0:T(8,128)(2,1)}, bf16[2,48,4096]{2,1,0:T(8,128)(2,1)S(1)}, u32[]{:S(2)}, u32[]{:S(2)}) collective-permute-start(bf16[2,48,4096]{2,1,0:T(8,128)(2,1)} %get-tuple-element.8), channel_id=1, source_target_pairs={{1,0},{2,1},{3,2},{5,4},{6,5},{7,6},{9,8},{10,9},{11,10},{13,12},{... | collective-permute-start | bytes 2359304 | tf_op jit(solution)/shard_map/ppermute | solution.py:136
  15.2 3.8 %collective-permute-start.3 = (f32[8,576]{1,0:T(8,128)S(1)}, f32[8,576]{1,0:T(8,128)S(1)}, u32[]{:S(2)}, u32[]{:S(2)}) collective-permute-start(f32[8,576]{1,0:T(8,128)S(1)} %pad_maximum_fusion.4), channel_id=1, source_target_pairs={{8,0},{12,4},{16,8},{20,12},{24,16},{28,20},{0,24},{4,28},{9,1},{1... | collective-permute-start | bytes 55304 | tf_op jit(solution)/shard_map/ppermute | solution.py:94
  19.0 5.0 %collective-permute-start.4 = (f32[16,576]{1,0:T(8,128)S(1)}, f32[16,576]{1,0:T(8,128)S(1)}, u32[]{:S(2)}, u32[]{:S(2)}) collective-permute-start(f32[16,576]{1,0:T(8,128)S(1)} %pad_maximum_fusion.3), channel_id=1, source_target_pairs={{16,0},{20,4},{24,8},{28,12},{0,16},{4,20},{8,24},{12,28},{17,1},{... | collective-permute-start | bytes 110600 | tf_op jit(solution)/shard_map/ppermute | solution.py:94
  56.9 4.2 %copy-start = (f32[32,66,514]{2,1,0:T(8,128)}, f32[32,66,514]{2,1,0:T(8,128)S(1)}, u32[]{:S(2)}) copy-start(f32[32,66,514]{2,1,0:T(8,128)S(1)} %slice_select_fusion) | copy-start | bytes 13026820
  68.2 14.7 %slice-start = ((s8[5898240]{0:T(1024)(128)(4,1)}), s8[1703936]{0:T(1024)(128)(4,1)S(1)}, s32[]{:S(2)}) async-start(s8[5898240]{0:T(1024)(128)(4,1)} %bitcast.5), calls=%async_computation | async-start | bytes 3407872
  75.2 7.7 %slice-start.1 = ((s8[5898240]{0:T(1024)(128)(4,1)}), s8[4194304]{0:T(1024)(128)(4,1)S(1)}, s32[]{:S(2)}) async-start(s8[5898240]{0:T(1024)(128)(4,1)} %bitcast.5), calls=%async_computation.1 | async-start | bytes 8388608
where the time goes:
time: 87.4 us; the launch traced here: 85.7 us
  Pallas kernels  30.2 us (35%)
  other arithmetic  25.5 us (29%)
  starting transfers between devices  10.7 us (12%)
  local copies, waits for them, and re-layouts  10.5 us (12%)
  waiting for transfers between devices  8.11 us (9%)
    pallas_call x2, Pallas kernels, propagate(): pl.pallas_call(body, grid=(planes,), in_specs=[pl.BlockSpec((1, 2, SPAN),...  30.2 us
    ppermute x3, waiting for transfers between devices, gather_depth(): lax.ppermute(block[:need * (block.shape[0] // have)], 'depth', [((j + hav...  8.11 us
    reduce_max x1, other arithmetic, local(): peak = jnp.max(score, axis=0)  7.65 us
    ppermute x3, starting transfers between devices, gather_depth(): lax.ppermute(block[:need * (block.shape[0] // have)], 'depth', [((j + hav...  5.1 us
    select_n x1, other arithmetic, local(): rimmed = jnp.where(inside[None], rimmed, 0.0)  4.86 us
    add x1, other arithmetic, sharpness(): horizontal = rimmed[:, :, :-2] + 2.0 * rimmed[:, :, 1:-1] + rimmed[:, :, 2:]  4.7 us
    add x1, other arithmetic, sharpness(): vertical = rimmed[:, :-2] + 2.0 * rimmed[:, 1:-1] + rimmed[:, 2:]  4.07 us
    ppermute x1, starting transfers between devices, local(): lax.ppermute(hologram[:, :halo], 'tile', [(i + 1, i) for i in range(tile_...  3.64 us
  transfers between devices with their start and end apart: 5, of which 2 were waited for; matrix products, arithmetic and copies ran while one was open for 7% of the time, Pallas kernels for 0%

commit v1 on v0

--- a/solution.py
+++ b/solution.py
@@ -12,7 +12,7 @@
 SPAN = 2 * LANE
 
 
-def propagate_kernel(taps_ref, window_ref, out_ref, *, n_out, n_in, block_count):
+def stacked_intensity(taps_ref, window_ref, n_out, n_in, block_count):
     def skew(taps):
         return pltpu.roll(jnp.broadcast_to(taps, (LANE, SPAN)), 0, 1, stride=1, stride_axis=0)
 
@@ -55,9 +55,62 @@
         axis=0,
     ).astype(jnp.bfloat16)
     field = jnp.dot(blocks, cols_matrix, preferred_element_type=jnp.float32)
-    intensity = field[:, :LANE] * field[:, :LANE] + field[:, LANE:] * field[:, LANE:]
+    return field[:, :LANE] * field[:, :LANE] + field[:, LANE:] * field[:, LANE:]
+
+
+def propagate_kernel(taps_ref, window_ref, out_ref, *, n_out, n_in, block_count):
+    intensity = stacked_intensity(taps_ref, window_ref, n_out, n_in, block_count)
     for b in range(block_count):
         out_ref[0, :, LANE * b : LANE * (b + 1)] = intensity[n_out * b : n_out * (b + 1)]
+
+
+def joining_kernel(
+    corner_ref, taps_ref, prior_ref, depth_ref, window_ref, joined_ref, mean_ref,
+    peak_ref, total_ref, weighted_ref, placed_ref, *, n_out, n_in, block_count, bounds,
+):
+    plane = pl.program_id(0)
+    stacked = stacked_intensity(taps_ref, window_ref, n_out, n_in, block_count)
+    intensity = jnp.concatenate(
+        [stacked[n_out * b : n_out * (b + 1)] for b in range(block_count)], axis=1
+    )
+    height, width = intensity.shape
+    row_at = corner_ref[0] + lax.broadcasted_iota(jnp.int32, (height, width), 0)
+    col_at = corner_ref[1] + lax.broadcasted_iota(jnp.int32, (height, width), 1)
+    inside = (row_at >= 0) & (row_at < bounds[0]) & (col_at >= 0) & (col_at < bounds[1])
+    intensity = jnp.where(inside, intensity, 0.0)
+    vertical = (
+        pltpu.roll(intensity, 1, 0) + 2.0 * intensity + pltpu.roll(intensity, height - 1, 0)
+    )
+    grad_x = pltpu.roll(vertical, width - 1, 1) - pltpu.roll(vertical, 1, 1)
+    horizontal = (
+        pltpu.roll(intensity, 1, 1) + 2.0 * intensity + pltpu.roll(intensity, width - 1, 1)
+    )
+    grad_y = pltpu.roll(horizontal, height - 1, 0) - pltpu.roll(horizontal, 1, 0)
+    score = prior_ref[0] + jnp.log(1.0 + (grad_x * grad_x + grad_y * grad_y))
+    depth_value = depth_ref[0]
+
+    @pl.when(plane == 0)
+    def _():
+        peak_ref[...] = score
+        total_ref[...] = jnp.ones_like(score)
+        weighted_ref[...] = intensity
+        placed_ref[...] = jnp.broadcast_to(depth_value, score.shape)
+
+    @pl.when(plane > 0)
+    def _():
+        peak_now = peak_ref[...]
+        peak_next = jnp.maximum(peak_now, score)
+        factor = jnp.exp(peak_now - peak_next)
+        fresh = jnp.exp(score - peak_next)
+        peak_ref[...] = peak_next
+        total_ref[...] = total_ref[...] * factor + fresh
+        weighted_ref[...] = weighted_ref[...] * factor + fresh * intensity
+        placed_ref[...] = placed_ref[...] * factor + fresh * depth_value
+
+    @pl.when(plane == pl.num_programs(0) - 1)
+    def _():
+        joined_ref[...] = weighted_ref[...] / total_ref[...]
+        mean_ref[...] = placed_ref[...] / total_ref[...]
 
 
 def propagate(taps, window, n_out):
@@ -86,27 +139,51 @@
     )(taps, stacked)
 
 
+def joining(corner, taps, prior, depth_values, window, n_out, bounds):
+    planes = taps.shape[0]
+    _, n_in, width = window.shape
+    block_count = width // LANE - 1
+    stacked = window.reshape(2 * n_in, width)
+    body = functools.partial(
+        joining_kernel, n_out=n_out, n_in=n_in, block_count=block_count, bounds=bounds
+    )
+    out_cols = block_count * LANE
+    flops = 2 * planes * (2 * n_out * 2 * n_in * width + block_count * n_out * 4 * LANE * SPAN)
+    grid_spec = pltpu.PrefetchScalarGridSpec(
+        num_scalar_prefetch=1,
+        grid=(planes,),
+        in_specs=[
+            pl.BlockSpec((1, 2, SPAN), lambda p, c: (p, 0, 0)),
+            pl.BlockSpec((1, n_out, 1), lambda p, c: (p, 0, 0)),
+            pl.BlockSpec((1, 1, 1), lambda p, c: (p, 0, 0)),
+            pl.BlockSpec((2 * n_in, width), lambda p, c: (0, 0)),
+        ],
+        out_specs=[
+            pl.BlockSpec((n_out, out_cols), lambda p, c: (0, 0)),
+            pl.BlockSpec((n_out, out_cols), lambda p, c: (0, 0)),
+        ],
+        scratch_shapes=[pltpu.VMEM((n_out, out_cols), jnp.float32) for _ in range(4)],
+    )
+    return pl.pallas_call(
+        body,
+        grid_spec=grid_spec,
+        out_shape=[jax.ShapeDtypeStruct((n_out, out_cols), jnp.float32)] * 2,
+        compiler_params=pltpu.CompilerParams(dimension_semantics=("arbitrary",)),
+        cost_estimate=pl.CostEstimate(
+            flops=flops,
+            transcendentals=3 * planes * n_out * out_cols,
+            bytes_accessed=stacked.size * 2 + 2 * n_out * out_cols * 4,
+        ),
+    )(corner, taps, prior, depth_values, stacked)
+
+
 def gather_depth(block):
     count = lax.axis_size("depth")
-    have = 1
-    while have < count:
-        need = min(have, count - have)
-        moved = lax.ppermute(
-            block[: need * (block.shape[0] // have)],
-            "depth",
-            [((j + have) % count, j) for j in range(count)],
-        )
-        block = jnp.concatenate([block, moved], axis=0)
-        have += need
-    return block
-
-
-def sharpness(rimmed):
-    vertical = rimmed[:, :-2] + 2.0 * rimmed[:, 1:-1] + rimmed[:, 2:]
-    grad_x = vertical[:, :, 2:] - vertical[:, :, :-2]
-    horizontal = rimmed[:, :, :-2] + 2.0 * rimmed[:, :, 1:-1] + rimmed[:, :, 2:]
-    grad_y = horizontal[:, 2:] - horizontal[:, :-2]
-    return grad_x * grad_x + grad_y * grad_y
+    moved = [
+        lax.ppermute(block, "depth", [((j + shift) % count, j) for j in range(count)])
+        for shift in range(1, count)
+    ]
+    return jnp.concatenate([block, *moved], axis=0)
 
 
 def local(hologram, kernel, depth_prior):
@@ -124,8 +201,6 @@
     taps = jnp.pad(kernel.astype(jnp.float32), ((0, 0), (0, 0), (0, SPAN - TAPS)))
     packed = jnp.concatenate([taps.reshape(local_planes, 2 * SPAN), depth_prior], axis=1)
     packed_all = gather_depth(packed)
-    taps_all = packed_all[:, : 2 * SPAN].reshape(planes_total, 2, SPAN)
-    prior_all = packed_all[:, 2 * SPAN :]
     owner = (depth_at + jnp.arange(planes_total) // local_planes) % depth_count
     plane_at = owner * local_planes + jnp.arange(planes_total) % local_planes
 
@@ -139,6 +214,9 @@
     window = extended[:, halo - half_taps : halo - half_taps + LANE]
     window = jnp.pad(window, ((0, 0), (0, 0), (half_taps, LANE - half_taps)))
     plane_stack = propagate(taps, window, rows)
+    plane_stack, packed_all = lax.optimization_barrier((plane_stack, packed_all))
+    taps_all = packed_all[:, : 2 * SPAN].reshape(planes_total, 2, SPAN)
+    prior_all = packed_all[:, 2 * SPAN :]
 
     lead_rows = 8
     n_out = rows + 2 * lead_rows
@@ -150,24 +228,18 @@
         window, ((0, 0), (0, SPAN - window.shape[1]), (lead, width - lead))
     )
     window = lax.dynamic_slice_in_dim(window, depth_at * own_cols, width, axis=2)
-    field = propagate(taps_all, window, n_out)
-    start = LANE // 2 - 1
-    rimmed = field[:, lead_rows - 1 : lead_rows + rows + 1, start : start + own_cols + 2]
-    row_at = tile_at * rows - 1 + jnp.arange(rows + 2)
-    col_at = depth_at * own_cols - 1 + jnp.arange(own_cols + 2)
-    inside = ((row_at >= 0) & (row_at < row_total))[:, None] & (
-        (col_at >= 0) & (col_at < col_total)
-    )[None, :]
-    rimmed = jnp.where(inside[None], rimmed, 0.0)
-    score = prior_all[:, :, None] + jnp.log(1.0 + sharpness(rimmed))
-    intensity = rimmed[:, 1:-1, 1:-1]
-    peak = jnp.max(score, axis=0)
-    fresh = jnp.exp(score - peak[None])
-    depth_values = (plane_at.astype(jnp.float32) + 0.5) / planes_total
-    weight_sum = jnp.sum(fresh, axis=0)
-    weighted = jnp.sum(fresh * intensity, axis=0)
-    placed = jnp.sum(fresh * depth_values[:, None, None], axis=0)
-    return (plane_stack, weighted / weight_sum, placed / weight_sum)
+    corner = jnp.stack([tile_at * rows - lead_rows, depth_at * own_cols - LANE // 2]).astype(
+        jnp.int32
+    )
+    prior_rows = jnp.pad(prior_all, ((0, 0), (lead_rows, lead_rows)))[:, :, None]
+    depth_values = ((plane_at.astype(jnp.float32) + 0.5) / planes_total)[:, None, None]
+    joined, mean_depth = joining(
+        corner, taps_all, prior_rows, depth_values, window, n_out, (row_total, col_total)
+    )
+    start = LANE // 2
+    joined = joined[lead_rows : lead_rows + rows, start : start + own_cols]
+    mean_depth = mean_depth[lead_rows : lead_rows + rows, start : start + own_cols]
+    return (plane_stack, joined, mean_depth)
 
 
 def solution(mesh):

time: 87.4 us -> 87.3 us (level)
  the two profiles are of different devices: /device:TPU:4 before, /device:TPU:1 now
where the time goes in v1:
time: 87.3 us; the launch traced here: 86.9 us
  Pallas kernels  43.7 us (50%)
  starting transfers between devices  17.5 us (20%)
  local copies, waits for them, and re-layouts  15 us (17%)
  waiting for transfers between devices  8.06 us (9%)
  other arithmetic  1.83 us (2%)
    pallas_call x1, Pallas kernels, joining(): pl.pallas_call(body, grid_spec=grid_spec, out_shape=[jax.ShapeDtypeStruct...  36.9 us
    ppermute x7, starting transfers between devices, gather_depth(): lax.ppermute(block, 'depth', [((j + shift) % count, j) for j in range(cou...  10.4 us
    ppermute x1, waiting for transfers between devices, local(): lax.ppermute(hologram[:, :halo], 'tile', [(i + 1, i) for i in range(tile_...  8.04 us
    pallas_call x1, Pallas kernels, propagate(): pl.pallas_call(body, grid=(planes,), in_specs=[pl.BlockSpec((1, 2, SPAN),...  6.88 us
    ppermute x1, starting transfers between devices, local(): lax.ppermute(hologram[:, rows - halo:], 'tile', [(i, i + 1) for i in rang...  4.53 us
    ppermute x1, starting transfers between devices, local(): lax.ppermute(hologram[:, :halo], 'tile', [(i + 1, i) for i in range(tile_...  2.61 us
    slice x1, local copies, waits for them, and re-layouts, local(): hologram[:, :halo]  2.49 us
    pad x1, local copies, waits for them, and re-layouts, local(): window = jnp.pad(window, ((0, 0), (0, 0), (half_taps, LANE - half_taps)))  2.24 us
  transfers between devices with their start and end apart: 9, of which 1 were waited for; matrix products, arithmetic and copies ran while one was open for 4% of the time, Pallas kernels for 0%

profile of v1, /device:TPU:1, one launch (start us, length us, event | category | flops | bytes accessed | tf_op | source)
XLA Modules:
  0.0 86.9 jit_solution(11150277764218494549)
XLA Ops:
  0.7 2.5 %fusion.8 = (bf16[2,48,4096]{2,1,0:T(8,128)(2,1)S(1)}, bf16[2,48,4096]{2,1,0:T(8,128)(2,1)}) fusion(bf16[2,64,4096]{2,1,0:T(8,128)(2,1)} %param.3), kind=kLoop, calls=%fused_computation.25 | loop fusion | bytes 3145728 | tf_op jit(solution)/shard_map/slice | solution.py:211
  3.2 4.5 %collective-permute-start = (bf16[2,48,4096]{2,1,0:T(8,128)(2,1)}, bf16[2,48,4096]{2,1,0:T(8,128)(2,1)S(1)}, u32[]{:S(2)}, u32[]{:S(2)}) collective-permute-start(bf16[2,48,4096]{2,1,0:T(8,128)(2,1)} %get-tuple-element.12), channel_id=1, source_target_pairs={{0,1},{1,2},{2,3},{4,5},{5,6},{6,7},{8,9},{9,10},{10,11},{12,13},{... | collective-permute-start | bytes 2359304 | tf_op jit(solution)/shard_map/ppermute | solution.py:208
  7.7 0.6 fusion.7
  8.3 1.3 %collective-permute-start.8 = (f32[4,576]{1,0:T(4,128)S(1)}, f32[4,576]{1,0:T(4,128)S(1)}, u32[]{:S(2)}, u32[]{:S(2)}) collective-permute-start(f32[4,576]{1,0:T(4,128)S(1)} %constant_dynamic-update-slice_fusion.3), channel_id=1, source_target_pairs={{28,0},{0,4},{4,8},{8,12},{12,16},{16,20},{20,24},{24,28},{29,1},{... | collective-permute-start | bytes 27656 | tf_op jit(solution)/shard_map/ppermute | solution.py:183
  9.6 1.3 %collective-permute-start.7 = (f32[4,576]{1,0:T(4,128)S(1)}, f32[4,576]{1,0:T(4,128)S(1)}, u32[]{:S(2)}, u32[]{:S(2)}) collective-permute-start(f32[4,576]{1,0:T(4,128)S(1)} %constant_dynamic-update-slice_fusion.3), channel_id=1, source_target_pairs={{24,0},{28,4},{0,8},{4,12},{8,16},{12,20},{16,24},{20,28},{25,1},{... | collective-permute-start | bytes 27656 | tf_op jit(solution)/shard_map/ppermute | solution.py:183
  10.9 2.3 %collective-permute-start.6 = (f32[4,576]{1,0:T(4,128)S(1)}, f32[4,576]{1,0:T(4,128)S(1)}, u32[]{:S(2)}, u32[]{:S(2)}) collective-permute-start(f32[4,576]{1,0:T(4,128)S(1)} %constant_dynamic-update-slice_fusion.3), channel_id=1, source_target_pairs={{20,0},{24,4},{28,8},{0,12},{4,16},{8,20},{12,24},{16,28},{21,1},{... | collective-permute-start | bytes 27656 | tf_op jit(solution)/shard_map/ppermute | solution.py:183
  13.2 1.0 %collective-permute-start.5 = (f32[4,576]{1,0:T(4,128)S(1)}, f32[4,576]{1,0:T(4,128)S(1)}, u32[]{:S(2)}, u32[]{:S(2)}) collective-permute-start(f32[4,576]{1,0:T(4,128)S(1)} %constant_dynamic-update-slice_fusion.3), channel_id=1, source_target_pairs={{16,0},{20,4},{24,8},{28,12},{0,16},{4,20},{8,24},{12,28},{17,1},{... | collective-permute-start | bytes 27656 | tf_op jit(solution)/shard_map/ppermute | solution.py:183
  14.1 0.6 fusion.3.depth_ref
  14.8 2.3 %collective-permute-start.4 = (f32[4,576]{1,0:T(4,128)S(1)}, f32[4,576]{1,0:T(4,128)S(1)}, u32[]{:S(2)}, u32[]{:S(2)}) collective-permute-start(f32[4,576]{1,0:T(4,128)S(1)} %constant_dynamic-update-slice_fusion.3), channel_id=1, source_target_pairs={{12,0},{16,4},{20,8},{24,12},{28,16},{0,20},{4,24},{8,28},{13,1},{... | collective-permute-start | bytes 27656 | tf_op jit(solution)/shard_map/ppermute | solution.py:183
  17.1 1.1 %collective-permute-start.3 = (f32[4,576]{1,0:T(4,128)S(1)}, f32[4,576]{1,0:T(4,128)S(1)}, u32[]{:S(2)}, u32[]{:S(2)}) collective-permute-start(f32[4,576]{1,0:T(4,128)S(1)} %constant_dynamic-update-slice_fusion.3), channel_id=1, source_target_pairs={{8,0},{12,4},{16,8},{20,12},{24,16},{28,20},{0,24},{4,28},{9,1},{1... | collective-permute-start | bytes 27656 | tf_op jit(solution)/shard_map/ppermute | solution.py:183
  18.2 1.2 %collective-permute-start.2 = (f32[4,576]{1,0:T(4,128)S(1)}, f32[4,576]{1,0:T(4,128)}, u32[]{:S(2)}, u32[]{:S(2)}) collective-permute-start(f32[4,576]{1,0:T(4,128)S(1)} %constant_dynamic-update-slice_fusion.3), channel_id=1, source_target_pairs={{4,0},{8,4},{12,8},{16,12},{20,16},{24,20},{28,24},{0,28},{5,1},{9... | collective-permute-start | bytes 27656 | tf_op jit(solution)/shard_map/ppermute | solution.py:183
  19.3 0.6 pad_add_fusion.corner_ref
  19.9 2.6 %collective-permute-start.1 = (bf16[2,48,4096]{2,1,0:T(8,128)(2,1)S(1)}, bf16[2,48,4096]{2,1,0:T(8,128)(2,1)S(1)}, u32[]{:S(2)}, u32[]{:S(2)}) collective-permute-start(bf16[2,48,4096]{2,1,0:T(8,128)(2,1)S(1)} %get-tuple-element.11), channel_id=1, source_target_pairs={{1,0},{2,1},{3,2},{5,4},{6,5},{7,6},{9,8},{10,9},{11,10},{13,12},{... | collective-permute-start | bytes 2359304 | tf_op jit(solution)/shard_map/ppermute | solution.py:211
  23.2 0.6 copy-done.2
  23.8 1.5 %concatenate.11 = f32[32,576]{1,0:T(8,128)S(1)} concatenate(f32[4,576]{1,0:T(4,128)S(1)} %constant_dynamic-update-slice_fusion.3, f32[4,576]{1,0:T(4,128)} %collective-permute-done.2, f32[4,576]{1,0:T(4,128)} %copy-done.2, f32[4,576]{1,0:T(4,128)} %copy-done.1, f32[4,576]{1,0:T(4,128)S(1)} %collective-permute-done.5, f32[4,576]{1,0:T(4,128)S(1)} %collective-permute-done.6, ...), dimensions={0} | concatenate | bytes 147456 | tf_op jit(solution)/shard_map/concatenate | solution.py:186
  25.4 8.0 %collective-permute-done.1 = bf16[2,48,4096]{2,1,0:T(8,128)(2,1)S(1)} collective-permute-done((bf16[2,48,4096]{2,1,0:T(8,128)(2,1)S(1)}, bf16[2,48,4096]{2,1,0:T(8,128)(2,1)S(1)}, u32[]{:S(2)}, u32[]{:S(2)}) %collective-permute-start.1) | collective-permute-done | bytes 786464 | tf_op jit(solution)/shard_map/ppermute | solution.py:211
  33.9 2.2 %pad.20 = bf16[2,128,4224]{2,1,0:T(8,128)(2,1)} pad(bf16[2,128,4096]{2,1,0:T(8,128)(2,1)S(1)} %slice.32, bf16[]{:T(256)} %constant.53.clone.1), padding=0_0x0_0x32_96 | pad | bytes 4259842 | tf_op jit(solution)/shard_map/jit(_pad)/pad | solution.py:215
  36.1 6.9 %shard_map.58 = f32[4,64,4096]{2,1,0:T(8,128)} custom-call(f32[4,2,256]{2,1,0:T(2,128)} %get-tuple-element.14.taps_ref, bf16[256,4224]{1,0:T(8,128)(2,1)} %bitcast.9), custom_call_target="tpu_custom_call" | custom-call | flops 3254779904 | bytes 6356992 | tf_op jit(solution)/shard_map/pallas_call | solution.py:125
  43.0 0.7 reshape.121.taps_ref
  43.8 1.5 %copy.7.prior_ref = f32[32,80,1]{2,1,0:T(8,128)} copy(f32[32,80,1]{1,0,2:T(8,128)S(1)} %pad_bitcast_fusion) | data formatting | bytes 20480 | tf_op jit(solution)/shard_map/broadcast_in_dim | solution.py:234
  45.3 1.4 %pad_dynamic-slice_fusion = bf16[2,256,768]{2,1,0:T(8,128)(2,1)} fusion(s32[]{:T(128)S(6)} %select_n.43, bf16[2,143,4096]{2,1,0:T(8,128)(2,1)S(1)} %slice.33), kind=kLoop, calls=%fused_computation | loop fusion | bytes 3129348 | tf_op jit(solution)/shard_map/dynamic_slice | solution.py:230
  46.7 36.9 %shard_map.59 = (f32[80,640]{1,0:T(8,128)}, f32[80,640]{1,0:T(8,128)}) custom-call(s32[2]{0:T(128)} %pad_add_fusion.corner_ref, f32[32,2,256]{2,1,0:T(2,128)} %reshape.121.taps_ref, f32[32,80,1]{2,1,0:T(8,128)} %copy.7.prior_ref, f32[32,1,1]{2,1,0:T(1,128)} %fusion.3.depth_ref, bf16[512,768]{1,0:T(8,128)(2,1)} %bitcast.10), custom_call_target="tpu_custom_call" | custom-call | flops 7381975040 | bytes 1196032 | tf_op jit(solution)/shard_map/pallas_call | solution.py:167
  83.5 1.7 %slice.30 = f32[64,512]{1,0:T(8,128)} slice(f32[80,640]{1,0:T(8,128)} %get-tuple-element.9), slice={[8:72], [64:576]} | slice | bytes 262144 | tf_op jit(solution)/shard_map/slice | solution.py:240
  85.2 1.7 %slice.31 = f32[64,512]{1,0:T(8,128)} slice(f32[80,640]{1,0:T(8,128)} %get-tuple-element.10), slice={[8:72], [64:576]} | slice | bytes 262144 | tf_op jit(solution)/shard_map/slice | solution.py:241
  (28 shorter events, 1.3 us)
Async XLA Ops:
  0.6 24.7 %copy-start = (bf16[2,64,4096]{2,1,0:T(8,128)(2,1)S(1)}, bf16[2,64,4096]{2,1,0:T(8,128)(2,1)}, u32[]{:S(2)}) copy-start(bf16[2,64,4096]{2,1,0:T(8,128)(2,1)} %param.3) | copy-start | bytes 3145732
  0.6 7.0 %copy-start.3 = (bf16[4,2,64]{2,1,0:T(2,128)(2,1)S(1)}, bf16[4,2,64]{2,1,0:T(2,128)(2,1)}, u32[]{:S(2)}) copy-start(bf16[4,2,64]{2,1,0:T(2,128)(2,1)} %param.4) | copy-start | bytes 3076
  0.7 7.7 %copy-start.4 = (f32[4,64]{1,0:T(4,128)S(1)}, f32[4,64]{1,0:T(4,128)}, u32[]{:S(2)}) copy-start(f32[4,64]{1,0:T(4,128)} %param.5) | copy-start | bytes 3076
  3.2 22.1 %collective-permute-start = (bf16[2,48,4096]{2,1,0:T(8,128)(2,1)}, bf16[2,48,4096]{2,1,0:T(8,128)(2,1)S(1)}, u32[]{:S(2)}, u32[]{:S(2)}) collective-permute-start(bf16[2,48,4096]{2,1,0:T(8,128)(2,1)} %get-tuple-element.12), channel_id=1, source_target_pairs={{0,1},{1,2},{2,3},{4,5},{5,6},{6,7},{8,9},{9,10},{10,11},{12,13},{... | collective-permute-start | bytes 2359304 | tf_op jit(solution)/shard_map/ppermute | solution.py:208
  8.3 6.4 %collective-permute-start.8 = (f32[4,576]{1,0:T(4,128)S(1)}, f32[4,576]{1,0:T(4,128)S(1)}, u32[]{:S(2)}, u32[]{:S(2)}) collective-permute-start(f32[4,576]{1,0:T(4,128)S(1)} %constant_dynamic-update-slice_fusion.3), channel_id=1, source_target_pairs={{28,0},{0,4},{4,8},{8,12},{12,16},{16,20},{20,24},{24,28},{29,1},{... | collective-permute-start | bytes 27656 | tf_op jit(solution)/shard_map/ppermute | solution.py:183
  9.6 7.5 %collective-permute-start.7 = (f32[4,576]{1,0:T(4,128)S(1)}, f32[4,576]{1,0:T(4,128)S(1)}, u32[]{:S(2)}, u32[]{:S(2)}) collective-permute-start(f32[4,576]{1,0:T(4,128)S(1)} %constant_dynamic-update-slice_fusion.3), channel_id=1, source_target_pairs={{24,0},{28,4},{0,8},{4,12},{8,16},{12,20},{16,24},{20,28},{25,1},{... | collective-permute-start | bytes 27656 | tf_op jit(solution)/shard_map/ppermute | solution.py:183
  10.9 7.3 %collective-permute-start.6 = (f32[4,576]{1,0:T(4,128)S(1)}, f32[4,576]{1,0:T(4,128)S(1)}, u32[]{:S(2)}, u32[]{:S(2)}) collective-permute-start(f32[4,576]{1,0:T(4,128)S(1)} %constant_dynamic-update-slice_fusion.3), channel_id=1, source_target_pairs={{20,0},{24,4},{28,8},{0,12},{4,16},{8,20},{12,24},{16,28},{21,1},{... | collective-permute-start | bytes 27656 | tf_op jit(solution)/shard_map/ppermute | solution.py:183
  13.2 6.8 %collective-permute-start.5 = (f32[4,576]{1,0:T(4,128)S(1)}, f32[4,576]{1,0:T(4,128)S(1)}, u32[]{:S(2)}, u32[]{:S(2)}) collective-permute-start(f32[4,576]{1,0:T(4,128)S(1)} %constant_dynamic-update-slice_fusion.3), channel_id=1, source_target_pairs={{16,0},{20,4},{24,8},{28,12},{0,16},{4,20},{8,24},{12,28},{17,1},{... | collective-permute-start | bytes 27656 | tf_op jit(solution)/shard_map/ppermute | solution.py:183
  14.8 7.8 %collective-permute-start.4 = (f32[4,576]{1,0:T(4,128)S(1)}, f32[4,576]{1,0:T(4,128)S(1)}, u32[]{:S(2)}, u32[]{:S(2)}) collective-permute-start(f32[4,576]{1,0:T(4,128)S(1)} %constant_dynamic-update-slice_fusion.3), channel_id=1, source_target_pairs={{12,0},{16,4},{20,8},{24,12},{28,16},{0,20},{4,24},{8,28},{13,1},{... | collective-permute-start | bytes 27656 | tf_op jit(solution)/shard_map/ppermute | solution.py:183
  17.1 5.5 %collective-permute-start.3 = (f32[4,576]{1,0:T(4,128)S(1)}, f32[4,576]{1,0:T(4,128)S(1)}, u32[]{:S(2)}, u32[]{:S(2)}) collective-permute-start(f32[4,576]{1,0:T(4,128)S(1)} %constant_dynamic-update-slice_fusion.3), channel_id=1, source_target_pairs={{8,0},{12,4},{16,8},{20,12},{24,16},{28,20},{0,24},{4,28},{9,1},{1... | collective-permute-start | bytes 27656 | tf_op jit(solution)/shard_map/ppermute | solution.py:183
  18.2 5.6 %collective-permute-start.2 = (f32[4,576]{1,0:T(4,128)S(1)}, f32[4,576]{1,0:T(4,128)}, u32[]{:S(2)}, u32[]{:S(2)}) collective-permute-start(f32[4,576]{1,0:T(4,128)S(1)} %constant_dynamic-update-slice_fusion.3), channel_id=1, source_target_pairs={{4,0},{8,4},{12,8},{16,12},{20,16},{24,20},{28,24},{0,28},{5,1},{9... | collective-permute-start | bytes 27656 | tf_op jit(solution)/shard_map/ppermute | solution.py:183
  19.9 13.5 %collective-permute-start.1 = (bf16[2,48,4096]{2,1,0:T(8,128)(2,1)S(1)}, bf16[2,48,4096]{2,1,0:T(8,128)(2,1)S(1)}, u32[]{:S(2)}, u32[]{:S(2)}) collective-permute-start(bf16[2,48,4096]{2,1,0:T(8,128)(2,1)S(1)} %get-tuple-element.11), channel_id=1, source_target_pairs={{1,0},{2,1},{3,2},{5,4},{6,5},{7,6},{9,8},{10,9},{11,10},{13,12},{... | collective-permute-start | bytes 2359304 | tf_op jit(solution)/shard_map/ppermute | solution.py:211
  22.5 0.6 copy-start.1
  23.1 0.6 copy-start.2

commit v2 on v1

--- a/solution.py
+++ b/solution.py
@@ -12,23 +12,34 @@
 SPAN = 2 * LANE
 
 
-def stacked_intensity(taps_ref, window_ref, n_out, n_in, block_count):
+def skews(taps_ref, plane):
     def skew(taps):
         return pltpu.roll(jnp.broadcast_to(taps, (LANE, SPAN)), 0, 1, stride=1, stride_axis=0)
 
-    skew_re = skew(taps_ref[0, 0:1, :])
-    skew_im = skew(taps_ref[0, 1:2, :])
+    return skew(taps_ref[plane, 0:1, :]), skew(taps_ref[plane, 1:2, :])
+
+
+def rows_matrix(skew_re, skew_im, n_out, n_in):
     rows_re = skew_re[:n_out, :n_in]
     rows_im = skew_im[:n_out, :n_in]
-    rows_matrix = jnp.concatenate(
+    return jnp.concatenate(
         [
             jnp.concatenate([rows_re, -rows_im], axis=1),
             jnp.concatenate([rows_im, rows_re], axis=1),
         ],
         axis=0,
     ).astype(jnp.bfloat16)
-    across = jnp.dot(rows_matrix, window_ref[...], preferred_element_type=jnp.float32)
-    across = across.astype(jnp.bfloat16)
+
+
+def across_planes(taps_ref, window_ref, n_out, n_in):
+    group = taps_ref.shape[0]
+    skewed = [skews(taps_ref, g) for g in range(group)]
+    matrix = jnp.concatenate([rows_matrix(*sk, n_out, n_in) for sk in skewed], axis=0)
+    across = jnp.dot(matrix, window_ref[...], preferred_element_type=jnp.float32)
+    return skewed, across.astype(jnp.bfloat16)
+
+
+def column_intensity(across, skew_re, skew_im, n_out, block_count):
     across_re = across[:n_out]
     across_im = across[n_out:]
 
@@ -59,45 +70,50 @@
 
 
 def propagate_kernel(taps_ref, window_ref, out_ref, *, n_out, n_in, block_count):
-    intensity = stacked_intensity(taps_ref, window_ref, n_out, n_in, block_count)
-    for b in range(block_count):
-        out_ref[0, :, LANE * b : LANE * (b + 1)] = intensity[n_out * b : n_out * (b + 1)]
+    skewed, across = across_planes(taps_ref, window_ref, n_out, n_in)
+    for g, (skew_re, skew_im) in enumerate(skewed):
+        intensity = column_intensity(
+            across[2 * n_out * g : 2 * n_out * (g + 1)], skew_re, skew_im, n_out, block_count
+        )
+        for b in range(block_count):
+            out_ref[g, :, LANE * b : LANE * (b + 1)] = intensity[n_out * b : n_out * (b + 1)]
 
 
 def joining_kernel(
     corner_ref, taps_ref, prior_ref, depth_ref, window_ref, joined_ref, mean_ref,
     peak_ref, total_ref, weighted_ref, placed_ref, *, n_out, n_in, block_count, bounds,
 ):
-    plane = pl.program_id(0)
-    stacked = stacked_intensity(taps_ref, window_ref, n_out, n_in, block_count)
-    intensity = jnp.concatenate(
-        [stacked[n_out * b : n_out * (b + 1)] for b in range(block_count)], axis=1
-    )
-    height, width = intensity.shape
+    step = pl.program_id(0)
+
+    @pl.when(step == 0)
+    def _():
+        peak_ref[...] = jnp.full(peak_ref.shape, -jnp.inf, jnp.float32)
+        total_ref[...] = jnp.zeros(total_ref.shape, jnp.float32)
+        weighted_ref[...] = jnp.zeros(weighted_ref.shape, jnp.float32)
+        placed_ref[...] = jnp.zeros(placed_ref.shape, jnp.float32)
+
+    skewed, across = across_planes(taps_ref, window_ref, n_out, n_in)
+    height, width = n_out, block_count * LANE
     row_at = corner_ref[0] + lax.broadcasted_iota(jnp.int32, (height, width), 0)
     col_at = corner_ref[1] + lax.broadcasted_iota(jnp.int32, (height, width), 1)
     inside = (row_at >= 0) & (row_at < bounds[0]) & (col_at >= 0) & (col_at < bounds[1])
-    intensity = jnp.where(inside, intensity, 0.0)
-    vertical = (
-        pltpu.roll(intensity, 1, 0) + 2.0 * intensity + pltpu.roll(intensity, height - 1, 0)
-    )
-    grad_x = pltpu.roll(vertical, width - 1, 1) - pltpu.roll(vertical, 1, 1)
-    horizontal = (
-        pltpu.roll(intensity, 1, 1) + 2.0 * intensity + pltpu.roll(intensity, width - 1, 1)
-    )
-    grad_y = pltpu.roll(horizontal, height - 1, 0) - pltpu.roll(horizontal, 1, 0)
-    score = prior_ref[0] + jnp.log(1.0 + (grad_x * grad_x + grad_y * grad_y))
-    depth_value = depth_ref[0]
-
-    @pl.when(plane == 0)
-    def _():
-        peak_ref[...] = score
-        total_ref[...] = jnp.ones_like(score)
-        weighted_ref[...] = intensity
-        placed_ref[...] = jnp.broadcast_to(depth_value, score.shape)
-
-    @pl.when(plane > 0)
-    def _():
+    for g, (skew_re, skew_im) in enumerate(skewed):
+        stacked = column_intensity(
+            across[2 * n_out * g : 2 * n_out * (g + 1)], skew_re, skew_im, n_out, block_count
+        )
+        intensity = jnp.concatenate(
+            [stacked[n_out * b : n_out * (b + 1)] for b in range(block_count)], axis=1
+        )
+        intensity = jnp.where(inside, intensity, 0.0)
+        vertical = (
+            pltpu.roll(intensity, 1, 0) + 2.0 * intensity + pltpu.roll(intensity, height - 1, 0)
+        )
+        grad_x = pltpu.roll(vertical, width - 1, 1) - pltpu.roll(vertical, 1, 1)
+        horizontal = (
+            pltpu.roll(intensity, 1, 1) + 2.0 * intensity + pltpu.roll(intensity, width - 1, 1)
+        )
+        grad_y = pltpu.roll(horizontal, height - 1, 0) - pltpu.roll(horizontal, 1, 0)
+        score = prior_ref[g] + jnp.log(1.0 + (grad_x * grad_x + grad_y * grad_y))
         peak_now = peak_ref[...]
         peak_next = jnp.maximum(peak_now, score)
         factor = jnp.exp(peak_now - peak_next)
@@ -105,9 +121,9 @@
         peak_ref[...] = peak_next
         total_ref[...] = total_ref[...] * factor + fresh
         weighted_ref[...] = weighted_ref[...] * factor + fresh * intensity
-        placed_ref[...] = placed_ref[...] * factor + fresh * depth_value
-
-    @pl.when(plane == pl.num_programs(0) - 1)
+        placed_ref[...] = placed_ref[...] * factor + fresh * depth_ref[g]
+
+    @pl.when(step == pl.num_programs(0) - 1)
     def _():
         joined_ref[...] = weighted_ref[...] / total_ref[...]
         mean_ref[...] = placed_ref[...] / total_ref[...]
@@ -124,12 +140,12 @@
     flops = 2 * planes * (2 * n_out * 2 * n_in * width + block_count * n_out * 4 * LANE * SPAN)
     return pl.pallas_call(
         body,
-        grid=(planes,),
+        grid=(1,),
         in_specs=[
-            pl.BlockSpec((1, 2, SPAN), lambda p: (p, 0, 0)),
+            pl.BlockSpec((planes, 2, SPAN), lambda p: (0, 0, 0)),
             pl.BlockSpec((2 * n_in, width), lambda p: (0, 0)),
         ],
-        out_specs=pl.BlockSpec((1, n_out, block_count * LANE), lambda p: (p, 0, 0)),
+        out_specs=pl.BlockSpec((planes, n_out, block_count * LANE), lambda p: (0, 0, 0)),
         out_shape=jax.ShapeDtypeStruct((planes, n_out, block_count * LANE), jnp.float32),
         cost_estimate=pl.CostEstimate(
             flops=flops,
@@ -141,6 +157,7 @@
 
 def joining(corner, taps, prior, depth_values, window, n_out, bounds):
     planes = taps.shape[0]
+    group = 8 if planes % 8 == 0 else planes
     _, n_in, width = window.shape
     block_count = width // LANE - 1
     stacked = window.reshape(2 * n_in, width)
@@ -151,11 +168,11 @@
     flops = 2 * planes * (2 * n_out * 2 * n_in * width + block_count * n_out * 4 * LANE * SPAN)
     grid_spec = pltpu.PrefetchScalarGridSpec(
         num_scalar_prefetch=1,
-        grid=(planes,),
+        grid=(planes // group,),
         in_specs=[
-            pl.BlockSpec((1, 2, SPAN), lambda p, c: (p, 0, 0)),
-            pl.BlockSpec((1, n_out, 1), lambda p, c: (p, 0, 0)),
-            pl.BlockSpec((1, 1, 1), lambda p, c: (p, 0, 0)),
+            pl.BlockSpec((group, 2, SPAN), lambda p, c: (p, 0, 0)),
+            pl.BlockSpec((group, n_out, 1), lambda p, c: (p, 0, 0)),
+            pl.BlockSpec((group, 1, 1), lambda p, c: (p, 0, 0)),
             pl.BlockSpec((2 * n_in, width), lambda p, c: (0, 0)),
         ],
         out_specs=[

time: 87.3 us -> 74.2 us (0.85)
  Pallas kernels: 43.7 us -> 30.6 us
    pallas_call x1, Pallas kernels: 36.9 us -> 23.3 us  [joining(): pl.pallas_call(body, grid_spec=grid_spec, out_shape=[jax.ShapeDtypeStruct...]
  transfers between devices with their start and end apart: 9 -> 9, of which waited for: 1 -> 1; matrix products, arithmetic and copies ran while one was open for 4% -> 5% of each run, Pallas kernels for 0% -> 0%
where the time goes in v2:
time: 74.2 us; the launch traced here: 73.7 us
  Pallas kernels  30.6 us (41%)
  starting transfers between devices  17.5 us (24%)
  local copies, waits for them, and re-layouts  15 us (20%)
  waiting for transfers between devices  8.06 us (11%)
  other arithmetic  1.83 us (2%)
  between operations  0.77 us (1%)
    pallas_call x1, Pallas kernels, joining(): pl.pallas_call(body, grid_spec=grid_spec, out_shape=[jax.ShapeDtypeStruct...  23.3 us
    ppermute x7, starting transfers between devices, gather_depth(): lax.ppermute(block, 'depth', [((j + shift) % count, j) for j in range(cou...  10.4 us
    ppermute x1, waiting for transfers between devices, local(): lax.ppermute(hologram[:, :halo], 'tile', [(i + 1, i) for i in range(tile_...  8.04 us
    pallas_call x1, Pallas kernels, propagate(): pl.pallas_call(body, grid=(1,), in_specs=[pl.BlockSpec((planes, 2, SPAN),...  7.24 us
    ppermute x1, starting transfers between devices, local(): lax.ppermute(hologram[:, rows - halo:], 'tile', [(i, i + 1) for i in rang...  4.53 us
    ppermute x1, starting transfers between devices, local(): lax.ppermute(hologram[:, :halo], 'tile', [(i + 1, i) for i in range(tile_...  2.61 us
    slice x1, local copies, waits for them, and re-layouts, local(): hologram[:, :halo]  2.49 us
    pad x1, local copies, waits for them, and re-layouts, local(): window = jnp.pad(window, ((0, 0), (0, 0), (half_taps, LANE - half_taps)))  2.24 us
  transfers between devices with their start and end apart: 9, of which 1 were waited for; matrix products, arithmetic and copies ran while one was open for 5% of the time, Pallas kernels for 0%

profile of v2, /device:TPU:1, one launch (start us, length us, event | category | flops | bytes accessed | tf_op | source)
XLA Modules:
  0.0 73.7 jit_solution(11527377358345122464)
XLA Ops:
  0.7 2.5 %fusion.8 = (bf16[2,48,4096]{2,1,0:T(8,128)(2,1)S(1)}, bf16[2,48,4096]{2,1,0:T(8,128)(2,1)}) fusion(bf16[2,64,4096]{2,1,0:T(8,128)(2,1)} %param.3), kind=kLoop, calls=%fused_computation.25 | loop fusion | bytes 3145728 | tf_op jit(solution)/shard_map/slice | solution.py:228
  3.2 4.5 %collective-permute-start = (bf16[2,48,4096]{2,1,0:T(8,128)(2,1)}, bf16[2,48,4096]{2,1,0:T(8,128)(2,1)S(1)}, u32[]{:S(2)}, u32[]{:S(2)}) collective-permute-start(bf16[2,48,4096]{2,1,0:T(8,128)(2,1)} %get-tuple-element.12), channel_id=1, source_target_pairs={{0,1},{1,2},{2,3},{4,5},{5,6},{6,7},{8,9},{9,10},{10,11},{12,13},{... | collective-permute-start | bytes 2359304 | tf_op jit(solution)/shard_map/ppermute | solution.py:225
  7.7 0.6 fusion.7
  8.3 1.3 %collective-permute-start.8 = (f32[4,576]{1,0:T(4,128)S(1)}, f32[4,576]{1,0:T(4,128)S(1)}, u32[]{:S(2)}, u32[]{:S(2)}) collective-permute-start(f32[4,576]{1,0:T(4,128)S(1)} %constant_dynamic-update-slice_fusion.3), channel_id=1, source_target_pairs={{28,0},{0,4},{4,8},{8,12},{12,16},{16,20},{20,24},{24,28},{29,1},{... | collective-permute-start | bytes 27656 | tf_op jit(solution)/shard_map/ppermute | solution.py:200
  9.6 1.3 %collective-permute-start.7 = (f32[4,576]{1,0:T(4,128)S(1)}, f32[4,576]{1,0:T(4,128)S(1)}, u32[]{:S(2)}, u32[]{:S(2)}) collective-permute-start(f32[4,576]{1,0:T(4,128)S(1)} %constant_dynamic-update-slice_fusion.3), channel_id=1, source_target_pairs={{24,0},{28,4},{0,8},{4,12},{8,16},{12,20},{16,24},{20,28},{25,1},{... | collective-permute-start | bytes 27656 | tf_op jit(solution)/shard_map/ppermute | solution.py:200
  10.9 2.3 %collective-permute-start.6 = (f32[4,576]{1,0:T(4,128)S(1)}, f32[4,576]{1,0:T(4,128)S(1)}, u32[]{:S(2)}, u32[]{:S(2)}) collective-permute-start(f32[4,576]{1,0:T(4,128)S(1)} %constant_dynamic-update-slice_fusion.3), channel_id=1, source_target_pairs={{20,0},{24,4},{28,8},{0,12},{4,16},{8,20},{12,24},{16,28},{21,1},{... | collective-permute-start | bytes 27656 | tf_op jit(solution)/shard_map/ppermute | solution.py:200
  13.2 1.0 %collective-permute-start.5 = (f32[4,576]{1,0:T(4,128)S(1)}, f32[4,576]{1,0:T(4,128)S(1)}, u32[]{:S(2)}, u32[]{:S(2)}) collective-permute-start(f32[4,576]{1,0:T(4,128)S(1)} %constant_dynamic-update-slice_fusion.3), channel_id=1, source_target_pairs={{16,0},{20,4},{24,8},{28,12},{0,16},{4,20},{8,24},{12,28},{17,1},{... | collective-permute-start | bytes 27656 | tf_op jit(solution)/shard_map/ppermute | solution.py:200
  14.1 0.6 fusion.3.depth_ref
  14.8 2.3 %collective-permute-start.4 = (f32[4,576]{1,0:T(4,128)S(1)}, f32[4,576]{1,0:T(4,128)S(1)}, u32[]{:S(2)}, u32[]{:S(2)}) collective-permute-start(f32[4,576]{1,0:T(4,128)S(1)} %constant_dynamic-update-slice_fusion.3), channel_id=1, source_target_pairs={{12,0},{16,4},{20,8},{24,12},{28,16},{0,20},{4,24},{8,28},{13,1},{... | collective-permute-start | bytes 27656 | tf_op jit(solution)/shard_map/ppermute | solution.py:200
  17.1 1.1 %collective-permute-start.3 = (f32[4,576]{1,0:T(4,128)S(1)}, f32[4,576]{1,0:T(4,128)S(1)}, u32[]{:S(2)}, u32[]{:S(2)}) collective-permute-start(f32[4,576]{1,0:T(4,128)S(1)} %constant_dynamic-update-slice_fusion.3), channel_id=1, source_target_pairs={{8,0},{12,4},{16,8},{20,12},{24,16},{28,20},{0,24},{4,28},{9,1},{1... | collective-permute-start | bytes 27656 | tf_op jit(solution)/shard_map/ppermute | solution.py:200
  18.2 1.2 %collective-permute-start.2 = (f32[4,576]{1,0:T(4,128)S(1)}, f32[4,576]{1,0:T(4,128)}, u32[]{:S(2)}, u32[]{:S(2)}) collective-permute-start(f32[4,576]{1,0:T(4,128)S(1)} %constant_dynamic-update-slice_fusion.3), channel_id=1, source_target_pairs={{4,0},{8,4},{12,8},{16,12},{20,16},{24,20},{28,24},{0,28},{5,1},{9... | collective-permute-start | bytes 27656 | tf_op jit(solution)/shard_map/ppermute | solution.py:200
  19.3 0.6 pad_add_fusion.corner_ref
  19.9 2.6 %collective-permute-start.1 = (bf16[2,48,4096]{2,1,0:T(8,128)(2,1)S(1)}, bf16[2,48,4096]{2,1,0:T(8,128)(2,1)S(1)}, u32[]{:S(2)}, u32[]{:S(2)}) collective-permute-start(bf16[2,48,4096]{2,1,0:T(8,128)(2,1)S(1)} %get-tuple-element.11), channel_id=1, source_target_pairs={{1,0},{2,1},{3,2},{5,4},{6,5},{7,6},{9,8},{10,9},{11,10},{13,12},{... | collective-permute-start | bytes 2359304 | tf_op jit(solution)/shard_map/ppermute | solution.py:228
  23.2 0.6 copy-done.2
  23.8 1.5 %concatenate.11 = f32[32,576]{1,0:T(8,128)S(1)} concatenate(f32[4,576]{1,0:T(4,128)S(1)} %constant_dynamic-update-slice_fusion.3, f32[4,576]{1,0:T(4,128)} %collective-permute-done.2, f32[4,576]{1,0:T(4,128)} %copy-done.2, f32[4,576]{1,0:T(4,128)} %copy-done.1, f32[4,576]{1,0:T(4,128)S(1)} %collective-permute-done.5, f32[4,576]{1,0:T(4,128)S(1)} %collective-permute-done.6, ...), dimensions={0} | concatenate | bytes 147456 | tf_op jit(solution)/shard_map/concatenate | solution.py:203
  25.4 8.0 %collective-permute-done.1 = bf16[2,48,4096]{2,1,0:T(8,128)(2,1)S(1)} collective-permute-done((bf16[2,48,4096]{2,1,0:T(8,128)(2,1)S(1)}, bf16[2,48,4096]{2,1,0:T(8,128)(2,1)S(1)}, u32[]{:S(2)}, u32[]{:S(2)}) %collective-permute-start.1) | collective-permute-done | bytes 786464 | tf_op jit(solution)/shard_map/ppermute | solution.py:228
  33.9 2.2 %pad.20 = bf16[2,128,4224]{2,1,0:T(8,128)(2,1)} pad(bf16[2,128,4096]{2,1,0:T(8,128)(2,1)S(1)} %slice.32, bf16[]{:T(256)} %constant.53.clone.1), padding=0_0x0_0x32_96 | pad | bytes 4259842 | tf_op jit(solution)/shard_map/jit(_pad)/pad | solution.py:232
  36.1 7.2 %shard_map.58 = f32[4,64,4096]{2,1,0:T(8,128)} custom-call(f32[4,2,256]{2,1,0:T(2,128)} %get-tuple-element.14.taps_ref, bf16[256,4224]{1,0:T(8,128)(2,1)} %bitcast.9), custom_call_target="tpu_custom_call" | custom-call | flops 3254779904 | bytes 6356992 | tf_op jit(solution)/shard_map/pallas_call | solution.py:141
  43.4 0.7 reshape.121.taps_ref
  44.1 1.5 %copy.7.prior_ref = f32[32,80,1]{2,1,0:T(8,128)} copy(f32[32,80,1]{1,0,2:T(8,128)S(1)} %pad_bitcast_fusion) | data formatting | bytes 20480 | tf_op jit(solution)/shard_map/broadcast_in_dim | solution.py:251
  45.7 1.4 %pad_dynamic-slice_fusion = bf16[2,256,768]{2,1,0:T(8,128)(2,1)} fusion(s32[]{:T(128)S(6)} %select_n.43, bf16[2,143,4096]{2,1,0:T(8,128)(2,1)S(1)} %slice.33), kind=kLoop, calls=%fused_computation | loop fusion | bytes 3129348 | tf_op jit(solution)/shard_map/dynamic_slice | solution.py:247
  47.0 23.3 %shard_map.59 = (f32[80,640]{1,0:T(8,128)}, f32[80,640]{1,0:T(8,128)}) custom-call(s32[2]{0:T(128)} %pad_add_fusion.corner_ref, f32[32,2,256]{2,1,0:T(2,128)} %reshape.121.taps_ref, f32[32,80,1]{2,1,0:T(8,128)} %copy.7.prior_ref, f32[32,1,1]{2,1,0:T(1,128)} %fusion.3.depth_ref, bf16[512,768]{1,0:T(8,128)(2,1)} %bitcast.10), custom_call_target="tpu_custom_call" | custom-call | flops 7381975040 | bytes 1196032 | tf_op jit(solution)/shard_map/pallas_call | solution.py:184
  70.4 1.7 %slice.30 = f32[64,512]{1,0:T(8,128)} slice(f32[80,640]{1,0:T(8,128)} %get-tuple-element.9), slice={[8:72], [64:576]} | slice | bytes 262144 | tf_op jit(solution)/shard_map/slice | solution.py:257
  72.1 1.7 %slice.31 = f32[64,512]{1,0:T(8,128)} slice(f32[80,640]{1,0:T(8,128)} %get-tuple-element.10), slice={[8:72], [64:576]} | slice | bytes 262144 | tf_op jit(solution)/shard_map/slice | solution.py:258
  (28 shorter events, 1.3 us)
Async XLA Ops:
  0.6 24.7 %copy-start = (bf16[2,64,4096]{2,1,0:T(8,128)(2,1)S(1)}, bf16[2,64,4096]{2,1,0:T(8,128)(2,1)}, u32[]{:S(2)}) copy-start(bf16[2,64,4096]{2,1,0:T(8,128)(2,1)} %param.3) | copy-start | bytes 3145732
  0.6 7.0 %copy-start.3 = (bf16[4,2,64]{2,1,0:T(2,128)(2,1)S(1)}, bf16[4,2,64]{2,1,0:T(2,128)(2,1)}, u32[]{:S(2)}) copy-start(bf16[4,2,64]{2,1,0:T(2,128)(2,1)} %param.4) | copy-start | bytes 3076
  0.7 7.7 %copy-start.4 = (f32[4,64]{1,0:T(4,128)S(1)}, f32[4,64]{1,0:T(4,128)}, u32[]{:S(2)}) copy-start(f32[4,64]{1,0:T(4,128)} %param.5) | copy-start | bytes 3076
  3.2 22.1 %collective-permute-start = (bf16[2,48,4096]{2,1,0:T(8,128)(2,1)}, bf16[2,48,4096]{2,1,0:T(8,128)(2,1)S(1)}, u32[]{:S(2)}, u32[]{:S(2)}) collective-permute-start(bf16[2,48,4096]{2,1,0:T(8,128)(2,1)} %get-tuple-element.12), channel_id=1, source_target_pairs={{0,1},{1,2},{2,3},{4,5},{5,6},{6,7},{8,9},{9,10},{10,11},{12,13},{... | collective-permute-start | bytes 2359304 | tf_op jit(solution)/shard_map/ppermute | solution.py:225
  8.3 6.4 %collective-permute-start.8 = (f32[4,576]{1,0:T(4,128)S(1)}, f32[4,576]{1,0:T(4,128)S(1)}, u32[]{:S(2)}, u32[]{:S(2)}) collective-permute-start(f32[4,576]{1,0:T(4,128)S(1)} %constant_dynamic-update-slice_fusion.3), channel_id=1, source_target_pairs={{28,0},{0,4},{4,8},{8,12},{12,16},{16,20},{20,24},{24,28},{29,1},{... | collective-permute-start | bytes 27656 | tf_op jit(solution)/shard_map/ppermute | solution.py:200
  9.6 7.5 %collective-permute-start.7 = (f32[4,576]{1,0:T(4,128)S(1)}, f32[4,576]{1,0:T(4,128)S(1)}, u32[]{:S(2)}, u32[]{:S(2)}) collective-permute-start(f32[4,576]{1,0:T(4,128)S(1)} %constant_dynamic-update-slice_fusion.3), channel_id=1, source_target_pairs={{24,0},{28,4},{0,8},{4,12},{8,16},{12,20},{16,24},{20,28},{25,1},{... | collective-permute-start | bytes 27656 | tf_op jit(solution)/shard_map/ppermute | solution.py:200
  10.9 7.3 %collective-permute-start.6 = (f32[4,576]{1,0:T(4,128)S(1)}, f32[4,576]{1,0:T(4,128)S(1)}, u32[]{:S(2)}, u32[]{:S(2)}) collective-permute-start(f32[4,576]{1,0:T(4,128)S(1)} %constant_dynamic-update-slice_fusion.3), channel_id=1, source_target_pairs={{20,0},{24,4},{28,8},{0,12},{4,16},{8,20},{12,24},{16,28},{21,1},{... | collective-permute-start | bytes 27656 | tf_op jit(solution)/shard_map/ppermute | solution.py:200
  13.2 6.8 %collective-permute-start.5 = (f32[4,576]{1,0:T(4,128)S(1)}, f32[4,576]{1,0:T(4,128)S(1)}, u32[]{:S(2)}, u32[]{:S(2)}) collective-permute-start(f32[4,576]{1,0:T(4,128)S(1)} %constant_dynamic-update-slice_fusion.3), channel_id=1, source_target_pairs={{16,0},{20,4},{24,8},{28,12},{0,16},{4,20},{8,24},{12,28},{17,1},{... | collective-permute-start | bytes 27656 | tf_op jit(solution)/shard_map/ppermute | solution.py:200
  14.8 7.8 %collective-permute-start.4 = (f32[4,576]{1,0:T(4,128)S(1)}, f32[4,576]{1,0:T(4,128)S(1)}, u32[]{:S(2)}, u32[]{:S(2)}) collective-permute-start(f32[4,576]{1,0:T(4,128)S(1)} %constant_dynamic-update-slice_fusion.3), channel_id=1, source_target_pairs={{12,0},{16,4},{20,8},{24,12},{28,16},{0,20},{4,24},{8,28},{13,1},{... | collective-permute-start | bytes 27656 | tf_op jit(solution)/shard_map/ppermute | solution.py:200
  17.1 5.5 %collective-permute-start.3 = (f32[4,576]{1,0:T(4,128)S(1)}, f32[4,576]{1,0:T(4,128)S(1)}, u32[]{:S(2)}, u32[]{:S(2)}) collective-permute-start(f32[4,576]{1,0:T(4,128)S(1)} %constant_dynamic-update-slice_fusion.3), channel_id=1, source_target_pairs={{8,0},{12,4},{16,8},{20,12},{24,16},{28,20},{0,24},{4,28},{9,1},{1... | collective-permute-start | bytes 27656 | tf_op jit(solution)/shard_map/ppermute | solution.py:200
  18.2 5.6 %collective-permute-start.2 = (f32[4,576]{1,0:T(4,128)S(1)}, f32[4,576]{1,0:T(4,128)}, u32[]{:S(2)}, u32[]{:S(2)}) collective-permute-start(f32[4,576]{1,0:T(4,128)S(1)} %constant_dynamic-update-slice_fusion.3), channel_id=1, source_target_pairs={{4,0},{8,4},{12,8},{16,12},{20,16},{24,20},{28,24},{0,28},{5,1},{9... | collective-permute-start | bytes 27656 | tf_op jit(solution)/shard_map/ppermute | solution.py:200
  19.9 13.5 %collective-permute-start.1 = (bf16[2,48,4096]{2,1,0:T(8,128)(2,1)S(1)}, bf16[2,48,4096]{2,1,0:T(8,128)(2,1)S(1)}, u32[]{:S(2)}, u32[]{:S(2)}) collective-permute-start(bf16[2,48,4096]{2,1,0:T(8,128)(2,1)S(1)} %get-tuple-element.11), channel_id=1, source_target_pairs={{1,0},{2,1},{3,2},{5,4},{6,5},{7,6},{9,8},{10,9},{11,10},{13,12},{... | collective-permute-start | bytes 2359304 | tf_op jit(solution)/shard_map/ppermute | solution.py:228
  22.5 0.6 copy-start.1
  23.1 0.6 copy-start.2

commit v3 on v2

--- a/solution.py
+++ b/solution.py
@@ -81,13 +81,12 @@
 
 def joining_kernel(
     corner_ref, taps_ref, prior_ref, depth_ref, window_ref, joined_ref, mean_ref,
-    peak_ref, total_ref, weighted_ref, placed_ref, *, n_out, n_in, block_count, bounds,
+    total_ref, weighted_ref, placed_ref, *, n_out, n_in, block_count, bounds, crop,
 ):
     step = pl.program_id(0)
 
     @pl.when(step == 0)
     def _():
-        peak_ref[...] = jnp.full(peak_ref.shape, -jnp.inf, jnp.float32)
         total_ref[...] = jnp.zeros(total_ref.shape, jnp.float32)
         weighted_ref[...] = jnp.zeros(weighted_ref.shape, jnp.float32)
         placed_ref[...] = jnp.zeros(placed_ref.shape, jnp.float32)
@@ -113,20 +112,21 @@
             pltpu.roll(intensity, 1, 1) + 2.0 * intensity + pltpu.roll(intensity, width - 1, 1)
         )
         grad_y = pltpu.roll(horizontal, height - 1, 0) - pltpu.roll(horizontal, 1, 0)
-        score = prior_ref[g] + jnp.log(1.0 + (grad_x * grad_x + grad_y * grad_y))
-        peak_now = peak_ref[...]
-        peak_next = jnp.maximum(peak_now, score)
-        factor = jnp.exp(peak_now - peak_next)
-        fresh = jnp.exp(score - peak_next)
-        peak_ref[...] = peak_next
-        total_ref[...] = total_ref[...] * factor + fresh
-        weighted_ref[...] = weighted_ref[...] * factor + fresh * intensity
-        placed_ref[...] = placed_ref[...] * factor + fresh * depth_ref[g]
+        fresh = prior_ref[g] * (1.0 + (grad_x * grad_x + grad_y * grad_y))
+        total_ref[...] = total_ref[...] + fresh
+        weighted_ref[...] = weighted_ref[...] + fresh * intensity
+        placed_ref[...] = placed_ref[...] + fresh * depth_ref[g]
 
     @pl.when(step == pl.num_programs(0) - 1)
     def _():
-        joined_ref[...] = weighted_ref[...] / total_ref[...]
-        mean_ref[...] = placed_ref[...] / total_ref[...]
+        rows, cols = joined_ref.shape
+        top, left = crop
+
+        def cropped(values):
+            return pltpu.roll(values, width - left, 1)[top : top + rows, :cols]
+
+        joined_ref[...] = cropped(weighted_ref[...] / total_ref[...])
+        mean_ref[...] = cropped(placed_ref[...] / total_ref[...])
 
 
 def propagate(taps, window, n_out):
@@ -155,14 +155,15 @@
     )(taps, stacked)
 
 
-def joining(corner, taps, prior, depth_values, window, n_out, bounds):
+def joining(corner, taps, prior, depth_values, window, n_out, bounds, crop, out_shape):
     planes = taps.shape[0]
     group = 8 if planes % 8 == 0 else planes
     _, n_in, width = window.shape
     block_count = width // LANE - 1
     stacked = window.reshape(2 * n_in, width)
     body = functools.partial(
-        joining_kernel, n_out=n_out, n_in=n_in, block_count=block_count, bounds=bounds
+        joining_kernel, n_out=n_out, n_in=n_in, block_count=block_count, bounds=bounds,
+        crop=crop,
     )
     out_cols = block_count * LANE
     flops = 2 * planes * (2 * n_out * 2 * n_in * width + block_count * n_out * 4 * LANE * SPAN)
@@ -176,19 +177,19 @@
             pl.BlockSpec((2 * n_in, width), lambda p, c: (0, 0)),
         ],
         out_specs=[
-            pl.BlockSpec((n_out, out_cols), lambda p, c: (0, 0)),
-            pl.BlockSpec((n_out, out_cols), lambda p, c: (0, 0)),
-        ],
-        scratch_shapes=[pltpu.VMEM((n_out, out_cols), jnp.float32) for _ in range(4)],
+            pl.BlockSpec(out_shape, lambda p, c: (0, 0)),
+            pl.BlockSpec(out_shape, lambda p, c: (0, 0)),
+        ],
+        scratch_shapes=[pltpu.VMEM((n_out, out_cols), jnp.float32) for _ in range(3)],
     )
     return pl.pallas_call(
         body,
         grid_spec=grid_spec,
-        out_shape=[jax.ShapeDtypeStruct((n_out, out_cols), jnp.float32)] * 2,
+        out_shape=[jax.ShapeDtypeStruct(out_shape, jnp.float32)] * 2,
         compiler_params=pltpu.CompilerParams(dimension_semantics=("arbitrary",)),
         cost_estimate=pl.CostEstimate(
             flops=flops,
-            transcendentals=3 * planes * n_out * out_cols,
+            transcendentals=0,
             bytes_accessed=stacked.size * 2 + 2 * n_out * out_cols * 4,
         ),
     )(corner, taps, prior, depth_values, stacked)
@@ -196,11 +197,11 @@
 
 def gather_depth(block):
     count = lax.axis_size("depth")
-    moved = [
-        lax.ppermute(block, "depth", [((j + shift) % count, j) for j in range(count)])
-        for shift in range(1, count)
-    ]
-    return jnp.concatenate([block, *moved], axis=0)
+    placed = jnp.zeros((count * block.shape[0], block.shape[1]), block.dtype)
+    placed = lax.dynamic_update_slice_in_dim(
+        placed, block, lax.axis_index("depth") * block.shape[0], axis=0
+    )
+    return lax.psum(placed, "depth")
 
 
 def local(hologram, kernel, depth_prior):
@@ -218,8 +219,7 @@
     taps = jnp.pad(kernel.astype(jnp.float32), ((0, 0), (0, 0), (0, SPAN - TAPS)))
     packed = jnp.concatenate([taps.reshape(local_planes, 2 * SPAN), depth_prior], axis=1)
     packed_all = gather_depth(packed)
-    owner = (depth_at + jnp.arange(planes_total) // local_planes) % depth_count
-    plane_at = owner * local_planes + jnp.arange(planes_total) % local_planes
+    plane_at = jnp.arange(planes_total)
 
     halo = 48
     above = lax.ppermute(
@@ -248,14 +248,13 @@
     corner = jnp.stack([tile_at * rows - lead_rows, depth_at * own_cols - LANE // 2]).astype(
         jnp.int32
     )
-    prior_rows = jnp.pad(prior_all, ((0, 0), (lead_rows, lead_rows)))[:, :, None]
+    prior_weight = jnp.exp(prior_all - jnp.max(prior_all, axis=0, keepdims=True))
+    prior_rows = jnp.pad(prior_weight, ((0, 0), (lead_rows, lead_rows)), constant_values=1.0)
     depth_values = ((plane_at.astype(jnp.float32) + 0.5) / planes_total)[:, None, None]
     joined, mean_depth = joining(
-        corner, taps_all, prior_rows, depth_values, window, n_out, (row_total, col_total)
-    )
-    start = LANE // 2
-    joined = joined[lead_rows : lead_rows + rows, start : start + own_cols]
-    mean_depth = mean_depth[lead_rows : lead_rows + rows, start : start + own_cols]
+        corner, taps_all, prior_rows[:, :, None], depth_values, window, n_out,
+        (row_total, col_total), (lead_rows, LANE // 2), (rows, own_cols),
+    )
     return (plane_stack, joined, mean_depth)
 
 

time: 74.2 us -> 120 us (1.62)
  the two profiles are of different devices: /device:TPU:1 before, /device:TPU:4 now
where the time goes in v3:
time: 120 us; the launch traced here: 118 us
  waiting for transfers between devices  51.6 us (43%)
  Pallas kernels  28.3 us (24%)
  local copies, waits for them, and re-layouts  14.9 us (12%)
  between operations  14.1 us (12%)
  starting transfers between devices  5.59 us (5%)
  other arithmetic  3.34 us (3%)
    psum x1, waiting for transfers between devices, gather_depth(): return lax.psum(placed, 'depth')  44.5 us
    pallas_call x1, Pallas kernels, joining(): pl.pallas_call(body, grid_spec=grid_spec, out_shape=[jax.ShapeDtypeStruct...  21.1 us
    pallas_call x1, Pallas kernels, propagate(): pl.pallas_call(body, grid=(1,), in_specs=[pl.BlockSpec((planes, 2, SPAN),...  7.25 us
    ppermute x1, waiting for transfers between devices, local(): lax.ppermute(hologram[:, rows - halo:], 'tile', [(i, i + 1) for i in rang...  5.04 us
    ppermute x1, starting transfers between devices, local(): lax.ppermute(hologram[:, :halo], 'tile', [(i + 1, i) for i in range(tile_...  3.64 us
  transfers between devices with their start and end apart: 3, of which 3 were waited for; matrix products, arithmetic and copies ran while one was open for 7% of the time, Pallas kernels for 6%

profile of v3, /device:TPU:4, one launch (start us, length us, event | category | flops | bytes accessed | tf_op | source)
XLA Modules:
  0.0 118.0 jit_solution(16415622580953519165)
XLA Ops:
  7.2 2.4 %fusion.1 = (bf16[2,48,4096]{2,1,0:T(8,128)(2,1)}, bf16[2,48,4096]{2,1,0:T(8,128)(2,1)S(1)}) fusion(bf16[2,64,4096]{2,1,0:T(8,128)(2,1)} %param.3), kind=kLoop, calls=%fused_computation.13 | loop fusion | bytes 3145728 | tf_op jit(solution)/shard_map/slice | solution.py:228
  9.6 1.9 %collective-permute-start = (bf16[2,48,4096]{2,1,0:T(8,128)(2,1)S(1)}, bf16[2,48,4096]{2,1,0:T(8,128)(2,1)S(1)}, u32[]{:S(2)}, u32[]{:S(2)}) collective-permute-start(bf16[2,48,4096]{2,1,0:T(8,128)(2,1)S(1)} %get-tuple-element.12), channel_id=1, source_target_pairs={{0,1},{1,2},{2,3},{4,5},{5,6},{6,7},{8,9},{9,10},{10,11},{12,13},{... | collective-permute-start | bytes 2359304 | tf_op jit(solution)/shard_map/ppermute | solution.py:225
  11.5 0.6 fusion
  12.2 0.6 copy-done
  12.9 3.6 %collective-permute-start.1 = (bf16[2,48,4096]{2,1,0:T(8,128)(2,1)}, bf16[2,48,4096]{2,1,0:T(8,128)(2,1)}, u32[]{:S(2)}, u32[]{:S(2)}) collective-permute-start(bf16[2,48,4096]{2,1,0:T(8,128)(2,1)} %get-tuple-element.11), channel_id=1, source_target_pairs={{1,0},{2,1},{3,2},{5,4},{6,5},{7,6},{9,8},{10,9},{11,10},{13,12},{... | collective-permute-start | bytes 2359304 | tf_op jit(solution)/shard_map/ppermute | solution.py:228
  16.5 0.1 copy.8
  16.6 0.6 pad_add_fusion.corner_ref
  17.3 0.6 broadcast_multiply_fusion.depth_ref
  17.9 5.0 %collective-permute-done = bf16[2,48,4096]{2,1,0:T(8,128)(2,1)S(1)} collective-permute-done((bf16[2,48,4096]{2,1,0:T(8,128)(2,1)S(1)}, bf16[2,48,4096]{2,1,0:T(8,128)(2,1)S(1)}, u32[]{:S(2)}, u32[]{:S(2)}) %collective-permute-start) | collective-permute-done | bytes 786464 | tf_op jit(solution)/shard_map/ppermute | solution.py:225
  23.0 1.3 %constant_dynamic-update-slice_fusion.1 = bf16[2,160,4096]{2,1,0:T(8,128)(2,1)S(1)} fusion(bf16[2,160,4096]{2,1,0:T(8,128)(2,1)S(1)} %constant_dynamic-update-slice_fusion.2, bf16[2,64,4096]{2,1,0:T(8,128)(2,1)} %param.3), kind=kLoop, calls=%fused_computation.6 | loop fusion | bytes 2097152
  24.3 2.0 %collective-permute-done.1 = bf16[2,48,4096]{2,1,0:T(8,128)(2,1)} collective-permute-done((bf16[2,48,4096]{2,1,0:T(8,128)(2,1)}, bf16[2,48,4096]{2,1,0:T(8,128)(2,1)}, u32[]{:S(2)}, u32[]{:S(2)}) %collective-permute-start.1) | collective-permute-done | bytes 786464 | tf_op jit(solution)/shard_map/ppermute | solution.py:228
  26.3 1.2 %constant_dynamic-update-slice_fusion = bf16[2,160,4096]{2,1,0:T(8,128)(2,1)S(1)} fusion(bf16[2,160,4096]{2,1,0:T(8,128)(2,1)S(1)} %constant_dynamic-update-slice_fusion.1, bf16[2,48,4096]{2,1,0:T(8,128)(2,1)} %collective-permute-done.1), kind=kLoop, calls=%fused_computation.5 | loop fusion | bytes 1572864 | tf_op jit(solution)/shard_map/concatenate | solution.py:229
  27.5 0.2 slice.24
  27.7 2.2 %pad.20 = bf16[2,128,4224]{2,1,0:T(8,128)(2,1)} pad(bf16[2,128,4096]{2,1,0:T(8,128)(2,1)S(1)} %slice.24, bf16[]{:T(256)} %constant.9.clone.1), padding=0_0x0_0x32_96 | pad | bytes 4259842 | tf_op jit(solution)/shard_map/jit(_pad)/pad | solution.py:232
  30.0 7.3 %shard_map.58 = f32[4,64,4096]{2,1,0:T(8,128)} custom-call(f32[4,2,256]{2,1,0:T(2,128)} %get-tuple-element.14.taps_ref, bf16[256,4224]{1,0:T(8,128)(2,1)} %bitcast.9), custom_call_target="tpu_custom_call" | custom-call | flops 3254779904 | bytes 6356992 | tf_op jit(solution)/shard_map/pallas_call | solution.py:141
  37.2 1.6 %slice.25 = bf16[2,143,4096]{2,1,0:T(8,128)(2,1)} slice(bf16[2,160,4096]{2,1,0:T(8,128)(2,1)S(1)} %constant_dynamic-update-slice_fusion), slice={[0:2], [8:151], [0:4096]} | slice | bytes 4685824 | tf_op jit(solution)/shard_map/slice | solution.py:241
  38.8 44.5 %all-reduce.6.cloned.1.call-done = f32[32,576]{1,0:T(8,128)} async-done(((f32[32,576]{1,0:T(8,128)}), f32[32,576]{1,0:T(8,128)}) %all-reduce.6.cloned.1.call-update) | async-done | bytes 73744 | tf_op jit(solution)/shard_map/psum | solution.py:204
  83.3 0.7 slice_reduce_fusion
  84.0 0.8 slice.21
  84.9 0.7 subtract_exponential_fusion
  85.6 0.7 reshape.34.taps_ref
  86.3 1.6 %copy.9.prior_ref = f32[32,80,1]{2,1,0:T(8,128)} copy(f32[32,80,1]{1,0,2:T(8,128)S(1)} %pad_bitcast_fusion) | data formatting | bytes 20480 | tf_op jit(solution)/shard_map/broadcast_in_dim | solution.py:255
  87.9 2.1 %pad_dynamic-slice_fusion = bf16[2,256,768]{2,1,0:T(8,128)(2,1)} fusion(s32[]{:T(128)S(6)} %select_n.7, bf16[2,143,4096]{2,1,0:T(8,128)(2,1)} %slice.25), kind=kLoop, calls=%fused_computation | loop fusion | bytes 3129348 | tf_op jit(solution)/shard_map/dynamic_slice | solution.py:247
  90.0 21.1 %shard_map.59 = (f32[64,512]{1,0:T(8,128)}, f32[64,512]{1,0:T(8,128)}) custom-call(s32[2]{0:T(128)} %pad_add_fusion.corner_ref, f32[32,2,256]{2,1,0:T(2,128)} %reshape.34.taps_ref, f32[32,80,1]{2,1,0:T(8,128)} %copy.9.prior_ref, f32[32,1,1]{2,1,0:T(1,128)} %broadcast_multiply_fusion.depth_ref, bf16[512,768]{1,0:T(8,128)(2,1)} %bitcast.10), custom_call_target="tpu_custom_call" | custom-call | flops 7381975040 | bytes 1196032 | tf_op jit(solution)/shard_map/pallas_call | solution.py:185
  (13 shorter events, 0.2 us)
Async XLA Ops:
  7.2 4.4 %copy-start.1 = (bf16[4,2,64]{2,1,0:T(2,128)(2,1)S(1)}, bf16[4,2,64]{2,1,0:T(2,128)(2,1)}, u32[]{:S(2)}) copy-start(bf16[4,2,64]{2,1,0:T(2,128)(2,1)} %param.4) | copy-start | bytes 3076
  7.2 5.0 %copy-start.2 = (f32[4,64]{1,0:T(4,128)S(1)}, f32[4,64]{1,0:T(4,128)}, u32[]{:S(2)}) copy-start(f32[4,64]{1,0:T(4,128)} %param.5) | copy-start | bytes 3076
  7.2 76.1 %all-reduce.6.cloned.1.call-start = ((), (), s32[]{:S(2)}) async-start(), calls=%async_computation | async-start | bytes 163840 | tf_op jit(solution)/shard_map/psum | solution.py:204
  9.6 13.3 %collective-permute-start = (bf16[2,48,4096]{2,1,0:T(8,128)(2,1)S(1)}, bf16[2,48,4096]{2,1,0:T(8,128)(2,1)S(1)}, u32[]{:S(2)}, u32[]{:S(2)}) collective-permute-start(bf16[2,48,4096]{2,1,0:T(8,128)(2,1)S(1)} %get-tuple-element.12), channel_id=1, source_target_pairs={{0,1},{1,2},{2,3},{4,5},{5,6},{6,7},{8,9},{9,10},{10,11},{12,13},{... | collective-permute-start | bytes 2359304 | tf_op jit(solution)/shard_map/ppermute | solution.py:225
  12.2 0.6 copy-start
  12.9 13.5 %collective-permute-start.1 = (bf16[2,48,4096]{2,1,0:T(8,128)(2,1)}, bf16[2,48,4096]{2,1,0:T(8,128)(2,1)}, u32[]{:S(2)}, u32[]{:S(2)}) collective-permute-start(bf16[2,48,4096]{2,1,0:T(8,128)(2,1)} %get-tuple-element.11), channel_id=1, source_target_pairs={{1,0},{2,1},{3,2},{5,4},{6,5},{7,6},{9,8},{10,9},{11,10},{13,12},{... | collective-permute-start | bytes 2359304 | tf_op jit(solution)/shard_map/ppermute | solution.py:228
Sparse Core Ops, SparseCore 0:
  13.0 70.2 all-reduce.5

commit v4 on v3

--- a/solution.py
+++ b/solution.py
@@ -197,11 +197,11 @@
 
 def gather_depth(block):
     count = lax.axis_size("depth")
-    placed = jnp.zeros((count * block.shape[0], block.shape[1]), block.dtype)
-    placed = lax.dynamic_update_slice_in_dim(
-        placed, block, lax.axis_index("depth") * block.shape[0], axis=0
-    )
-    return lax.psum(placed, "depth")
+    moved = [
+        lax.ppermute(block, "depth", [((j + shift) % count, j) for j in range(count)])
+        for shift in range(1, count)
+    ]
+    return jnp.concatenate([block, *moved], axis=0)
 
 
 def local(hologram, kernel, depth_prior):
@@ -219,7 +219,8 @@
     taps = jnp.pad(kernel.astype(jnp.float32), ((0, 0), (0, 0), (0, SPAN - TAPS)))
     packed = jnp.concatenate([taps.reshape(local_planes, 2 * SPAN), depth_prior], axis=1)
     packed_all = gather_depth(packed)
-    plane_at = jnp.arange(planes_total)
+    owner = (depth_at + jnp.arange(planes_total) // local_planes) % depth_count
+    plane_at = owner * local_planes + jnp.arange(planes_total) % local_planes
 
     halo = 48
     above = lax.ppermute(

time: 120 us -> 68.6 us (0.57)
  the two profiles are of different devices: /device:TPU:4 before, /device:TPU:1 now
where the time goes in v4:
time: 68.6 us; the launch traced here: 68.1 us
  Pallas kernels  28.3 us (41%)
  starting transfers between devices  17.5 us (26%)
  local copies, waits for them, and re-layouts  11.6 us (17%)
  waiting for transfers between devices  8.06 us (12%)
  other arithmetic  1.84 us (3%)
  between operations  0.78 us (1%)
    pallas_call x1, Pallas kernels, joining(): pl.pallas_call(body, grid_spec=grid_spec, out_shape=[jax.ShapeDtypeStruct...  21.1 us
    ppermute x7, starting transfers between devices, gather_depth(): lax.ppermute(block, 'depth', [((j + shift) % count, j) for j in range(cou...  10.4 us
    ppermute x1, waiting for transfers between devices, local(): lax.ppermute(hologram[:, :halo], 'tile', [(i + 1, i) for i in range(tile_...  8.04 us
    pallas_call x1, Pallas kernels, propagate(): pl.pallas_call(body, grid=(1,), in_specs=[pl.BlockSpec((planes, 2, SPAN),...  7.24 us
    ppermute x1, starting transfers between devices, local(): lax.ppermute(hologram[:, rows - halo:], 'tile', [(i, i + 1) for i in rang...  4.53 us
    ppermute x1, starting transfers between devices, local(): lax.ppermute(hologram[:, :halo], 'tile', [(i + 1, i) for i in range(tile_...  2.61 us
    slice x1, local copies, waits for them, and re-layouts, local(): hologram[:, :halo]  2.49 us
    pad x1, local copies, waits for them, and re-layouts, local(): window = jnp.pad(window, ((0, 0), (0, 0), (half_taps, LANE - half_taps)))  2.24 us
  transfers between devices with their start and end apart: 9, of which 1 were waited for; matrix products, arithmetic and copies ran while one was open for 5% of the time, Pallas kernels for 0%

profile of v4, /device:TPU:1, one launch (start us, length us, event | category | flops | bytes accessed | tf_op | source)
XLA Modules:
  0.0 68.1 jit_solution(1182718894715775950)
XLA Ops:
  0.7 2.5 %fusion.8 = (bf16[2,48,4096]{2,1,0:T(8,128)(2,1)S(1)}, bf16[2,48,4096]{2,1,0:T(8,128)(2,1)}) fusion(bf16[2,64,4096]{2,1,0:T(8,128)(2,1)} %param.3), kind=kLoop, calls=%fused_computation.27 | loop fusion | bytes 3145728 | tf_op jit(solution)/shard_map/slice | solution.py:229
  3.2 4.5 %collective-permute-start = (bf16[2,48,4096]{2,1,0:T(8,128)(2,1)}, bf16[2,48,4096]{2,1,0:T(8,128)(2,1)S(1)}, u32[]{:S(2)}, u32[]{:S(2)}) collective-permute-start(bf16[2,48,4096]{2,1,0:T(8,128)(2,1)} %get-tuple-element.12), channel_id=1, source_target_pairs={{0,1},{1,2},{2,3},{4,5},{5,6},{6,7},{8,9},{9,10},{10,11},{12,13},{... | collective-permute-start | bytes 2359304 | tf_op jit(solution)/shard_map/ppermute | solution.py:226
  7.7 0.6 fusion.7
  8.3 1.3 %collective-permute-start.8 = (f32[4,576]{1,0:T(4,128)S(1)}, f32[4,576]{1,0:T(4,128)S(1)}, u32[]{:S(2)}, u32[]{:S(2)}) collective-permute-start(f32[4,576]{1,0:T(4,128)S(1)} %constant_dynamic-update-slice_fusion.3), channel_id=1, source_target_pairs={{28,0},{0,4},{4,8},{8,12},{12,16},{16,20},{20,24},{24,28},{29,1},{... | collective-permute-start | bytes 27656 | tf_op jit(solution)/shard_map/ppermute | solution.py:201
  9.6 1.3 %collective-permute-start.7 = (f32[4,576]{1,0:T(4,128)S(1)}, f32[4,576]{1,0:T(4,128)S(1)}, u32[]{:S(2)}, u32[]{:S(2)}) collective-permute-start(f32[4,576]{1,0:T(4,128)S(1)} %constant_dynamic-update-slice_fusion.3), channel_id=1, source_target_pairs={{24,0},{28,4},{0,8},{4,12},{8,16},{12,20},{16,24},{20,28},{25,1},{... | collective-permute-start | bytes 27656 | tf_op jit(solution)/shard_map/ppermute | solution.py:201
  10.9 2.3 %collective-permute-start.6 = (f32[4,576]{1,0:T(4,128)S(1)}, f32[4,576]{1,0:T(4,128)S(1)}, u32[]{:S(2)}, u32[]{:S(2)}) collective-permute-start(f32[4,576]{1,0:T(4,128)S(1)} %constant_dynamic-update-slice_fusion.3), channel_id=1, source_target_pairs={{20,0},{24,4},{28,8},{0,12},{4,16},{8,20},{12,24},{16,28},{21,1},{... | collective-permute-start | bytes 27656 | tf_op jit(solution)/shard_map/ppermute | solution.py:201
  13.1 1.0 %collective-permute-start.5 = (f32[4,576]{1,0:T(4,128)S(1)}, f32[4,576]{1,0:T(4,128)S(1)}, u32[]{:S(2)}, u32[]{:S(2)}) collective-permute-start(f32[4,576]{1,0:T(4,128)S(1)} %constant_dynamic-update-slice_fusion.3), channel_id=1, source_target_pairs={{16,0},{20,4},{24,8},{28,12},{0,16},{4,20},{8,24},{12,28},{17,1},{... | collective-permute-start | bytes 27656 | tf_op jit(solution)/shard_map/ppermute | solution.py:201
  14.1 0.6 fusion.3.depth_ref
  14.7 2.3 %collective-permute-start.4 = (f32[4,576]{1,0:T(4,128)S(1)}, f32[4,576]{1,0:T(4,128)S(1)}, u32[]{:S(2)}, u32[]{:S(2)}) collective-permute-start(f32[4,576]{1,0:T(4,128)S(1)} %constant_dynamic-update-slice_fusion.3), channel_id=1, source_target_pairs={{12,0},{16,4},{20,8},{24,12},{28,16},{0,20},{4,24},{8,28},{13,1},{... | collective-permute-start | bytes 27656 | tf_op jit(solution)/shard_map/ppermute | solution.py:201
  17.1 1.1 %collective-permute-start.3 = (f32[4,576]{1,0:T(4,128)S(1)}, f32[4,576]{1,0:T(4,128)S(1)}, u32[]{:S(2)}, u32[]{:S(2)}) collective-permute-start(f32[4,576]{1,0:T(4,128)S(1)} %constant_dynamic-update-slice_fusion.3), channel_id=1, source_target_pairs={{8,0},{12,4},{16,8},{20,12},{24,16},{28,20},{0,24},{4,28},{9,1},{1... | collective-permute-start | bytes 27656 | tf_op jit(solution)/shard_map/ppermute | solution.py:201
  18.2 1.2 %collective-permute-start.2 = (f32[4,576]{1,0:T(4,128)S(1)}, f32[4,576]{1,0:T(4,128)}, u32[]{:S(2)}, u32[]{:S(2)}) collective-permute-start(f32[4,576]{1,0:T(4,128)S(1)} %constant_dynamic-update-slice_fusion.3), channel_id=1, source_target_pairs={{4,0},{8,4},{12,8},{16,12},{20,16},{24,20},{28,24},{0,28},{5,1},{9... | collective-permute-start | bytes 27656 | tf_op jit(solution)/shard_map/ppermute | solution.py:201
  19.3 0.6 pad_add_fusion.corner_ref
  19.9 2.6 %collective-permute-start.1 = (bf16[2,48,4096]{2,1,0:T(8,128)(2,1)S(1)}, bf16[2,48,4096]{2,1,0:T(8,128)(2,1)S(1)}, u32[]{:S(2)}, u32[]{:S(2)}) collective-permute-start(bf16[2,48,4096]{2,1,0:T(8,128)(2,1)S(1)} %get-tuple-element.11), channel_id=1, source_target_pairs={{1,0},{2,1},{3,2},{5,4},{6,5},{7,6},{9,8},{10,9},{11,10},{13,12},{... | collective-permute-start | bytes 2359304 | tf_op jit(solution)/shard_map/ppermute | solution.py:229
  22.5 0.6 copy-done.1
  23.1 0.6 copy-done.2
  23.7 1.5 %concatenate.11 = f32[32,576]{1,0:T(8,128)S(1)} concatenate(f32[4,576]{1,0:T(4,128)S(1)} %constant_dynamic-update-slice_fusion.3, f32[4,576]{1,0:T(4,128)} %collective-permute-done.2, f32[4,576]{1,0:T(4,128)} %copy-done.2, f32[4,576]{1,0:T(4,128)} %copy-done.1, f32[4,576]{1,0:T(4,128)S(1)} %collective-permute-done.5, f32[4,576]{1,0:T(4,128)S(1)} %collective-permute-done.6, ...), dimensions={0} | concatenate | bytes 147456 | tf_op jit(solution)/shard_map/concatenate | solution.py:204
  25.4 8.0 %collective-permute-done.1 = bf16[2,48,4096]{2,1,0:T(8,128)(2,1)S(1)} collective-permute-done((bf16[2,48,4096]{2,1,0:T(8,128)(2,1)S(1)}, bf16[2,48,4096]{2,1,0:T(8,128)(2,1)S(1)}, u32[]{:S(2)}, u32[]{:S(2)}) %collective-permute-start.1) | collective-permute-done | bytes 786464 | tf_op jit(solution)/shard_map/ppermute | solution.py:229
  33.5 0.2 slice.24
  33.9 2.2 %pad.20 = bf16[2,128,4224]{2,1,0:T(8,128)(2,1)} pad(bf16[2,128,4096]{2,1,0:T(8,128)(2,1)S(1)} %slice.24, bf16[]{:T(256)} %constant.55.clone.1), padding=0_0x0_0x32_96 | pad | bytes 4259842 | tf_op jit(solution)/shard_map/jit(_pad)/pad | solution.py:233
  36.1 7.2 %shard_map.58 = f32[4,64,4096]{2,1,0:T(8,128)} custom-call(f32[4,2,256]{2,1,0:T(2,128)} %get-tuple-element.14.taps_ref, bf16[256,4224]{1,0:T(8,128)(2,1)} %bitcast.9), custom_call_target="tpu_custom_call" | custom-call | flops 3254779904 | bytes 6356992 | tf_op jit(solution)/shard_map/pallas_call | solution.py:141
  43.4 0.7 reshape.122.taps_ref
  44.1 1.5 %copy.7.prior_ref = f32[32,80,1]{2,1,0:T(8,128)} copy(f32[32,80,1]{1,0,2:T(8,128)S(1)} %pad_bitcast_fusion) | data formatting | bytes 20480 | tf_op jit(solution)/shard_map/broadcast_in_dim | solution.py:256
  45.7 1.3 %pad_dynamic-slice_fusion = bf16[2,256,768]{2,1,0:T(8,128)(2,1)} fusion(s32[]{:T(128)S(6)} %select_n.43, bf16[2,143,4096]{2,1,0:T(8,128)(2,1)S(1)} %slice.25), kind=kLoop, calls=%fused_computation | loop fusion | bytes 3129348 | tf_op jit(solution)/shard_map/dynamic_slice | solution.py:248
  47.0 21.1 %shard_map.59 = (f32[64,512]{1,0:T(8,128)}, f32[64,512]{1,0:T(8,128)}) custom-call(s32[2]{0:T(128)} %pad_add_fusion.corner_ref, f32[32,2,256]{2,1,0:T(2,128)} %reshape.122.taps_ref, f32[32,80,1]{2,1,0:T(8,128)} %copy.7.prior_ref, f32[32,1,1]{2,1,0:T(1,128)} %fusion.3.depth_ref, bf16[512,768]{1,0:T(8,128)(2,1)} %bitcast.10), custom_call_target="tpu_custom_call" | custom-call | flops 7381975040 | bytes 1196032 | tf_op jit(solution)/shard_map/pallas_call | solution.py:185
  (27 shorter events, 0.5 us)
Async XLA Ops:
  0.6 24.7 %copy-start = (bf16[2,64,4096]{2,1,0:T(8,128)(2,1)S(1)}, bf16[2,64,4096]{2,1,0:T(8,128)(2,1)}, u32[]{:S(2)}) copy-start(bf16[2,64,4096]{2,1,0:T(8,128)(2,1)} %param.3) | copy-start | bytes 3145732
  0.6 7.0 %copy-start.3 = (bf16[4,2,64]{2,1,0:T(2,128)(2,1)S(1)}, bf16[4,2,64]{2,1,0:T(2,128)(2,1)}, u32[]{:S(2)}) copy-start(bf16[4,2,64]{2,1,0:T(2,128)(2,1)} %param.4) | copy-start | bytes 3076
  0.7 7.7 %copy-start.4 = (f32[4,64]{1,0:T(4,128)S(1)}, f32[4,64]{1,0:T(4,128)}, u32[]{:S(2)}) copy-start(f32[4,64]{1,0:T(4,128)} %param.5) | copy-start | bytes 3076
  3.2 22.1 %collective-permute-start = (bf16[2,48,4096]{2,1,0:T(8,128)(2,1)}, bf16[2,48,4096]{2,1,0:T(8,128)(2,1)S(1)}, u32[]{:S(2)}, u32[]{:S(2)}) collective-permute-start(bf16[2,48,4096]{2,1,0:T(8,128)(2,1)} %get-tuple-element.12), channel_id=1, source_target_pairs={{0,1},{1,2},{2,3},{4,5},{5,6},{6,7},{8,9},{9,10},{10,11},{12,13},{... | collective-permute-start | bytes 2359304 | tf_op jit(solution)/shard_map/ppermute | solution.py:226
  8.3 6.4 %collective-permute-start.8 = (f32[4,576]{1,0:T(4,128)S(1)}, f32[4,576]{1,0:T(4,128)S(1)}, u32[]{:S(2)}, u32[]{:S(2)}) collective-permute-start(f32[4,576]{1,0:T(4,128)S(1)} %constant_dynamic-update-slice_fusion.3), channel_id=1, source_target_pairs={{28,0},{0,4},{4,8},{8,12},{12,16},{16,20},{20,24},{24,28},{29,1},{... | collective-permute-start | bytes 27656 | tf_op jit(solution)/shard_map/ppermute | solution.py:201
  9.6 7.5 %collective-permute-start.7 = (f32[4,576]{1,0:T(4,128)S(1)}, f32[4,576]{1,0:T(4,128)S(1)}, u32[]{:S(2)}, u32[]{:S(2)}) collective-permute-start(f32[4,576]{1,0:T(4,128)S(1)} %constant_dynamic-update-slice_fusion.3), channel_id=1, source_target_pairs={{24,0},{28,4},{0,8},{4,12},{8,16},{12,20},{16,24},{20,28},{25,1},{... | collective-permute-start | bytes 27656 | tf_op jit(solution)/shard_map/ppermute | solution.py:201
  10.9 7.3 %collective-permute-start.6 = (f32[4,576]{1,0:T(4,128)S(1)}, f32[4,576]{1,0:T(4,128)S(1)}, u32[]{:S(2)}, u32[]{:S(2)}) collective-permute-start(f32[4,576]{1,0:T(4,128)S(1)} %constant_dynamic-update-slice_fusion.3), channel_id=1, source_target_pairs={{20,0},{24,4},{28,8},{0,12},{4,16},{8,20},{12,24},{16,28},{21,1},{... | collective-permute-start | bytes 27656 | tf_op jit(solution)/shard_map/ppermute | solution.py:201
  13.1 6.7 %collective-permute-start.5 = (f32[4,576]{1,0:T(4,128)S(1)}, f32[4,576]{1,0:T(4,128)S(1)}, u32[]{:S(2)}, u32[]{:S(2)}) collective-permute-start(f32[4,576]{1,0:T(4,128)S(1)} %constant_dynamic-update-slice_fusion.3), channel_id=1, source_target_pairs={{16,0},{20,4},{24,8},{28,12},{0,16},{4,20},{8,24},{12,28},{17,1},{... | collective-permute-start | bytes 27656 | tf_op jit(solution)/shard_map/ppermute | solution.py:201
  14.7 7.8 %collective-permute-start.4 = (f32[4,576]{1,0:T(4,128)S(1)}, f32[4,576]{1,0:T(4,128)S(1)}, u32[]{:S(2)}, u32[]{:S(2)}) collective-permute-start(f32[4,576]{1,0:T(4,128)S(1)} %constant_dynamic-update-slice_fusion.3), channel_id=1, source_target_pairs={{12,0},{16,4},{20,8},{24,12},{28,16},{0,20},{4,24},{8,28},{13,1},{... | collective-permute-start | bytes 27656 | tf_op jit(solution)/shard_map/ppermute | solution.py:201
  17.1 5.5 %collective-permute-start.3 = (f32[4,576]{1,0:T(4,128)S(1)}, f32[4,576]{1,0:T(4,128)S(1)}, u32[]{:S(2)}, u32[]{:S(2)}) collective-permute-start(f32[4,576]{1,0:T(4,128)S(1)} %constant_dynamic-update-slice_fusion.3), channel_id=1, source_target_pairs={{8,0},{12,4},{16,8},{20,12},{24,16},{28,20},{0,24},{4,28},{9,1},{1... | collective-permute-start | bytes 27656 | tf_op jit(solution)/shard_map/ppermute | solution.py:201
  18.2 5.6 %collective-permute-start.2 = (f32[4,576]{1,0:T(4,128)S(1)}, f32[4,576]{1,0:T(4,128)}, u32[]{:S(2)}, u32[]{:S(2)}) collective-permute-start(f32[4,576]{1,0:T(4,128)S(1)} %constant_dynamic-update-slice_fusion.3), channel_id=1, source_target_pairs={{4,0},{8,4},{12,8},{16,12},{20,16},{24,20},{28,24},{0,28},{5,1},{9... | collective-permute-start | bytes 27656 | tf_op jit(solution)/shard_map/ppermute | solution.py:201
  19.9 13.5 %collective-permute-start.1 = (bf16[2,48,4096]{2,1,0:T(8,128)(2,1)S(1)}, bf16[2,48,4096]{2,1,0:T(8,128)(2,1)S(1)}, u32[]{:S(2)}, u32[]{:S(2)}) collective-permute-start(bf16[2,48,4096]{2,1,0:T(8,128)(2,1)S(1)} %get-tuple-element.11), channel_id=1, source_target_pairs={{1,0},{2,1},{3,2},{5,4},{6,5},{7,6},{9,8},{10,9},{11,10},{13,12},{... | collective-permute-start | bytes 2359304 | tf_op jit(solution)/shard_map/ppermute | solution.py:229
  22.5 0.6 copy-start.1
  23.1 0.6 copy-start.2

commit v5 on v4

--- a/solution.py
+++ b/solution.py
@@ -31,11 +31,15 @@
     ).astype(jnp.bfloat16)
 
 
-def across_planes(taps_ref, window_ref, n_out, n_in):
+def across_planes(taps_ref, window_ref, n_out, n_in, starts):
     group = taps_ref.shape[0]
     skewed = [skews(taps_ref, g) for g in range(group)]
     matrix = jnp.concatenate([rows_matrix(*sk, n_out, n_in) for sk in skewed], axis=0)
-    across = jnp.dot(matrix, window_ref[...], preferred_element_type=jnp.float32)
+    across = jnp.dot(
+        matrix[:, :n_in], window_ref[starts[0] : starts[0] + n_in], preferred_element_type=jnp.float32
+    ) + jnp.dot(
+        matrix[:, n_in:], window_ref[starts[1] : starts[1] + n_in], preferred_element_type=jnp.float32
+    )
     return skewed, across.astype(jnp.bfloat16)
 
 
@@ -69,8 +73,8 @@
     return field[:, :LANE] * field[:, :LANE] + field[:, LANE:] * field[:, LANE:]
 
 
-def propagate_kernel(taps_ref, window_ref, out_ref, *, n_out, n_in, block_count):
-    skewed, across = across_planes(taps_ref, window_ref, n_out, n_in)
+def propagate_kernel(taps_ref, window_ref, out_ref, *, n_out, n_in, block_count, starts):
+    skewed, across = across_planes(taps_ref, window_ref, n_out, n_in, starts)
     for g, (skew_re, skew_im) in enumerate(skewed):
         intensity = column_intensity(
             across[2 * n_out * g : 2 * n_out * (g + 1)], skew_re, skew_im, n_out, block_count
@@ -91,7 +95,7 @@
         weighted_ref[...] = jnp.zeros(weighted_ref.shape, jnp.float32)
         placed_ref[...] = jnp.zeros(placed_ref.shape, jnp.float32)
 
-    skewed, across = across_planes(taps_ref, window_ref, n_out, n_in)
+    skewed, across = across_planes(taps_ref, window_ref, n_out, n_in, (0, n_in))
     height, width = n_out, block_count * LANE
     row_at = corner_ref[0] + lax.broadcasted_iota(jnp.int32, (height, width), 0)
     col_at = corner_ref[1] + lax.broadcasted_iota(jnp.int32, (height, width), 1)
@@ -129,13 +133,15 @@
         mean_ref[...] = cropped(placed_ref[...] / total_ref[...])
 
 
-def propagate(taps, window, n_out):
+def propagate(taps, window, n_out, first_row):
     planes = taps.shape[0]
-    _, n_in, width = window.shape
+    _, window_rows, width = window.shape
+    n_in = n_out + TAPS
     block_count = width // LANE - 1
-    stacked = window.reshape(2 * n_in, width)
+    stacked = window.reshape(2 * window_rows, width)
     body = functools.partial(
-        propagate_kernel, n_out=n_out, n_in=n_in, block_count=block_count
+        propagate_kernel, n_out=n_out, n_in=n_in, block_count=block_count,
+        starts=(first_row, window_rows + first_row),
     )
     flops = 2 * planes * (2 * n_out * 2 * n_in * width + block_count * n_out * 4 * LANE * SPAN)
     return pl.pallas_call(
@@ -143,7 +149,7 @@
         grid=(1,),
         in_specs=[
             pl.BlockSpec((planes, 2, SPAN), lambda p: (0, 0, 0)),
-            pl.BlockSpec((2 * n_in, width), lambda p: (0, 0)),
+            pl.BlockSpec((2 * window_rows, width), lambda p: (0, 0)),
         ],
         out_specs=pl.BlockSpec((planes, n_out, block_count * LANE), lambda p: (0, 0, 0)),
         out_shape=jax.ShapeDtypeStruct((planes, n_out, block_count * LANE), jnp.float32),
@@ -197,11 +203,16 @@
 
 def gather_depth(block):
     count = lax.axis_size("depth")
-    moved = [
-        lax.ppermute(block, "depth", [((j + shift) % count, j) for j in range(count)])
-        for shift in range(1, count)
-    ]
-    return jnp.concatenate([block, *moved], axis=0)
+    have = 1
+    while have < count:
+        moved = [
+            lax.ppermute(block, "depth", [((j + have * m) % count, j) for j in range(count)])
+            for m in range(1, 4)
+            if have * m < count
+        ]
+        block = jnp.concatenate([block, *moved], axis=0)
+        have *= 1 + len(moved)
+    return block[: count * (block.shape[0] // have)]
 
 
 def local(hologram, kernel, depth_prior):
@@ -223,15 +234,14 @@
     plane_at = owner * local_planes + jnp.arange(planes_total) % local_planes
 
     halo = 48
+    padded = jnp.pad(hologram, ((0, 0), (0, 0), (half_taps, LANE - half_taps)))
     above = lax.ppermute(
-        hologram[:, rows - halo :], "tile", [(i, i + 1) for i in range(tile_count - 1)]
-    )
-    below = lax.ppermute(hologram[:, :halo], "tile", [(i + 1, i) for i in range(tile_count - 1)])
-    extended = jnp.concatenate([above, hologram, below], axis=1)
-
-    window = extended[:, halo - half_taps : halo - half_taps + LANE]
-    window = jnp.pad(window, ((0, 0), (0, 0), (half_taps, LANE - half_taps)))
-    plane_stack = propagate(taps, window, rows)
+        padded[:, rows - halo :], "tile", [(i, i + 1) for i in range(tile_count - 1)]
+    )
+    below = lax.ppermute(padded[:, :halo], "tile", [(i + 1, i) for i in range(tile_count - 1)])
+    extended = jnp.concatenate([above, padded, below], axis=1)
+
+    plane_stack = propagate(taps, extended, rows, halo - half_taps)
     plane_stack, packed_all = lax.optimization_barrier((plane_stack, packed_all))
     taps_all = packed_all[:, : 2 * SPAN].reshape(planes_total, 2, SPAN)
     prior_all = packed_all[:, 2 * SPAN :]
@@ -239,7 +249,7 @@
     lead_rows = 8
     n_out = rows + 2 * lead_rows
     first = halo - half_taps - lead_rows
-    window = extended[:, first : first + n_out + TAPS - 1]
+    window = extended[:, first : first + n_out + TAPS - 1, half_taps : half_taps + col_total]
     lead = LANE // 2 + half_taps
     width = own_cols + 2 * LANE
     window = jnp.pad(

time: 68.6 us -> 65.7 us (0.958)
  the two profiles are of different devices: /device:TPU:1 before, /device:TPU:4 now
where the time goes in v5:
time: 65.7 us; the launch traced here: 65.3 us
  Pallas kernels  29.7 us (45%)
  local copies, waits for them, and re-layouts  12.9 us (20%)
  starting transfers between devices  12.7 us (19%)
  other arithmetic  4.84 us (7%)
  waiting for transfers between devices  4.52 us (7%)
  between operations  0.7 us (1%)
    pallas_call x1, Pallas kernels, joining(): pl.pallas_call(body, grid_spec=grid_spec, out_shape=[jax.ShapeDtypeStruct...  21.2 us
    pallas_call x1, Pallas kernels, propagate(): pl.pallas_call(body, grid=(1,), in_specs=[pl.BlockSpec((planes, 2, SPAN),...  8.5 us
    ppermute x4, starting transfers between devices, gather_depth(): lax.ppermute(block, 'depth', [((j + have * m) % count, j) for j in range(...  7.14 us
    ppermute x4, waiting for transfers between devices, gather_depth(): lax.ppermute(block, 'depth', [((j + have * m) % count, j) for j in range(...  4.52 us
    ppermute x1, starting transfers between devices, local(): lax.ppermute(padded[:, :halo], 'tile', [(i + 1, i) for i in range(tile_co...  3.64 us
    concatenate x1, local copies, waits for them, and re-layouts, gather_depth(): block = jnp.concatenate([block, *moved], axis=0)  2.64 us
    slice x1, local copies, waits for them, and re-layouts, local(): extended[:, first:first + n_out + TAPS - 1, half_taps:half_taps + col_total]  2.38 us
    dynamic_slice x1, local copies, waits for them, and re-layouts, local(): lax.dynamic_slice_in_dim(window, depth_at * own_cols, width, axis=2)  2.14 us
  transfers between devices with their start and end apart: 6, of which 3 were waited for; matrix products, arithmetic and copies ran while one was open for 11% of the time, Pallas kernels for 0%

profile of v5, /device:TPU:4, one launch (start us, length us, event | category | flops | bytes accessed | tf_op | source)
XLA Modules:
  0.0 65.3 jit_solution(8017646727997714632)
XLA Ops:
  0.6 2.0 %pad_slice_fusion.1 = (bf16[2,48,4224]{2,1,0:T(8,128)(2,1)S(1)}, bf16[2,48,4224]{2,1,0:T(8,128)(2,1)S(1)}) fusion(bf16[2,64,4096]{2,1,0:T(8,128)(2,1)} %param.3), kind=kLoop, calls=%fused_computation.27 | loop fusion | bytes 2670592 | tf_op jit(solution)/shard_map/slice | solution.py:239
  2.7 1.9 %collective-permute-start = (bf16[2,48,4224]{2,1,0:T(8,128)(2,1)S(1)}, bf16[2,48,4224]{2,1,0:T(8,128)(2,1)S(1)}, u32[]{:S(2)}, u32[]{:S(2)}) collective-permute-start(bf16[2,48,4224]{2,1,0:T(8,128)(2,1)S(1)} %get-tuple-element.11), channel_id=1, source_target_pairs={{0,1},{1,2},{2,3},{4,5},{5,6},{6,7},{8,9},{9,10},{10,11},{12,13},{... | collective-permute-start | bytes 2433032 | tf_op jit(solution)/shard_map/ppermute | solution.py:238
  4.6 3.6 %collective-permute-start.1 = (bf16[2,48,4224]{2,1,0:T(8,128)(2,1)S(1)}, bf16[2,48,4224]{2,1,0:T(8,128)(2,1)}, u32[]{:S(2)}, u32[]{:S(2)}) collective-permute-start(bf16[2,48,4224]{2,1,0:T(8,128)(2,1)S(1)} %get-tuple-element.12), channel_id=1, source_target_pairs={{1,0},{2,1},{3,2},{5,4},{6,5},{7,6},{9,8},{10,9},{11,10},{13,12},{... | collective-permute-start | bytes 2433032 | tf_op jit(solution)/shard_map/ppermute | solution.py:241
  8.3 1.3 %fusion.7 = (f32[1,4,2,256]{3,2,1,0:T(2,128)S(1)}, f32[4,2,256]{2,1,0:T(2,128)}) fusion(bf16[4,2,64]{2,1,0:T(2,128)(2,1)} %param.4), kind=kLoop, calls=%fused_computation.24 | loop fusion | flops 2048 | bytes 17408
  9.6 3.6 %collective-permute-start.4 = (f32[4,576]{1,0:T(4,128)S(1)}, f32[4,576]{1,0:T(4,128)S(1)}, u32[]{:S(2)}, u32[]{:S(2)}) collective-permute-start(f32[4,576]{1,0:T(4,128)S(1)} %constant_dynamic-update-slice_fusion), channel_id=1, source_target_pairs={{12,0},{16,4},{20,8},{24,12},{28,16},{0,20},{4,24},{8,28},{13,1},{... | collective-permute-start | bytes 27656 | tf_op jit(solution)/shard_map/ppermute | solution.py:209
  13.1 1.3 %collective-permute-start.3 = (f32[4,576]{1,0:T(4,128)S(1)}, f32[4,576]{1,0:T(4,128)S(1)}, u32[]{:S(2)}, u32[]{:S(2)}) collective-permute-start(f32[4,576]{1,0:T(4,128)S(1)} %constant_dynamic-update-slice_fusion), channel_id=1, source_target_pairs={{8,0},{12,4},{16,8},{20,12},{24,16},{28,20},{0,24},{4,28},{9,1},{1... | collective-permute-start | bytes 27656 | tf_op jit(solution)/shard_map/ppermute | solution.py:209
  14.5 0.5 collective-permute-start.2
  15.0 0.6 fusion.3.depth_ref
  15.7 1.1 %collective-permute-done.3 = f32[4,576]{1,0:T(4,128)S(1)} collective-permute-done((f32[4,576]{1,0:T(4,128)S(1)}, f32[4,576]{1,0:T(4,128)S(1)}, u32[]{:S(2)}, u32[]{:S(2)}) %collective-permute-start.3) | collective-permute-done | bytes 9248 | tf_op jit(solution)/shard_map/ppermute | solution.py:209
  16.8 1.3 %collective-permute-done.2 = f32[4,576]{1,0:T(4,128)S(1)} collective-permute-done((f32[4,576]{1,0:T(4,128)S(1)}, f32[4,576]{1,0:T(4,128)S(1)}, u32[]{:S(2)}, u32[]{:S(2)}) %collective-permute-start.2) | collective-permute-done | bytes 9248 | tf_op jit(solution)/shard_map/ppermute | solution.py:209
  18.2 0.6 pad_maximum_fusion.1
  18.8 1.7 %collective-permute-start.5 = (f32[16,576]{1,0:T(8,128)}, f32[16,576]{1,0:T(8,128)}, u32[]{:S(2)}, u32[]{:S(2)}) collective-permute-start(f32[16,576]{1,0:T(8,128)} %pad_maximum_fusion.1), channel_id=1, source_target_pairs={{16,0},{20,4},{24,8},{28,12},{0,16},{4,20},{8,24},{12,28},{17,1},{... | collective-permute-start | bytes 110600 | tf_op jit(solution)/shard_map/ppermute | solution.py:209
  20.5 0.6 pad_add_fusion.corner_ref
  21.1 1.4 %pad.20 = bf16[2,64,4224]{2,1,0:T(8,128)(2,1)} pad(bf16[2,64,4096]{2,1,0:T(8,128)(2,1)S(1)} %copy-done.1, bf16[]{:T(256)} %constant.55.clone.1), padding=0_0x0_0x32_96 | pad | bytes 2129922 | tf_op jit(solution)/shard_map/jit(_pad)/pad | solution.py:237
  22.4 2.0 %collective-permute-done.5 = f32[16,576]{1,0:T(8,128)} collective-permute-done((f32[16,576]{1,0:T(8,128)}, f32[16,576]{1,0:T(8,128)}, u32[]{:S(2)}, u32[]{:S(2)}) %collective-permute-start.5) | collective-permute-done | bytes 36896 | tf_op jit(solution)/shard_map/ppermute | solution.py:209
  24.5 2.6 %concatenate.16 = f32[32,576]{1,0:T(8,128)} concatenate(f32[4,576]{1,0:T(4,128)S(1)} %constant_dynamic-update-slice_fusion, f32[4,576]{1,0:T(4,128)S(1)} %collective-permute-done.2, f32[4,576]{1,0:T(4,128)S(1)} %collective-permute-done.3, f32[4,576]{1,0:T(4,128)S(1)} %collective-permute-done.4, f32[16,576]{1,0:T(8,128)} %collective-permute-done.5), dimensions={0} | concatenate | bytes 147456 | tf_op jit(solution)/shard_map/concatenate | solution.py:213
  27.1 1.7 %pad_maximum_fusion = bf16[2,160,4224]{2,1,0:T(8,128)(2,1)S(1)} fusion(bf16[2,48,4224]{2,1,0:T(8,128)(2,1)} %collective-permute-done.1, bf16[2,64,4224]{2,1,0:T(8,128)(2,1)} %pad.20, bf16[2,48,4224]{2,1,0:T(8,128)(2,1)S(1)} %collective-permute-done), kind=kLoop, calls=%fused_computation.1 | loop fusion | flops 8110080 | bytes 5406720 | tf_op jit(solution)/shard_map/concatenate | solution.py:242
  28.8 2.4 %slice.20 = bf16[2,143,4096]{2,1,0:T(8,128)(2,1)} slice(bf16[2,160,4224]{2,1,0:T(8,128)(2,1)S(1)} %pad_maximum_fusion), slice={[0:2], [8:151], [32:4128]} | slice | bytes 4685824 | tf_op jit(solution)/shard_map/slice | solution.py:252
  31.2 8.5 %shard_map.58 = f32[4,64,4096]{2,1,0:T(8,128)} custom-call(f32[4,2,256]{2,1,0:T(2,128)} %get-tuple-element.14.taps_ref, bf16[320,4224]{1,0:T(8,128)(2,1)} %bitcast.9), custom_call_target="tpu_custom_call" | custom-call | flops 3254779904 | bytes 6897664 | tf_op jit(solution)/shard_map/pallas_call | solution.py:147
  39.7 0.7 %reshape.122.taps_ref = f32[32,2,256]{2,1,0:T(2,128)} reshape(f32[32,512]{1,0:T(8,128)S(1)} %slice-done) | data formatting | bytes 131072 | tf_op jit(solution)/shard_map/reshape | solution.py:246
  40.4 0.1 pad_bitcast_fusion
  40.5 1.6 %copy.7.prior_ref = f32[32,80,1]{2,1,0:T(8,128)} copy(f32[32,80,1]{1,0,2:T(8,128)S(1)} %pad_bitcast_fusion) | data formatting | bytes 20480 | tf_op jit(solution)/shard_map/broadcast_in_dim | solution.py:266
  42.0 2.1 %pad_dynamic-slice_fusion = bf16[2,256,768]{2,1,0:T(8,128)(2,1)} fusion(s32[]{:T(128)S(6)} %select_n.43, bf16[2,143,4096]{2,1,0:T(8,128)(2,1)} %slice.20), kind=kLoop, calls=%fused_computation | loop fusion | bytes 3129348 | tf_op jit(solution)/shard_map/dynamic_slice | solution.py:258
  44.2 21.2 %shard_map.59 = (f32[64,512]{1,0:T(8,128)}, f32[64,512]{1,0:T(8,128)}) custom-call(s32[2]{0:T(128)} %pad_add_fusion.corner_ref, f32[32,2,256]{2,1,0:T(2,128)} %reshape.122.taps_ref, f32[32,80,1]{2,1,0:T(8,128)} %copy.7.prior_ref, f32[32,1,1]{2,1,0:T(1,128)} %fusion.3.depth_ref, bf16[512,768]{1,0:T(8,128)(2,1)} %bitcast.10), custom_call_target="tpu_custom_call" | custom-call | flops 7381975040 | bytes 1196032 | tf_op jit(solution)/shard_map/pallas_call | solution.py:191
  (18 shorter events, 0.1 us)
Async XLA Ops:
  0.6 20.4 %copy-start.1 = (bf16[2,64,4096]{2,1,0:T(8,128)(2,1)S(1)}, bf16[2,64,4096]{2,1,0:T(8,128)(2,1)}, u32[]{:S(2)}) copy-start(bf16[2,64,4096]{2,1,0:T(8,128)(2,1)} %param.3) | copy-start | bytes 3145732
  0.6 8.9 %copy-start.3 = (f32[4,64]{1,0:T(4,128)S(1)}, f32[4,64]{1,0:T(4,128)}, u32[]{:S(2)}) copy-start(f32[4,64]{1,0:T(4,128)} %param.5) | copy-start | bytes 3076
  2.7 24.4 %collective-permute-start = (bf16[2,48,4224]{2,1,0:T(8,128)(2,1)S(1)}, bf16[2,48,4224]{2,1,0:T(8,128)(2,1)S(1)}, u32[]{:S(2)}, u32[]{:S(2)}) collective-permute-start(bf16[2,48,4224]{2,1,0:T(8,128)(2,1)S(1)} %get-tuple-element.11), channel_id=1, source_target_pairs={{0,1},{1,2},{2,3},{4,5},{5,6},{6,7},{8,9},{9,10},{10,11},{12,13},{... | collective-permute-start | bytes 2433032 | tf_op jit(solution)/shard_map/ppermute | solution.py:238
  4.6 22.5 %collective-permute-start.1 = (bf16[2,48,4224]{2,1,0:T(8,128)(2,1)S(1)}, bf16[2,48,4224]{2,1,0:T(8,128)(2,1)}, u32[]{:S(2)}, u32[]{:S(2)}) collective-permute-start(bf16[2,48,4224]{2,1,0:T(8,128)(2,1)S(1)} %get-tuple-element.12), channel_id=1, source_target_pairs={{1,0},{2,1},{3,2},{5,4},{6,5},{7,6},{9,8},{10,9},{11,10},{13,12},{... | collective-permute-start | bytes 2433032 | tf_op jit(solution)/shard_map/ppermute | solution.py:241
  9.6 6.1 %collective-permute-start.4 = (f32[4,576]{1,0:T(4,128)S(1)}, f32[4,576]{1,0:T(4,128)S(1)}, u32[]{:S(2)}, u32[]{:S(2)}) collective-permute-start(f32[4,576]{1,0:T(4,128)S(1)} %constant_dynamic-update-slice_fusion), channel_id=1, source_target_pairs={{12,0},{16,4},{20,8},{24,12},{28,16},{0,20},{4,24},{8,28},{13,1},{... | collective-permute-start | bytes 27656 | tf_op jit(solution)/shard_map/ppermute | solution.py:209
  13.1 3.7 %collective-permute-start.3 = (f32[4,576]{1,0:T(4,128)S(1)}, f32[4,576]{1,0:T(4,128)S(1)}, u32[]{:S(2)}, u32[]{:S(2)}) collective-permute-start(f32[4,576]{1,0:T(4,128)S(1)} %constant_dynamic-update-slice_fusion), channel_id=1, source_target_pairs={{8,0},{12,4},{16,8},{20,12},{24,16},{28,20},{0,24},{4,28},{9,1},{1... | collective-permute-start | bytes 27656 | tf_op jit(solution)/shard_map/ppermute | solution.py:209
  14.5 3.7 %collective-permute-start.2 = (f32[4,576]{1,0:T(4,128)S(1)}, f32[4,576]{1,0:T(4,128)S(1)}, u32[]{:S(2)}, u32[]{:S(2)}) collective-permute-start(f32[4,576]{1,0:T(4,128)S(1)} %constant_dynamic-update-slice_fusion), channel_id=1, source_target_pairs={{4,0},{8,4},{12,8},{16,12},{20,16},{24,20},{28,24},{0,28},{5,1},{9... | collective-permute-start | bytes 27656 | tf_op jit(solution)/shard_map/ppermute | solution.py:209
  18.8 5.7 %collective-permute-start.5 = (f32[16,576]{1,0:T(8,128)}, f32[16,576]{1,0:T(8,128)}, u32[]{:S(2)}, u32[]{:S(2)}) collective-permute-start(f32[16,576]{1,0:T(8,128)} %pad_maximum_fusion.1), channel_id=1, source_target_pairs={{16,0},{20,4},{24,8},{28,12},{0,16},{4,20},{8,24},{12,28},{17,1},{... | collective-permute-start | bytes 110600 | tf_op jit(solution)/shard_map/ppermute | solution.py:209
  28.8 2.4 %copy-start = (bf16[2,160,4224]{2,1,0:T(8,128)(2,1)}, bf16[2,160,4224]{2,1,0:T(8,128)(2,1)S(1)}, u32[]{:S(2)}) copy-start(bf16[2,160,4224]{2,1,0:T(8,128)(2,1)S(1)} %pad_maximum_fusion) | copy-start | bytes 8110084
  31.2 8.5 %copy-start.2 = (f32[32,576]{1,0:T(8,128)S(1)}, f32[32,576]{1,0:T(8,128)}, u32[]{:S(2)}) copy-start(f32[32,576]{1,0:T(8,128)} %concatenate.16) | copy-start | bytes 221188
  31.2 8.5 %slice-start = ((f32[32,576]{1,0:T(8,128)}), f32[32,512]{1,0:T(8,128)S(1)}, s32[]{:S(2)}) async-start(f32[32,576]{1,0:T(8,128)} %concatenate.16), calls=%async_computation | async-start | bytes 131072 | tf_op jit(solution)/shard_map/slice | solution.py:246

commit v6 on v5

--- a/solution.py
+++ b/solution.py
@@ -146,12 +146,12 @@
     flops = 2 * planes * (2 * n_out * 2 * n_in * width + block_count * n_out * 4 * LANE * SPAN)
     return pl.pallas_call(
         body,
-        grid=(1,),
+        grid=(planes,),
         in_specs=[
-            pl.BlockSpec((planes, 2, SPAN), lambda p: (0, 0, 0)),
+            pl.BlockSpec((1, 2, SPAN), lambda p: (p, 0, 0)),
             pl.BlockSpec((2 * window_rows, width), lambda p: (0, 0)),
         ],
-        out_specs=pl.BlockSpec((planes, n_out, block_count * LANE), lambda p: (0, 0, 0)),
+        out_specs=pl.BlockSpec((1, n_out, block_count * LANE), lambda p: (p, 0, 0)),
         out_shape=jax.ShapeDtypeStruct((planes, n_out, block_count * LANE), jnp.float32),
         cost_estimate=pl.CostEstimate(
             flops=flops,
@@ -163,7 +163,7 @@
 
 def joining(corner, taps, prior, depth_values, window, n_out, bounds, crop, out_shape):
     planes = taps.shape[0]
-    group = 8 if planes % 8 == 0 else planes
+    group = 16 if planes % 16 == 0 else planes
     _, n_in, width = window.shape
     block_count = width // LANE - 1
     stacked = window.reshape(2 * n_in, width)

time: 65.7 us -> 64.6 us (0.983)
  Pallas kernels: 29.7 us -> 28.5 us
    pallas_call x1, Pallas kernels: 21.2 us -> 20.2 us  [joining(): pl.pallas_call(body, grid_spec=grid_spec, out_shape=[jax.ShapeDtypeStruct...]
where the time goes in v6:
time: 64.6 us; the launch traced here: 64.2 us
  Pallas kernels  28.5 us (44%)
  local copies, waits for them, and re-layouts  12.9 us (20%)
  starting transfers between devices  12.7 us (20%)
  other arithmetic  4.84 us (7%)
  waiting for transfers between devices  4.52 us (7%)
  between operations  0.7 us (1%)
    pallas_call x1, Pallas kernels, joining(): pl.pallas_call(body, grid_spec=grid_spec, out_shape=[jax.ShapeDtypeStruct...  20.2 us
    pallas_call x1, Pallas kernels, propagate(): pl.pallas_call(body, grid=(planes,), in_specs=[pl.BlockSpec((1, 2, SPAN),...  8.33 us
    ppermute x4, starting transfers between devices, gather_depth(): lax.ppermute(block, 'depth', [((j + have * m) % count, j) for j in range(...  7.14 us
    ppermute x4, waiting for transfers between devices, gather_depth(): lax.ppermute(block, 'depth', [((j + have * m) % count, j) for j in range(...  4.52 us
    ppermute x1, starting transfers between devices, local(): lax.ppermute(padded[:, :halo], 'tile', [(i + 1, i) for i in range(tile_co...  3.64 us
    concatenate x1, local copies, waits for them, and re-layouts, gather_depth(): block = jnp.concatenate([block, *moved], axis=0)  2.64 us
    slice x1, local copies, waits for them, and re-layouts, local(): extended[:, first:first + n_out + TAPS - 1, half_taps:half_taps + col_total]  2.38 us
    dynamic_slice x1, local copies, waits for them, and re-layouts, local(): lax.dynamic_slice_in_dim(window, depth_at * own_cols, width, axis=2)  2.14 us
  transfers between devices with their start and end apart: 6, of which 3 were waited for; matrix products, arithmetic and copies ran while one was open for 11% of the time, Pallas kernels for 0%

profile of v6, /device:TPU:4, one launch (start us, length us, event | category | flops | bytes accessed | tf_op | source)
XLA Modules:
  0.0 64.2 jit_solution(11880957998126665837)
XLA Ops:
  0.6 2.0 %pad_slice_fusion.1 = (bf16[2,48,4224]{2,1,0:T(8,128)(2,1)S(1)}, bf16[2,48,4224]{2,1,0:T(8,128)(2,1)S(1)}) fusion(bf16[2,64,4096]{2,1,0:T(8,128)(2,1)} %param.3), kind=kLoop, calls=%fused_computation.27 | loop fusion | bytes 2670592 | tf_op jit(solution)/shard_map/slice | solution.py:239
  2.7 1.9 %collective-permute-start = (bf16[2,48,4224]{2,1,0:T(8,128)(2,1)S(1)}, bf16[2,48,4224]{2,1,0:T(8,128)(2,1)S(1)}, u32[]{:S(2)}, u32[]{:S(2)}) collective-permute-start(bf16[2,48,4224]{2,1,0:T(8,128)(2,1)S(1)} %get-tuple-element.11), channel_id=1, source_target_pairs={{0,1},{1,2},{2,3},{4,5},{5,6},{6,7},{8,9},{9,10},{10,11},{12,13},{... | collective-permute-start | bytes 2433032 | tf_op jit(solution)/shard_map/ppermute | solution.py:238
  4.6 3.6 %collective-permute-start.1 = (bf16[2,48,4224]{2,1,0:T(8,128)(2,1)S(1)}, bf16[2,48,4224]{2,1,0:T(8,128)(2,1)}, u32[]{:S(2)}, u32[]{:S(2)}) collective-permute-start(bf16[2,48,4224]{2,1,0:T(8,128)(2,1)S(1)} %get-tuple-element.12), channel_id=1, source_target_pairs={{1,0},{2,1},{3,2},{5,4},{6,5},{7,6},{9,8},{10,9},{11,10},{13,12},{... | collective-permute-start | bytes 2433032 | tf_op jit(solution)/shard_map/ppermute | solution.py:241
  8.3 1.3 %fusion.7 = (f32[1,4,2,256]{3,2,1,0:T(2,128)S(1)}, f32[4,2,256]{2,1,0:T(2,128)}) fusion(bf16[4,2,64]{2,1,0:T(2,128)(2,1)} %param.4), kind=kLoop, calls=%fused_computation.24 | loop fusion | flops 2048 | bytes 17408
  9.6 3.6 %collective-permute-start.4 = (f32[4,576]{1,0:T(4,128)S(1)}, f32[4,576]{1,0:T(4,128)S(1)}, u32[]{:S(2)}, u32[]{:S(2)}) collective-permute-start(f32[4,576]{1,0:T(4,128)S(1)} %constant_dynamic-update-slice_fusion), channel_id=1, source_target_pairs={{12,0},{16,4},{20,8},{24,12},{28,16},{0,20},{4,24},{8,28},{13,1},{... | collective-permute-start | bytes 27656 | tf_op jit(solution)/shard_map/ppermute | solution.py:209
  13.1 1.3 %collective-permute-start.3 = (f32[4,576]{1,0:T(4,128)S(1)}, f32[4,576]{1,0:T(4,128)S(1)}, u32[]{:S(2)}, u32[]{:S(2)}) collective-permute-start(f32[4,576]{1,0:T(4,128)S(1)} %constant_dynamic-update-slice_fusion), channel_id=1, source_target_pairs={{8,0},{12,4},{16,8},{20,12},{24,16},{28,20},{0,24},{4,28},{9,1},{1... | collective-permute-start | bytes 27656 | tf_op jit(solution)/shard_map/ppermute | solution.py:209
  14.5 0.5 collective-permute-start.2
  15.0 0.6 fusion.3.depth_ref
  15.7 1.1 %collective-permute-done.3 = f32[4,576]{1,0:T(4,128)S(1)} collective-permute-done((f32[4,576]{1,0:T(4,128)S(1)}, f32[4,576]{1,0:T(4,128)S(1)}, u32[]{:S(2)}, u32[]{:S(2)}) %collective-permute-start.3) | collective-permute-done | bytes 9248 | tf_op jit(solution)/shard_map/ppermute | solution.py:209
  16.8 1.3 %collective-permute-done.2 = f32[4,576]{1,0:T(4,128)S(1)} collective-permute-done((f32[4,576]{1,0:T(4,128)S(1)}, f32[4,576]{1,0:T(4,128)S(1)}, u32[]{:S(2)}, u32[]{:S(2)}) %collective-permute-start.2) | collective-permute-done | bytes 9248 | tf_op jit(solution)/shard_map/ppermute | solution.py:209
  18.2 0.6 pad_maximum_fusion.1
  18.8 1.7 %collective-permute-start.5 = (f32[16,576]{1,0:T(8,128)}, f32[16,576]{1,0:T(8,128)}, u32[]{:S(2)}, u32[]{:S(2)}) collective-permute-start(f32[16,576]{1,0:T(8,128)} %pad_maximum_fusion.1), channel_id=1, source_target_pairs={{16,0},{20,4},{24,8},{28,12},{0,16},{4,20},{8,24},{12,28},{17,1},{... | collective-permute-start | bytes 110600 | tf_op jit(solution)/shard_map/ppermute | solution.py:209
  20.5 0.6 pad_add_fusion.corner_ref
  21.1 1.4 %pad.20 = bf16[2,64,4224]{2,1,0:T(8,128)(2,1)} pad(bf16[2,64,4096]{2,1,0:T(8,128)(2,1)S(1)} %copy-done.1, bf16[]{:T(256)} %constant.55.clone.1), padding=0_0x0_0x32_96 | pad | bytes 2129922 | tf_op jit(solution)/shard_map/jit(_pad)/pad | solution.py:237
  22.4 2.0 %collective-permute-done.5 = f32[16,576]{1,0:T(8,128)} collective-permute-done((f32[16,576]{1,0:T(8,128)}, f32[16,576]{1,0:T(8,128)}, u32[]{:S(2)}, u32[]{:S(2)}) %collective-permute-start.5) | collective-permute-done | bytes 36896 | tf_op jit(solution)/shard_map/ppermute | solution.py:209
  24.5 2.6 %concatenate.16 = f32[32,576]{1,0:T(8,128)} concatenate(f32[4,576]{1,0:T(4,128)S(1)} %constant_dynamic-update-slice_fusion, f32[4,576]{1,0:T(4,128)S(1)} %collective-permute-done.2, f32[4,576]{1,0:T(4,128)S(1)} %collective-permute-done.3, f32[4,576]{1,0:T(4,128)S(1)} %collective-permute-done.4, f32[16,576]{1,0:T(8,128)} %collective-permute-done.5), dimensions={0} | concatenate | bytes 147456 | tf_op jit(solution)/shard_map/concatenate | solution.py:213
  27.1 1.7 %pad_maximum_fusion = bf16[2,160,4224]{2,1,0:T(8,128)(2,1)S(1)} fusion(bf16[2,48,4224]{2,1,0:T(8,128)(2,1)} %collective-permute-done.1, bf16[2,64,4224]{2,1,0:T(8,128)(2,1)} %pad.20, bf16[2,48,4224]{2,1,0:T(8,128)(2,1)S(1)} %collective-permute-done), kind=kLoop, calls=%fused_computation.1 | loop fusion | flops 8110080 | bytes 5406720 | tf_op jit(solution)/shard_map/concatenate | solution.py:242
  28.8 2.4 %slice.20 = bf16[2,143,4096]{2,1,0:T(8,128)(2,1)} slice(bf16[2,160,4224]{2,1,0:T(8,128)(2,1)S(1)} %pad_maximum_fusion), slice={[0:2], [8:151], [32:4128]} | slice | bytes 4685824 | tf_op jit(solution)/shard_map/slice | solution.py:252
  31.2 8.3 %shard_map.58 = f32[4,64,4096]{2,1,0:T(8,128)} custom-call(f32[4,2,256]{2,1,0:T(2,128)} %get-tuple-element.14.taps_ref, bf16[320,4224]{1,0:T(8,128)(2,1)} %bitcast.9), custom_call_target="tpu_custom_call" | custom-call | flops 3254779904 | bytes 6897664 | tf_op jit(solution)/shard_map/pallas_call | solution.py:147
  39.5 0.7 %reshape.122.taps_ref = f32[32,2,256]{2,1,0:T(2,128)} reshape(f32[32,512]{1,0:T(8,128)S(1)} %slice-done) | data formatting | bytes 131072 | tf_op jit(solution)/shard_map/reshape | solution.py:246
  40.2 0.1 pad_bitcast_fusion
  40.3 1.6 %copy.7.prior_ref = f32[32,80,1]{2,1,0:T(8,128)} copy(f32[32,80,1]{1,0,2:T(8,128)S(1)} %pad_bitcast_fusion) | data formatting | bytes 20480 | tf_op jit(solution)/shard_map/broadcast_in_dim | solution.py:266
  41.8 2.1 %pad_dynamic-slice_fusion = bf16[2,256,768]{2,1,0:T(8,128)(2,1)} fusion(s32[]{:T(128)S(6)} %select_n.43, bf16[2,143,4096]{2,1,0:T(8,128)(2,1)} %slice.20), kind=kLoop, calls=%fused_computation | loop fusion | bytes 3129348 | tf_op jit(solution)/shard_map/dynamic_slice | solution.py:258
  44.0 20.2 %shard_map.59 = (f32[64,512]{1,0:T(8,128)}, f32[64,512]{1,0:T(8,128)}) custom-call(s32[2]{0:T(128)} %pad_add_fusion.corner_ref, f32[32,2,256]{2,1,0:T(2,128)} %reshape.122.taps_ref, f32[32,80,1]{2,1,0:T(8,128)} %copy.7.prior_ref, f32[32,1,1]{2,1,0:T(1,128)} %fusion.3.depth_ref, bf16[512,768]{1,0:T(8,128)(2,1)} %bitcast.10), custom_call_target="tpu_custom_call" | custom-call | flops 7381975040 | bytes 1196032 | tf_op jit(solution)/shard_map/pallas_call | solution.py:191
  (18 shorter events, 0.1 us)
Async XLA Ops:
  0.6 20.4 %copy-start.1 = (bf16[2,64,4096]{2,1,0:T(8,128)(2,1)S(1)}, bf16[2,64,4096]{2,1,0:T(8,128)(2,1)}, u32[]{:S(2)}) copy-start(bf16[2,64,4096]{2,1,0:T(8,128)(2,1)} %param.3) | copy-start | bytes 3145732
  0.6 8.9 %copy-start.3 = (f32[4,64]{1,0:T(4,128)S(1)}, f32[4,64]{1,0:T(4,128)}, u32[]{:S(2)}) copy-start(f32[4,64]{1,0:T(4,128)} %param.5) | copy-start | bytes 3076
  2.7 24.4 %collective-permute-start = (bf16[2,48,4224]{2,1,0:T(8,128)(2,1)S(1)}, bf16[2,48,4224]{2,1,0:T(8,128)(2,1)S(1)}, u32[]{:S(2)}, u32[]{:S(2)}) collective-permute-start(bf16[2,48,4224]{2,1,0:T(8,128)(2,1)S(1)} %get-tuple-element.11), channel_id=1, source_target_pairs={{0,1},{1,2},{2,3},{4,5},{5,6},{6,7},{8,9},{9,10},{10,11},{12,13},{... | collective-permute-start | bytes 2433032 | tf_op jit(solution)/shard_map/ppermute | solution.py:238
  4.6 22.5 %collective-permute-start.1 = (bf16[2,48,4224]{2,1,0:T(8,128)(2,1)S(1)}, bf16[2,48,4224]{2,1,0:T(8,128)(2,1)}, u32[]{:S(2)}, u32[]{:S(2)}) collective-permute-start(bf16[2,48,4224]{2,1,0:T(8,128)(2,1)S(1)} %get-tuple-element.12), channel_id=1, source_target_pairs={{1,0},{2,1},{3,2},{5,4},{6,5},{7,6},{9,8},{10,9},{11,10},{13,12},{... | collective-permute-start | bytes 2433032 | tf_op jit(solution)/shard_map/ppermute | solution.py:241
  9.6 6.1 %collective-permute-start.4 = (f32[4,576]{1,0:T(4,128)S(1)}, f32[4,576]{1,0:T(4,128)S(1)}, u32[]{:S(2)}, u32[]{:S(2)}) collective-permute-start(f32[4,576]{1,0:T(4,128)S(1)} %constant_dynamic-update-slice_fusion), channel_id=1, source_target_pairs={{12,0},{16,4},{20,8},{24,12},{28,16},{0,20},{4,24},{8,28},{13,1},{... | collective-permute-start | bytes 27656 | tf_op jit(solution)/shard_map/ppermute | solution.py:209
  13.1 3.7 %collective-permute-start.3 = (f32[4,576]{1,0:T(4,128)S(1)}, f32[4,576]{1,0:T(4,128)S(1)}, u32[]{:S(2)}, u32[]{:S(2)}) collective-permute-start(f32[4,576]{1,0:T(4,128)S(1)} %constant_dynamic-update-slice_fusion), channel_id=1, source_target_pairs={{8,0},{12,4},{16,8},{20,12},{24,16},{28,20},{0,24},{4,28},{9,1},{1... | collective-permute-start | bytes 27656 | tf_op jit(solution)/shard_map/ppermute | solution.py:209
  14.5 3.7 %collective-permute-start.2 = (f32[4,576]{1,0:T(4,128)S(1)}, f32[4,576]{1,0:T(4,128)S(1)}, u32[]{:S(2)}, u32[]{:S(2)}) collective-permute-start(f32[4,576]{1,0:T(4,128)S(1)} %constant_dynamic-update-slice_fusion), channel_id=1, source_target_pairs={{4,0},{8,4},{12,8},{16,12},{20,16},{24,20},{28,24},{0,28},{5,1},{9... | collective-permute-start | bytes 27656 | tf_op jit(solution)/shard_map/ppermute | solution.py:209
  18.8 5.7 %collective-permute-start.5 = (f32[16,576]{1,0:T(8,128)}, f32[16,576]{1,0:T(8,128)}, u32[]{:S(2)}, u32[]{:S(2)}) collective-permute-start(f32[16,576]{1,0:T(8,128)} %pad_maximum_fusion.1), channel_id=1, source_target_pairs={{16,0},{20,4},{24,8},{28,12},{0,16},{4,20},{8,24},{12,28},{17,1},{... | collective-permute-start | bytes 110600 | tf_op jit(solution)/shard_map/ppermute | solution.py:209
  28.8 2.4 %copy-start = (bf16[2,160,4224]{2,1,0:T(8,128)(2,1)}, bf16[2,160,4224]{2,1,0:T(8,128)(2,1)S(1)}, u32[]{:S(2)}) copy-start(bf16[2,160,4224]{2,1,0:T(8,128)(2,1)S(1)} %pad_maximum_fusion) | copy-start | bytes 8110084
  31.2 8.3 %copy-start.2 = (f32[32,576]{1,0:T(8,128)S(1)}, f32[32,576]{1,0:T(8,128)}, u32[]{:S(2)}) copy-start(f32[32,576]{1,0:T(8,128)} %concatenate.16) | copy-start | bytes 221188
  31.2 8.4 %slice-start = ((f32[32,576]{1,0:T(8,128)}), f32[32,512]{1,0:T(8,128)S(1)}, s32[]{:S(2)}) async-start(f32[32,576]{1,0:T(8,128)} %concatenate.16), calls=%async_computation | async-start | bytes 131072 | tf_op jit(solution)/shard_map/slice | solution.py:246

commit v7 on v6

--- a/solution.py
+++ b/solution.py
@@ -85,7 +85,7 @@
 
 def joining_kernel(
     corner_ref, taps_ref, prior_ref, depth_ref, window_ref, joined_ref, mean_ref,
-    total_ref, weighted_ref, placed_ref, *, n_out, n_in, block_count, bounds, crop,
+    total_ref, weighted_ref, placed_ref, *, n_out, n_in, block_count, bounds, crop, starts,
 ):
     step = pl.program_id(0)
 
@@ -95,7 +95,7 @@
         weighted_ref[...] = jnp.zeros(weighted_ref.shape, jnp.float32)
         placed_ref[...] = jnp.zeros(placed_ref.shape, jnp.float32)
 
-    skewed, across = across_planes(taps_ref, window_ref, n_out, n_in, (0, n_in))
+    skewed, across = across_planes(taps_ref, window_ref, n_out, n_in, starts)
     height, width = n_out, block_count * LANE
     row_at = corner_ref[0] + lax.broadcasted_iota(jnp.int32, (height, width), 0)
     col_at = corner_ref[1] + lax.broadcasted_iota(jnp.int32, (height, width), 1)
@@ -161,15 +161,16 @@
     )(taps, stacked)
 
 
-def joining(corner, taps, prior, depth_values, window, n_out, bounds, crop, out_shape):
+def joining(corner, taps, prior, depth_values, window, n_out, first_row, bounds, crop, out_shape):
     planes = taps.shape[0]
     group = 16 if planes % 16 == 0 else planes
-    _, n_in, width = window.shape
+    _, window_rows, width = window.shape
+    n_in = SPAN
     block_count = width // LANE - 1
-    stacked = window.reshape(2 * n_in, width)
+    stacked = window.reshape(2 * window_rows, width)
     body = functools.partial(
         joining_kernel, n_out=n_out, n_in=n_in, block_count=block_count, bounds=bounds,
-        crop=crop,
+        crop=crop, starts=(first_row, window_rows + first_row),
     )
     out_cols = block_count * LANE
     flops = 2 * planes * (2 * n_out * 2 * n_in * width + block_count * n_out * 4 * LANE * SPAN)
@@ -180,7 +181,7 @@
             pl.BlockSpec((group, 2, SPAN), lambda p, c: (p, 0, 0)),
             pl.BlockSpec((group, n_out, 1), lambda p, c: (p, 0, 0)),
             pl.BlockSpec((group, 1, 1), lambda p, c: (p, 0, 0)),
-            pl.BlockSpec((2 * n_in, width), lambda p, c: (0, 0)),
+            pl.BlockSpec((2 * window_rows, width), lambda p, c: (0, 0)),
         ],
         out_specs=[
             pl.BlockSpec(out_shape, lambda p, c: (0, 0)),
@@ -249,12 +250,9 @@
     lead_rows = 8
     n_out = rows + 2 * lead_rows
     first = halo - half_taps - lead_rows
-    window = extended[:, first : first + n_out + TAPS - 1, half_taps : half_taps + col_total]
-    lead = LANE // 2 + half_taps
+    lead = LANE // 2
     width = own_cols + 2 * LANE
-    window = jnp.pad(
-        window, ((0, 0), (0, SPAN - window.shape[1]), (lead, width - lead))
-    )
+    window = jnp.pad(extended, ((0, 0), (0, first + SPAN - extended.shape[1]), (lead, lead)))
     window = lax.dynamic_slice_in_dim(window, depth_at * own_cols, width, axis=2)
     corner = jnp.stack([tile_at * rows - lead_rows, depth_at * own_cols - LANE // 2]).astype(
         jnp.int32
@@ -263,7 +261,7 @@
     prior_rows = jnp.pad(prior_weight, ((0, 0), (lead_rows, lead_rows)), constant_values=1.0)
     depth_values = ((plane_at.astype(jnp.float32) + 0.5) / planes_total)[:, None, None]
     joined, mean_depth = joining(
-        corner, taps_all, prior_rows[:, :, None], depth_values, window, n_out,
+        corner, taps_all, prior_rows[:, :, None], depth_values, window, n_out, first,
         (row_total, col_total), (lead_rows, LANE // 2), (rows, own_cols),
     )
     return (plane_stack, joined, mean_depth)

time: 64.6 us -> 59.9 us (0.927)
  local copies, waits for them, and re-layouts: 12.9 us -> 7.09 us
    concatenate x1, local copies, waits for them, and re-layouts: 2.64 us -> 0.04 us  [gather_depth(): block = jnp.concatenate([block, *moved], axis=0)]
    slice x1 -> x0, local copies, waits for them, and re-layouts: 2.38 us -> none  [local(): extended[:, first:first + n_out + TAPS - 1, half_taps:half_taps + col_total]]
    concatenate x1, other arithmetic: 1.67 us -> 2.86 us  [local(): extended = jnp.concatenate([above, padded, below], axis=1)]
    slice x1, local copies, waits for them, and re-layouts: 2.03 us -> 3.19 us  [local(): padded[:, rows - halo:]]
    pad x1, local copies, waits for them, and re-layouts: 1.36 us -> 0.37 us  [local(): padded = jnp.pad(hologram, ((0, 0), (0, 0), (half_taps, LANE - half_taps)))]
    dynamic_slice x1, local copies, waits for them, and re-layouts: 2.14 us -> 1.16 us  [local(): lax.dynamic_slice_in_dim(window, depth_at * own_cols, width, axis=2)]
  transfers between devices with their start and end apart: 6 -> 6, of which waited for: 3 -> 3; matrix products, arithmetic and copies ran while one was open for 11% -> 5% of each run, Pallas kernels for 0% -> 0%
where the time goes in v7:
time: 59.9 us; the launch traced here: 59.6 us
  Pallas kernels  28.5 us (48%)
  starting transfers between devices  12.8 us (21%)
  local copies, waits for them, and re-layouts  7.09 us (12%)
  other arithmetic  5.48 us (9%)
  waiting for transfers between devices  5.13 us (9%)
  between operations  0.71 us (1%)
    pallas_call x1, Pallas kernels, joining(): pl.pallas_call(body, grid_spec=grid_spec, out_shape=[jax.ShapeDtypeStruct...  20.2 us
    pallas_call x1, Pallas kernels, propagate(): pl.pallas_call(body, grid=(planes,), in_specs=[pl.BlockSpec((1, 2, SPAN),...  8.29 us
    ppermute x4, starting transfers between devices, gather_depth(): lax.ppermute(block, 'depth', [((j + have * m) % count, j) for j in range(...  7.21 us
    ppermute x4, waiting for transfers between devices, gather_depth(): lax.ppermute(block, 'depth', [((j + have * m) % count, j) for j in range(...  5.12 us
    ppermute x1, starting transfers between devices, local(): lax.ppermute(padded[:, :halo], 'tile', [(i + 1, i) for i in range(tile_co...  3.64 us
    slice x1, local copies, waits for them, and re-layouts, local(): padded[:, rows - halo:]  3.19 us
    concatenate x1, other arithmetic, local(): extended = jnp.concatenate([above, padded, below], axis=1)  2.86 us
    ppermute x1, starting transfers between devices, local(): lax.ppermute(padded[:, rows - halo:], 'tile', [(i, i + 1) for i in range(...  1.91 us
  transfers between devices with their start and end apart: 6, of which 3 were waited for; matrix products, arithmetic and copies ran while one was open for 5% of the time, Pallas kernels for 0%

profile of v7, /device:TPU:4, one launch (start us, length us, event | category | flops | bytes accessed | tf_op | source)
XLA Modules:
  0.0 59.6 jit_solution(7118525346814571013)
XLA Ops:
  0.6 3.2 %pad_slice_fusion.1 = (bf16[2,48,4224]{2,1,0:T(8,128)(2,1)}, bf16[2,48,4224]{2,1,0:T(8,128)(2,1)}) fusion(bf16[2,64,4096]{2,1,0:T(8,128)(2,1)} %param.3), kind=kLoop, calls=%fused_computation.27 | loop fusion | bytes 2670592 | tf_op jit(solution)/shard_map/slice | solution.py:240
  3.8 1.9 %collective-permute-start = (bf16[2,48,4224]{2,1,0:T(8,128)(2,1)}, bf16[2,48,4224]{2,1,0:T(8,128)(2,1)S(1)}, u32[]{:S(2)}, u32[]{:S(2)}) collective-permute-start(bf16[2,48,4224]{2,1,0:T(8,128)(2,1)} %get-tuple-element.11), channel_id=1, source_target_pairs={{0,1},{1,2},{2,3},{4,5},{5,6},{6,7},{8,9},{9,10},{10,11},{12,13},{... | collective-permute-start | bytes 2433032 | tf_op jit(solution)/shard_map/ppermute | solution.py:239
  5.8 3.6 %collective-permute-start.1 = (bf16[2,48,4224]{2,1,0:T(8,128)(2,1)}, bf16[2,48,4224]{2,1,0:T(8,128)(2,1)}, u32[]{:S(2)}, u32[]{:S(2)}) collective-permute-start(bf16[2,48,4224]{2,1,0:T(8,128)(2,1)} %get-tuple-element.12), channel_id=1, source_target_pairs={{1,0},{2,1},{3,2},{5,4},{6,5},{7,6},{9,8},{10,9},{11,10},{13,12},{... | collective-permute-start | bytes 2433032 | tf_op jit(solution)/shard_map/ppermute | solution.py:242
  9.4 1.3 %fusion.7 = (f32[1,4,2,256]{3,2,1,0:T(2,128)S(1)}, f32[4,2,256]{2,1,0:T(2,128)}) fusion(bf16[4,2,64]{2,1,0:T(2,128)(2,1)} %param.4), kind=kLoop, calls=%fused_computation.24 | loop fusion | flops 2048 | bytes 17408
  10.7 3.6 %collective-permute-start.4 = (f32[4,576]{1,0:T(4,128)S(1)}, f32[4,576]{1,0:T(4,128)S(1)}, u32[]{:S(2)}, u32[]{:S(2)}) collective-permute-start(f32[4,576]{1,0:T(4,128)S(1)} %constant_dynamic-update-slice_fusion), channel_id=1, source_target_pairs={{12,0},{16,4},{20,8},{24,12},{28,16},{0,20},{4,24},{8,28},{13,1},{... | collective-permute-start | bytes 27656 | tf_op jit(solution)/shard_map/ppermute | solution.py:210
  14.3 1.3 %collective-permute-start.3 = (f32[4,576]{1,0:T(4,128)S(1)}, f32[4,576]{1,0:T(4,128)S(1)}, u32[]{:S(2)}, u32[]{:S(2)}) collective-permute-start(f32[4,576]{1,0:T(4,128)S(1)} %constant_dynamic-update-slice_fusion), channel_id=1, source_target_pairs={{8,0},{12,4},{16,8},{20,12},{24,16},{28,20},{0,24},{4,28},{9,1},{1... | collective-permute-start | bytes 27656 | tf_op jit(solution)/shard_map/ppermute | solution.py:210
  15.6 0.5 collective-permute-start.2
  16.2 0.6 %fusion.3.depth_ref = f32[32,1,1]{2,1,0:T(1,128)} fusion(s32[]{:T(128)S(6)} %axis_index.25), kind=kLoop, calls=%fused_computation.14 | loop fusion | flops 928 | bytes 132 | tf_op jit(solution)/shard_map/div | solution.py:262
  16.8 0.0 collective-permute-done.4
  16.8 1.2 %collective-permute-done.3 = f32[4,576]{1,0:T(4,128)S(1)} collective-permute-done((f32[4,576]{1,0:T(4,128)S(1)}, f32[4,576]{1,0:T(4,128)S(1)}, u32[]{:S(2)}, u32[]{:S(2)}) %collective-permute-start.3) | collective-permute-done | bytes 9248 | tf_op jit(solution)/shard_map/ppermute | solution.py:210
  18.0 1.3 %collective-permute-done.2 = f32[4,576]{1,0:T(4,128)S(1)} collective-permute-done((f32[4,576]{1,0:T(4,128)S(1)}, f32[4,576]{1,0:T(4,128)S(1)}, u32[]{:S(2)}, u32[]{:S(2)}) %collective-permute-start.2) | collective-permute-done | bytes 9248 | tf_op jit(solution)/shard_map/ppermute | solution.py:210
  19.3 1.8 %collective-permute-start.5 = (f32[16,576]{1,0:T(8,128)S(1)}, f32[16,576]{1,0:T(8,128)S(1)}, u32[]{:S(2)}, u32[]{:S(2)}) collective-permute-start(f32[16,576]{1,0:T(8,128)S(1)} %pad_maximum_fusion.1), channel_id=1, source_target_pairs={{16,0},{20,4},{24,8},{28,12},{0,16},{4,20},{8,24},{12,28},{17,1},{... | collective-permute-start | bytes 110600 | tf_op jit(solution)/shard_map/ppermute | solution.py:210
  21.1 0.7 %pad_add_fusion.corner_ref = s32[2]{0:T(128)} fusion(s32[1]{0:T(128)} %bitcast.2, s32[1]{0:T(128)} %bitcast.1), kind=kLoop, calls=%fused_computation.25 | loop fusion | flops 2 | bytes 16 | tf_op jit(solution)/shard_map/stack | solution.py:257
  21.7 0.4 pad.20
  22.1 2.6 %collective-permute-done.5 = f32[16,576]{1,0:T(8,128)S(1)} collective-permute-done((f32[16,576]{1,0:T(8,128)S(1)}, f32[16,576]{1,0:T(8,128)S(1)}, u32[]{:S(2)}, u32[]{:S(2)}) %collective-permute-start.5) | collective-permute-done | bytes 36896 | tf_op jit(solution)/shard_map/ppermute | solution.py:210
  24.8 0.0 collective-permute-done
  24.8 0.0 collective-permute-done.1
  24.8 2.9 %pad_maximum_fusion = bf16[2,160,4224]{2,1,0:T(8,128)(2,1)} fusion(bf16[2,48,4224]{2,1,0:T(8,128)(2,1)} %collective-permute-done.1, bf16[2,64,4224]{2,1,0:T(8,128)(2,1)S(1)} %pad.20, bf16[2,48,4224]{2,1,0:T(8,128)(2,1)S(1)} %collective-permute-done), kind=kLoop, calls=%fused_computation.1 | loop fusion | flops 8110080 | bytes 5406720 | tf_op jit(solution)/shard_map/concatenate | solution.py:243
  27.7 8.3 %shard_map.58 = f32[4,64,4096]{2,1,0:T(8,128)} custom-call(f32[4,2,256]{2,1,0:T(2,128)} %get-tuple-element.14.taps_ref, bf16[320,4224]{1,0:T(8,128)(2,1)} %bitcast.9), custom_call_target="tpu_custom_call" | custom-call | flops 3254779904 | bytes 6897664 | tf_op jit(solution)/shard_map/pallas_call | solution.py:147
  36.0 1.2 %pad_dynamic-slice_fusion = bf16[2,264,768]{2,1,0:T(8,128)(2,1)} fusion(s32[]{:T(128)S(6)} %select_n.43, bf16[2,160,4224]{2,1,0:T(8,128)(2,1)S(1)} %copy-done), kind=kLoop, calls=%fused_computation | loop fusion | bytes 3514372 | tf_op jit(solution)/shard_map/dynamic_slice | solution.py:256
  37.2 0.7 %reshape.122.taps_ref = f32[32,2,256]{2,1,0:T(2,128)} reshape(f32[32,512]{1,0:T(8,128)S(1)} %slice.14) | data formatting | bytes 131072 | tf_op jit(solution)/shard_map/reshape | solution.py:247
  37.8 0.1 pad_bitcast_fusion
  37.9 1.6 %copy.7.prior_ref = f32[32,80,1]{2,1,0:T(8,128)} copy(f32[32,80,1]{1,0,2:T(8,128)S(1)} %pad_bitcast_fusion) | data formatting | bytes 20480 | tf_op jit(solution)/shard_map/broadcast_in_dim | solution.py:264
  39.4 20.2 %shard_map.59 = (f32[64,512]{1,0:T(8,128)}, f32[64,512]{1,0:T(8,128)}) custom-call(s32[2]{0:T(128)} %pad_add_fusion.corner_ref, f32[32,2,256]{2,1,0:T(2,128)} %reshape.122.taps_ref, f32[32,80,1]{2,1,0:T(8,128)} %copy.7.prior_ref, f32[32,1,1]{2,1,0:T(1,128)} %fusion.3.depth_ref, bf16[528,768]{1,0:T(8,128)(2,1)} %bitcast.10), custom_call_target="tpu_custom_call" | custom-call | flops 7381975040 | bytes 1220608 | tf_op jit(solution)/shard_map/pallas_call | solution.py:192
  (14 shorter events, 0.1 us)
Async XLA Ops:
  0.6 21.1 %copy-start.1 = (bf16[2,64,4096]{2,1,0:T(8,128)(2,1)S(1)}, bf16[2,64,4096]{2,1,0:T(8,128)(2,1)}, u32[]{:S(2)}) copy-start(bf16[2,64,4096]{2,1,0:T(8,128)(2,1)} %param.3) | copy-start | bytes 3145732
  0.6 10.1 %copy-start.2 = (f32[4,64]{1,0:T(4,128)S(1)}, f32[4,64]{1,0:T(4,128)}, u32[]{:S(2)}) copy-start(f32[4,64]{1,0:T(4,128)} %param.5) | copy-start | bytes 3076
  3.8 20.9 %collective-permute-start = (bf16[2,48,4224]{2,1,0:T(8,128)(2,1)}, bf16[2,48,4224]{2,1,0:T(8,128)(2,1)S(1)}, u32[]{:S(2)}, u32[]{:S(2)}) collective-permute-start(bf16[2,48,4224]{2,1,0:T(8,128)(2,1)} %get-tuple-element.11), channel_id=1, source_target_pairs={{0,1},{1,2},{2,3},{4,5},{5,6},{6,7},{8,9},{9,10},{10,11},{12,13},{... | collective-permute-start | bytes 2433032 | tf_op jit(solution)/shard_map/ppermute | solution.py:239
  5.8 19.0 %collective-permute-start.1 = (bf16[2,48,4224]{2,1,0:T(8,128)(2,1)}, bf16[2,48,4224]{2,1,0:T(8,128)(2,1)}, u32[]{:S(2)}, u32[]{:S(2)}) collective-permute-start(bf16[2,48,4224]{2,1,0:T(8,128)(2,1)} %get-tuple-element.12), channel_id=1, source_target_pairs={{1,0},{2,1},{3,2},{5,4},{6,5},{7,6},{9,8},{10,9},{11,10},{13,12},{... | collective-permute-start | bytes 2433032 | tf_op jit(solution)/shard_map/ppermute | solution.py:242
  10.7 6.1 %collective-permute-start.4 = (f32[4,576]{1,0:T(4,128)S(1)}, f32[4,576]{1,0:T(4,128)S(1)}, u32[]{:S(2)}, u32[]{:S(2)}) collective-permute-start(f32[4,576]{1,0:T(4,128)S(1)} %constant_dynamic-update-slice_fusion), channel_id=1, source_target_pairs={{12,0},{16,4},{20,8},{24,12},{28,16},{0,20},{4,24},{8,28},{13,1},{... | collective-permute-start | bytes 27656 | tf_op jit(solution)/shard_map/ppermute | solution.py:210
  14.3 3.7 %collective-permute-start.3 = (f32[4,576]{1,0:T(4,128)S(1)}, f32[4,576]{1,0:T(4,128)S(1)}, u32[]{:S(2)}, u32[]{:S(2)}) collective-permute-start(f32[4,576]{1,0:T(4,128)S(1)} %constant_dynamic-update-slice_fusion), channel_id=1, source_target_pairs={{8,0},{12,4},{16,8},{20,12},{24,16},{28,20},{0,24},{4,28},{9,1},{1... | collective-permute-start | bytes 27656 | tf_op jit(solution)/shard_map/ppermute | solution.py:210
  15.6 3.7 %collective-permute-start.2 = (f32[4,576]{1,0:T(4,128)S(1)}, f32[4,576]{1,0:T(4,128)S(1)}, u32[]{:S(2)}, u32[]{:S(2)}) collective-permute-start(f32[4,576]{1,0:T(4,128)S(1)} %constant_dynamic-update-slice_fusion), channel_id=1, source_target_pairs={{4,0},{8,4},{12,8},{16,12},{20,16},{24,20},{28,24},{0,28},{5,1},{9... | collective-permute-start | bytes 27656 | tf_op jit(solution)/shard_map/ppermute | solution.py:210
  19.3 5.4 %collective-permute-start.5 = (f32[16,576]{1,0:T(8,128)S(1)}, f32[16,576]{1,0:T(8,128)S(1)}, u32[]{:S(2)}, u32[]{:S(2)}) collective-permute-start(f32[16,576]{1,0:T(8,128)S(1)} %pad_maximum_fusion.1), channel_id=1, source_target_pairs={{16,0},{20,4},{24,8},{28,12},{0,16},{4,20},{8,24},{12,28},{17,1},{... | collective-permute-start | bytes 110600 | tf_op jit(solution)/shard_map/ppermute | solution.py:210
  27.7 8.3 %copy-start = (bf16[2,160,4224]{2,1,0:T(8,128)(2,1)S(1)}, bf16[2,160,4224]{2,1,0:T(8,128)(2,1)}, u32[]{:S(2)}) copy-start(bf16[2,160,4224]{2,1,0:T(8,128)(2,1)} %pad_maximum_fusion) | copy-start | bytes 8110084

commit v8 on v7

--- a/solution.py
+++ b/solution.py
@@ -204,16 +204,9 @@
 
 def gather_depth(block):
     count = lax.axis_size("depth")
-    have = 1
-    while have < count:
-        moved = [
-            lax.ppermute(block, "depth", [((j + have * m) % count, j) for j in range(count)])
-            for m in range(1, 4)
-            if have * m < count
-        ]
-        block = jnp.concatenate([block, *moved], axis=0)
-        have *= 1 + len(moved)
-    return block[: count * (block.shape[0] // have)]
+    copies = jnp.broadcast_to(block[None], (count,) + block.shape)
+    moved = lax.all_to_all(copies, "depth", 0, 0)
+    return moved.reshape(count * block.shape[0], block.shape[1])
 
 
 def local(hologram, kernel, depth_prior):
@@ -231,8 +224,7 @@
     taps = jnp.pad(kernel.astype(jnp.float32), ((0, 0), (0, 0), (0, SPAN - TAPS)))
     packed = jnp.concatenate([taps.reshape(local_planes, 2 * SPAN), depth_prior], axis=1)
     packed_all = gather_depth(packed)
-    owner = (depth_at + jnp.arange(planes_total) // local_planes) % depth_count
-    plane_at = owner * local_planes + jnp.arange(planes_total) % local_planes
+    plane_at = jnp.arange(planes_total)
 
     halo = 48
     padded = jnp.pad(hologram, ((0, 0), (0, 0), (half_taps, LANE - half_taps)))

time: 59.9 us -> 59.5 us (level)
  starting transfers between devices: 12.8 us -> 11.4 us
  local copies, waits for them, and re-layouts: 7.09 us -> 7.8 us
    ppermute x4 -> x0, starting transfers between devices: 7.21 us -> none  [gather_depth(): lax.ppermute(block, 'depth', [((j + have * m) % count, j) for j in range(...]
    all_to_all x0 -> x1, starting transfers between devices: none -> 5.81 us  [gather_depth(): moved = lax.all_to_all(copies, 'depth', 0, 0)]
    all_to_all x0 -> x1, waiting for transfers between devices: none -> 5.33 us  [gather_depth(): moved = lax.all_to_all(copies, 'depth', 0, 0)]
    ppermute x4 -> x0, waiting for transfers between devices: 5.12 us -> none  [gather_depth(): lax.ppermute(block, 'depth', [((j + have * m) % count, j) for j in range(...]
    broadcast_in_dim x0 -> x1, local copies, waits for them, and re-layouts: none -> 0.65 us  [gather_depth(): copies = jnp.broadcast_to(block[None], (count,) + block.shape)]
  transfers between devices with their start and end apart: 6 -> 3, of which waited for: 3 -> 1; matrix products, arithmetic and copies ran while one was open for 5% -> 6% of each run, Pallas kernels for 0% -> 0%
where the time goes in v8:
time: 59.5 us; the launch traced here: 59.1 us
  Pallas kernels  28.5 us (48%)
  starting transfers between devices  11.4 us (19%)
  local copies, waits for them, and re-layouts  7.8 us (13%)
  other arithmetic  5.4 us (9%)
  waiting for transfers between devices  5.34 us (9%)
  between operations  0.71 us (1%)
    pallas_call x1, Pallas kernels, joining(): pl.pallas_call(body, grid_spec=grid_spec, out_shape=[jax.ShapeDtypeStruct...  20.2 us
    pallas_call x1, Pallas kernels, propagate(): pl.pallas_call(body, grid=(planes,), in_specs=[pl.BlockSpec((1, 2, SPAN),...  8.29 us
    all_to_all x1, starting transfers between devices, gather_depth(): moved = lax.all_to_all(copies, 'depth', 0, 0)  5.81 us
    all_to_all x1, waiting for transfers between devices, gather_depth(): moved = lax.all_to_all(copies, 'depth', 0, 0)  5.33 us
    ppermute x1, starting transfers between devices, local(): lax.ppermute(padded[:, :halo], 'tile', [(i + 1, i) for i in range(tile_co...  3.64 us
    slice x1, local copies, waits for them, and re-layouts, local(): padded[:, rows - halo:]  3.18 us
    concatenate x1, other arithmetic, local(): extended = jnp.concatenate([above, padded, below], axis=1)  2.87 us
    ppermute x1, starting transfers between devices, local(): lax.ppermute(padded[:, rows - halo:], 'tile', [(i, i + 1) for i in range(...  1.91 us
  transfers between devices with their start and end apart: 3, of which 1 were waited for; matrix products, arithmetic and copies ran while one was open for 6% of the time, Pallas kernels for 0%

profile of v8, /device:TPU:4, one launch (start us, length us, event | category | flops | bytes accessed | tf_op | source)
XLA Modules:
  0.0 59.1 jit_solution(14749833188891221632)
XLA Ops:
  0.6 0.0 copy-start.1
  0.6 0.0 copy-start.2
  0.6 3.2 %pad_slice_fusion.1 = (bf16[2,48,4224]{2,1,0:T(8,128)(2,1)}, bf16[2,48,4224]{2,1,0:T(8,128)(2,1)}) fusion(bf16[2,64,4096]{2,1,0:T(8,128)(2,1)} %param.3), kind=kLoop, calls=%fused_computation.12 | loop fusion | bytes 2670592 | tf_op jit(solution)/shard_map/slice | solution.py:232
  3.8 1.9 %collective-permute-start = (bf16[2,48,4224]{2,1,0:T(8,128)(2,1)}, bf16[2,48,4224]{2,1,0:T(8,128)(2,1)S(1)}, u32[]{:S(2)}, u32[]{:S(2)}) collective-permute-start(bf16[2,48,4224]{2,1,0:T(8,128)(2,1)} %get-tuple-element.11), channel_id=1, source_target_pairs={{0,1},{1,2},{2,3},{4,5},{5,6},{6,7},{8,9},{9,10},{10,11},{12,13},{... | collective-permute-start | bytes 2433032 | tf_op jit(solution)/shard_map/ppermute | solution.py:231
  5.7 3.6 %collective-permute-start.1 = (bf16[2,48,4224]{2,1,0:T(8,128)(2,1)}, bf16[2,48,4224]{2,1,0:T(8,128)(2,1)}, u32[]{:S(2)}, u32[]{:S(2)}) collective-permute-start(bf16[2,48,4224]{2,1,0:T(8,128)(2,1)} %get-tuple-element.12), channel_id=1, source_target_pairs={{1,0},{2,1},{3,2},{5,4},{6,5},{7,6},{9,8},{10,9},{11,10},{13,12},{... | collective-permute-start | bytes 2433032 | tf_op jit(solution)/shard_map/ppermute | solution.py:234
  9.4 1.3 %fusion = (f32[1,4,2,256]{3,2,1,0:T(2,128)S(1)}, f32[4,2,256]{2,1,0:T(2,128)}) fusion(bf16[4,2,64]{2,1,0:T(2,128)(2,1)} %param.4), kind=kLoop, calls=%fused_computation.8 | loop fusion | flops 2048 | bytes 17408
  10.7 0.0 copy-done.2
  10.7 0.6 %broadcast_in_dim.4 = f32[8,4,576]{2,1,0:T(4,128)} broadcast(f32[4,576]{1,0:T(4,128)S(1)} %pad_maximum_fusion.1), dimensions={1,2} | broadcast | bytes 82944 | tf_op jit(solution)/shard_map/broadcast_in_dim | solution.py:207
  11.3 5.8 %all-to-all-start = ((f32[8,4,576]{2,1,0:T(4,128)}), f32[8,4,576]{2,1,0:T(4,128)S(1)}, u32[]{:S(2)}, u32[]{:S(2)}) async-start(f32[8,4,576]{2,1,0:T(4,128)} %broadcast_in_dim.4), calls=%async_computation | async-start | bytes 163840 | tf_op jit(solution)/shard_map/all_to_all | solution.py:208
  17.2 0.1 copy.8
  17.3 0.6 %broadcast_multiply_fusion.depth_ref = f32[32,1,1]{2,1,0:T(1,128)} fusion(f32[32,1,1]{2,1,0:T(1,128)S(1)} %copy.8), kind=kLoop, calls=%fused_computation.6 | loop fusion | flops 32 | bytes 256 | tf_op jit(solution)/shard_map/div | solution.py:254
  17.9 0.0 copy-done.1
  17.9 0.4 pad.20
  18.2 0.6 pad_add_fusion.corner_ref
  18.8 5.3 %all-to-all-done = f32[8,4,576]{2,1,0:T(4,128)S(1)} async-done(((f32[8,4,576]{2,1,0:T(4,128)}), f32[8,4,576]{2,1,0:T(4,128)S(1)}, u32[]{:S(2)}, u32[]{:S(2)}) %all-to-all-start) | async-done | bytes 73760 | tf_op jit(solution)/shard_map/all_to_all | solution.py:208
  24.2 0.0 collective-permute-done
  24.2 0.0 collective-permute-done.1
  24.2 2.9 %pad_maximum_fusion = bf16[2,160,4224]{2,1,0:T(8,128)(2,1)} fusion(bf16[2,48,4224]{2,1,0:T(8,128)(2,1)} %collective-permute-done.1, bf16[2,64,4224]{2,1,0:T(8,128)(2,1)S(1)} %pad.20, bf16[2,48,4224]{2,1,0:T(8,128)(2,1)S(1)} %collective-permute-done), kind=kLoop, calls=%fused_computation.1 | loop fusion | flops 8110080 | bytes 5406720 | tf_op jit(solution)/shard_map/concatenate | solution.py:235
  27.1 8.3 %shard_map.58 = f32[4,64,4096]{2,1,0:T(8,128)} custom-call(f32[4,2,256]{2,1,0:T(2,128)} %get-tuple-element.14.taps_ref, bf16[320,4224]{1,0:T(8,128)(2,1)} %bitcast.9), custom_call_target="tpu_custom_call" | custom-call | flops 3254779904 | bytes 6897664 | tf_op jit(solution)/shard_map/pallas_call | solution.py:147
  35.4 1.2 %pad_dynamic-slice_fusion = bf16[2,264,768]{2,1,0:T(8,128)(2,1)} fusion(s32[]{:T(128)S(6)} %select_n.3, bf16[2,160,4224]{2,1,0:T(8,128)(2,1)S(1)} %copy-done), kind=kLoop, calls=%fused_computation | loop fusion | bytes 3514372 | tf_op jit(solution)/shard_map/dynamic_slice | solution.py:248
  36.6 0.7 %reshape.39.taps_ref = f32[32,2,256]{2,1,0:T(2,128)} reshape(f32[32,512]{1,0:T(8,128)S(1)} %slice.14) | data formatting | bytes 131072 | tf_op jit(solution)/shard_map/reshape | solution.py:239
  37.3 0.1 pad_bitcast_fusion
  37.3 1.5 %copy.9.prior_ref = f32[32,80,1]{2,1,0:T(8,128)} copy(f32[32,80,1]{1,0,2:T(8,128)S(1)} %pad_bitcast_fusion) | data formatting | bytes 20480 | tf_op jit(solution)/shard_map/broadcast_in_dim | solution.py:256
  38.9 20.2 %shard_map.59 = (f32[64,512]{1,0:T(8,128)}, f32[64,512]{1,0:T(8,128)}) custom-call(s32[2]{0:T(128)} %pad_add_fusion.corner_ref, f32[32,2,256]{2,1,0:T(2,128)} %reshape.39.taps_ref, f32[32,80,1]{2,1,0:T(8,128)} %copy.9.prior_ref, f32[32,1,1]{2,1,0:T(1,128)} %broadcast_multiply_fusion.depth_ref, bf16[528,768]{1,0:T(8,128)(2,1)} %bitcast.10), custom_call_target="tpu_custom_call" | custom-call | flops 7381975040 | bytes 1220608 | tf_op jit(solution)/shard_map/pallas_call | solution.py:192
  (9 shorter events, 0.1 us)
Async XLA Ops:
  0.6 17.2 %copy-start.1 = (bf16[2,64,4096]{2,1,0:T(8,128)(2,1)S(1)}, bf16[2,64,4096]{2,1,0:T(8,128)(2,1)}, u32[]{:S(2)}) copy-start(bf16[2,64,4096]{2,1,0:T(8,128)(2,1)} %param.3) | copy-start | bytes 3145732
  0.6 10.1 %copy-start.2 = (f32[4,64]{1,0:T(4,128)S(1)}, f32[4,64]{1,0:T(4,128)}, u32[]{:S(2)}) copy-start(f32[4,64]{1,0:T(4,128)} %param.5) | copy-start | bytes 3076
  3.8 20.4 %collective-permute-start = (bf16[2,48,4224]{2,1,0:T(8,128)(2,1)}, bf16[2,48,4224]{2,1,0:T(8,128)(2,1)S(1)}, u32[]{:S(2)}, u32[]{:S(2)}) collective-permute-start(bf16[2,48,4224]{2,1,0:T(8,128)(2,1)} %get-tuple-element.11), channel_id=1, source_target_pairs={{0,1},{1,2},{2,3},{4,5},{5,6},{6,7},{8,9},{9,10},{10,11},{12,13},{... | collective-permute-start | bytes 2433032 | tf_op jit(solution)/shard_map/ppermute | solution.py:231
  5.7 18.5 %collective-permute-start.1 = (bf16[2,48,4224]{2,1,0:T(8,128)(2,1)}, bf16[2,48,4224]{2,1,0:T(8,128)(2,1)}, u32[]{:S(2)}, u32[]{:S(2)}) collective-permute-start(bf16[2,48,4224]{2,1,0:T(8,128)(2,1)} %get-tuple-element.12), channel_id=1, source_target_pairs={{1,0},{2,1},{3,2},{5,4},{6,5},{7,6},{9,8},{10,9},{11,10},{13,12},{... | collective-permute-start | bytes 2433032 | tf_op jit(solution)/shard_map/ppermute | solution.py:234
  11.3 12.8 %all-to-all-start = ((f32[8,4,576]{2,1,0:T(4,128)}), f32[8,4,576]{2,1,0:T(4,128)S(1)}, u32[]{:S(2)}, u32[]{:S(2)}) async-start(f32[8,4,576]{2,1,0:T(4,128)} %broadcast_in_dim.4), calls=%async_computation | async-start | bytes 163840 | tf_op jit(solution)/shard_map/all_to_all | solution.py:208
  27.1 8.3 %copy-start = (bf16[2,160,4224]{2,1,0:T(8,128)(2,1)S(1)}, bf16[2,160,4224]{2,1,0:T(8,128)(2,1)}, u32[]{:S(2)}) copy-start(bf16[2,160,4224]{2,1,0:T(8,128)(2,1)} %pad_maximum_fusion) | copy-start | bytes 8110084

commit v9 on v8

--- a/solution.py
+++ b/solution.py
@@ -227,12 +227,10 @@
     plane_at = jnp.arange(planes_total)
 
     halo = 48
-    padded = jnp.pad(hologram, ((0, 0), (0, 0), (half_taps, LANE - half_taps)))
-    above = lax.ppermute(
-        padded[:, rows - halo :], "tile", [(i, i + 1) for i in range(tile_count - 1)]
-    )
-    below = lax.ppermute(padded[:, :halo], "tile", [(i + 1, i) for i in range(tile_count - 1)])
-    extended = jnp.concatenate([above, padded, below], axis=1)
+    above = lax.ppermute(hologram, "tile", [(i, i + 1) for i in range(tile_count - 1)])
+    below = lax.ppermute(hologram, "tile", [(i + 1, i) for i in range(tile_count - 1)])
+    extended = jnp.concatenate([above[:, rows - halo :], hologram, below[:, :halo]], axis=1)
+    extended = jnp.pad(extended, ((0, 0), (0, 0), (half_taps, LANE - half_taps)))
 
     plane_stack = propagate(taps, extended, rows, halo - half_taps)
     plane_stack, packed_all = lax.optimization_barrier((plane_stack, packed_all))

time: 59.5 us -> 57 us (0.958)
  local copies, waits for them, and re-layouts: 7.8 us -> 4.35 us
    slice x1 -> x2, local copies, waits for them, and re-layouts: 3.18 us -> 0.11 us  [the longest x1 0.05 us: local(): above[:, rows - halo:]]
    concatenate x1, other arithmetic: 0.01 us -> 0.69 us  [local(): jnp.concatenate([taps.reshape(local_planes, 2 * SPAN), depth_prior], axis=1)]
  transfers between devices with their start and end apart: 3 -> 3, of which waited for: 1 -> 1; matrix products, arithmetic and copies ran while one was open for 6% -> 7% of each run, Pallas kernels for 0% -> 0%
where the time goes in v9:
time: 57 us; the launch traced here: 56.6 us
  Pallas kernels  28.5 us (50%)
  starting transfers between devices  11.5 us (20%)
  other arithmetic  5.9 us (10%)
  waiting for transfers between devices  5.69 us (10%)
  local copies, waits for them, and re-layouts  4.35 us (8%)
  between operations  0.72 us (1%)
    pallas_call x1, Pallas kernels, joining(): pl.pallas_call(body, grid_spec=grid_spec, out_shape=[jax.ShapeDtypeStruct...  20.2 us
    pallas_call x1, Pallas kernels, propagate(): pl.pallas_call(body, grid=(planes,), in_specs=[pl.BlockSpec((1, 2, SPAN),...  8.29 us
    all_to_all x1, starting transfers between devices, gather_depth(): moved = lax.all_to_all(copies, 'depth', 0, 0)  5.81 us
    all_to_all x1, waiting for transfers between devices, gather_depth(): moved = lax.all_to_all(copies, 'depth', 0, 0)  5.69 us
    ppermute x1, starting transfers between devices, local(): lax.ppermute(hologram, 'tile', [(i + 1, i) for i in range(tile_count - 1)])  3.64 us
    concatenate x1, other arithmetic, local(): jnp.concatenate([above[:, rows - halo:], hologram, below[:, :halo]], axis=1)  2.67 us
    ppermute x1, starting transfers between devices, local(): lax.ppermute(hologram, 'tile', [(i, i + 1) for i in range(tile_count - 1)])  2.05 us
    broadcast_in_dim x2, local copies, waits for them, and re-layouts, local(): prior_rows[:, :, None]  1.62 us
  transfers between devices with their start and end apart: 3, of which 1 were waited for; matrix products, arithmetic and copies ran while one was open for 7% of the time, Pallas kernels for 0%

profile of v9, /device:TPU:4, one launch (start us, length us, event | category | flops | bytes accessed | tf_op | source)
XLA Modules:
  0.0 56.6 jit_solution(10363394224861525759)
XLA Ops:
  0.6 0.0 copy-start.1
  0.6 2.1 %collective-permute-start = (bf16[2,64,4096]{2,1,0:T(8,128)(2,1)}, bf16[2,64,4096]{2,1,0:T(8,128)(2,1)S(1)}, u32[]{:S(2)}, u32[]{:S(2)}) collective-permute-start(bf16[2,64,4096]{2,1,0:T(8,128)(2,1)} %param.3), channel_id=1, source_target_pairs={{0,1},{1,2},{2,3},{4,5},{5,6},{6,7},{8,9},{9,10},{10,11},{12,13},{... | collective-permute-start | bytes 3145736 | tf_op jit(solution)/shard_map/ppermute | solution.py:230
  2.7 3.6 %collective-permute-start.1 = (bf16[2,64,4096]{2,1,0:T(8,128)(2,1)}, bf16[2,64,4096]{2,1,0:T(8,128)(2,1)S(1)}, u32[]{:S(2)}, u32[]{:S(2)}) collective-permute-start(bf16[2,64,4096]{2,1,0:T(8,128)(2,1)} %param.3), channel_id=1, source_target_pairs={{1,0},{2,1},{3,2},{5,4},{6,5},{7,6},{9,8},{10,9},{11,10},{13,12},{... | collective-permute-start | bytes 3145736 | tf_op jit(solution)/shard_map/ppermute | solution.py:231
  6.3 1.3 %fusion.6 = (f32[1,4,2,256]{3,2,1,0:T(2,128)S(1)}, f32[4,2,256]{2,1,0:T(2,128)}) fusion(bf16[4,2,64]{2,1,0:T(2,128)(2,1)} %param.4), kind=kLoop, calls=%fused_computation.15 | loop fusion | flops 2048 | bytes 17408
  7.6 0.7 %pad_maximum_fusion = f32[4,576]{1,0:T(4,128)S(1)} fusion(f32[4,64]{1,0:T(4,128)} %param.5, f32[4,512]{1,0:T(4,128)S(1)} %bitcast.11), kind=kLoop, calls=%fused_computation.12 | loop fusion | flops 2304 | bytes 18432 | tf_op jit(solution)/shard_map/concatenate | solution.py:225
  8.3 0.6 %broadcast_in_dim.4 = f32[8,4,576]{2,1,0:T(4,128)} broadcast(f32[4,576]{1,0:T(4,128)S(1)} %pad_maximum_fusion), dimensions={1,2} | broadcast | bytes 82944 | tf_op jit(solution)/shard_map/broadcast_in_dim | solution.py:207
  9.0 5.8 %all-to-all-start = ((f32[8,4,576]{2,1,0:T(4,128)}), f32[8,4,576]{2,1,0:T(4,128)S(1)}, u32[]{:S(2)}, u32[]{:S(2)}) async-start(f32[8,4,576]{2,1,0:T(4,128)} %broadcast_in_dim.4), calls=%async_computation | async-start | bytes 163840 | tf_op jit(solution)/shard_map/all_to_all | solution.py:208
  14.8 0.1 copy.8
  14.9 0.6 %broadcast_multiply_fusion.depth_ref = f32[32,1,1]{2,1,0:T(1,128)} fusion(f32[32,1,1]{2,1,0:T(1,128)S(1)} %copy.8), kind=kLoop, calls=%fused_computation.13 | loop fusion | flops 32 | bytes 256 | tf_op jit(solution)/shard_map/div | solution.py:252
  15.5 0.6 %pad_add_fusion.corner_ref = s32[2]{0:T(128)} fusion(s32[1]{0:T(128)} %bitcast.2, s32[1]{0:T(128)} %bitcast.1), kind=kLoop, calls=%fused_computation.16 | loop fusion | flops 2 | bytes 16 | tf_op jit(solution)/shard_map/stack | solution.py:247
  16.1 5.7 %all-to-all-done = f32[8,4,576]{2,1,0:T(4,128)S(1)} async-done(((f32[8,4,576]{2,1,0:T(4,128)}), f32[8,4,576]{2,1,0:T(4,128)S(1)}, u32[]{:S(2)}, u32[]{:S(2)}) %all-to-all-start) | async-done | bytes 73760 | tf_op jit(solution)/shard_map/all_to_all | solution.py:208
  21.8 0.0 collective-permute-done
  21.8 0.1 slice.16
  21.9 0.0 collective-permute-done.1
  21.9 0.1 slice.17
  22.0 0.0 copy-done.1
  22.0 2.7 %fusion.5 = bf16[2,160,4224]{2,1,0:T(8,128)(2,1)} fusion(bf16[2,48,4096]{2,1,0:T(8,128)(2,1)S(1)} %slice.17, bf16[2,64,4096]{2,1,0:T(8,128)(2,1)S(1)} %copy-done.1, bf16[2,48,4096]{2,1,0:T(8,128)(2,1)S(1)} %slice.16), kind=kLoop, calls=%fused_computation.8 | loop fusion | flops 16220160 | bytes 5324800 | tf_op jit(solution)/shard_map/concatenate | solution.py:232
  24.6 8.3 %shard_map.58 = f32[4,64,4096]{2,1,0:T(8,128)} custom-call(f32[4,2,256]{2,1,0:T(2,128)} %get-tuple-element.12.taps_ref, bf16[320,4224]{1,0:T(8,128)(2,1)} %bitcast.9), custom_call_target="tpu_custom_call" | custom-call | flops 3254779904 | bytes 6897664 | tf_op jit(solution)/shard_map/pallas_call | solution.py:147
  33.0 0.0 copy-done
  33.0 1.2 %pad_dynamic-slice_fusion = bf16[2,264,768]{2,1,0:T(8,128)(2,1)} fusion(s32[]{:T(128)S(6)} %select_n.3, bf16[2,160,4224]{2,1,0:T(8,128)(2,1)S(1)} %copy-done), kind=kLoop, calls=%fused_computation.3 | loop fusion | bytes 3514372 | tf_op jit(solution)/shard_map/dynamic_slice | solution.py:246
  34.2 0.1 pad_bitcast_fusion
  34.3 1.5 %copy.9.prior_ref = f32[32,80,1]{2,1,0:T(8,128)} copy(f32[32,80,1]{1,0,2:T(8,128)S(1)} %pad_bitcast_fusion) | data formatting | bytes 20480 | tf_op jit(solution)/shard_map/broadcast_in_dim | solution.py:254
  35.8 0.7 %reshape.39.taps_ref = f32[32,2,256]{2,1,0:T(2,128)} reshape(f32[32,512]{1,0:T(8,128)S(1)} %slice.14) | data formatting | bytes 131072 | tf_op jit(solution)/shard_map/reshape | solution.py:237
  36.5 20.2 %shard_map.59 = (f32[64,512]{1,0:T(8,128)}, f32[64,512]{1,0:T(8,128)}) custom-call(s32[2]{0:T(128)} %pad_add_fusion.corner_ref, f32[32,2,256]{2,1,0:T(2,128)} %reshape.39.taps_ref, f32[32,80,1]{2,1,0:T(8,128)} %copy.9.prior_ref, f32[32,1,1]{2,1,0:T(1,128)} %broadcast_multiply_fusion.depth_ref, bf16[528,768]{1,0:T(8,128)(2,1)} %bitcast.10), custom_call_target="tpu_custom_call" | custom-call | flops 7381975040 | bytes 1220608 | tf_op jit(solution)/shard_map/pallas_call | solution.py:192
  (7 shorter events, 0.1 us)
Async XLA Ops:
  0.6 21.3 %copy-start.1 = (bf16[2,64,4096]{2,1,0:T(8,128)(2,1)S(1)}, bf16[2,64,4096]{2,1,0:T(8,128)(2,1)}, u32[]{:S(2)}) copy-start(bf16[2,64,4096]{2,1,0:T(8,128)(2,1)} %param.3) | copy-start | bytes 3145732
  0.6 21.2 %collective-permute-start = (bf16[2,64,4096]{2,1,0:T(8,128)(2,1)}, bf16[2,64,4096]{2,1,0:T(8,128)(2,1)S(1)}, u32[]{:S(2)}, u32[]{:S(2)}) collective-permute-start(bf16[2,64,4096]{2,1,0:T(8,128)(2,1)} %param.3), channel_id=1, source_target_pairs={{0,1},{1,2},{2,3},{4,5},{5,6},{6,7},{8,9},{9,10},{10,11},{12,13},{... | collective-permute-start | bytes 3145736 | tf_op jit(solution)/shard_map/ppermute | solution.py:230
  2.7 19.2 %collective-permute-start.1 = (bf16[2,64,4096]{2,1,0:T(8,128)(2,1)}, bf16[2,64,4096]{2,1,0:T(8,128)(2,1)S(1)}, u32[]{:S(2)}, u32[]{:S(2)}) collective-permute-start(bf16[2,64,4096]{2,1,0:T(8,128)(2,1)} %param.3), channel_id=1, source_target_pairs={{1,0},{2,1},{3,2},{5,4},{6,5},{7,6},{9,8},{10,9},{11,10},{13,12},{... | collective-permute-start | bytes 3145736 | tf_op jit(solution)/shard_map/ppermute | solution.py:231
  9.0 12.8 %all-to-all-start = ((f32[8,4,576]{2,1,0:T(4,128)}), f32[8,4,576]{2,1,0:T(4,128)S(1)}, u32[]{:S(2)}, u32[]{:S(2)}) async-start(f32[8,4,576]{2,1,0:T(4,128)} %broadcast_in_dim.4), calls=%async_computation | async-start | bytes 163840 | tf_op jit(solution)/shard_map/all_to_all | solution.py:208
  24.6 8.3 %copy-start = (bf16[2,160,4224]{2,1,0:T(8,128)(2,1)S(1)}, bf16[2,160,4224]{2,1,0:T(8,128)(2,1)}, u32[]{:S(2)}) copy-start(bf16[2,160,4224]{2,1,0:T(8,128)(2,1)} %fusion.5) | copy-start | bytes 8110084

commit v10 on v9

--- a/solution.py
+++ b/solution.py
@@ -16,7 +16,10 @@
     def skew(taps):
         return pltpu.roll(jnp.broadcast_to(taps, (LANE, SPAN)), 0, 1, stride=1, stride_axis=0)
 
-    return skew(taps_ref[plane, 0:1, :]), skew(taps_ref[plane, 1:2, :])
+    if len(taps_ref.shape) == 3:
+        return skew(taps_ref[plane, 0:1, :]), skew(taps_ref[plane, 1:2, :])
+    row = taps_ref[plane : plane + 1]
+    return skew(row[:, :SPAN]), skew(row[:, SPAN : 2 * SPAN])
 
 
 def rows_matrix(skew_re, skew_im, n_out, n_in):
@@ -116,7 +119,7 @@
             pltpu.roll(intensity, 1, 1) + 2.0 * intensity + pltpu.roll(intensity, width - 1, 1)
         )
         grad_y = pltpu.roll(horizontal, height - 1, 0) - pltpu.roll(horizontal, 1, 0)
-        fresh = prior_ref[g] * (1.0 + (grad_x * grad_x + grad_y * grad_y))
+        fresh = prior_ref[g][:, 0:1] * (1.0 + (grad_x * grad_x + grad_y * grad_y))
         total_ref[...] = total_ref[...] + fresh
         weighted_ref[...] = weighted_ref[...] + fresh * intensity
         placed_ref[...] = placed_ref[...] + fresh * depth_ref[g]
@@ -178,8 +181,8 @@
         num_scalar_prefetch=1,
         grid=(planes // group,),
         in_specs=[
-            pl.BlockSpec((group, 2, SPAN), lambda p, c: (p, 0, 0)),
-            pl.BlockSpec((group, n_out, 1), lambda p, c: (p, 0, 0)),
+            pl.BlockSpec((group, taps.shape[1]), lambda p, c: (p, 0)),
+            pl.BlockSpec((group, n_out, LANE), lambda p, c: (p, 0, 0)),
             pl.BlockSpec((group, 1, 1), lambda p, c: (p, 0, 0)),
             pl.BlockSpec((2 * window_rows, width), lambda p, c: (0, 0)),
         ],
@@ -234,7 +237,6 @@
 
     plane_stack = propagate(taps, extended, rows, halo - half_taps)
     plane_stack, packed_all = lax.optimization_barrier((plane_stack, packed_all))
-    taps_all = packed_all[:, : 2 * SPAN].reshape(planes_total, 2, SPAN)
     prior_all = packed_all[:, 2 * SPAN :]
 
     lead_rows = 8
@@ -251,7 +253,8 @@
     prior_rows = jnp.pad(prior_weight, ((0, 0), (lead_rows, lead_rows)), constant_values=1.0)
     depth_values = ((plane_at.astype(jnp.float32) + 0.5) / planes_total)[:, None, None]
     joined, mean_depth = joining(
-        corner, taps_all, prior_rows[:, :, None], depth_values, window, n_out, first,
+        corner, packed_all, jnp.broadcast_to(prior_rows[:, :, None], prior_rows.shape + (LANE,)),
+        depth_values, window, n_out, first,
         (row_total, col_total), (lead_rows, LANE // 2), (rows, own_cols),
     )
     return (plane_stack, joined, mean_depth)

time: 57 us -> 56.6 us (level)
  other arithmetic: 5.9 us -> 4.84 us
  local copies, waits for them, and re-layouts: 4.35 us -> 5.29 us
    unnamed x5 -> x7, local copies, waits for them, and re-layouts: 0.01 us -> 1.48 us
    concatenate x1, other arithmetic: 2.67 us -> 1.57 us  [local(): jnp.concatenate([above[:, rows - halo:], hologram, below[:, :halo]], axis=1)]
    reshape x1 -> x0, local copies, waits for them, and re-layouts: 0.66 us -> none  [local(): taps_all = packed_all[:, :2 * SPAN].reshape(planes_total, 2, SPAN)]
    broadcast_in_dim x2 -> x1, local copies, waits for them, and re-layouts: 1.62 us -> 1.49 us  [local(): jnp.broadcast_to(prior_rows[:, :, None], prior_rows.shape + (LANE,))]
where the time goes in v10:
time: 56.6 us; the launch traced here: 56.2 us
  Pallas kernels  28.3 us (50%)
  starting transfers between devices  11.4 us (20%)
  waiting for transfers between devices  5.66 us (10%)
  local copies, waits for them, and re-layouts  5.29 us (9%)
  other arithmetic  4.84 us (9%)
  between operations  0.73 us (1%)
    pallas_call x1, Pallas kernels, joining(): pl.pallas_call(body, grid_spec=grid_spec, out_shape=[jax.ShapeDtypeStruct...  20.2 us
    pallas_call x1, Pallas kernels, propagate(): pl.pallas_call(body, grid=(planes,), in_specs=[pl.BlockSpec((1, 2, SPAN),...  8.14 us
    all_to_all x1, starting transfers between devices, gather_depth(): moved = lax.all_to_all(copies, 'depth', 0, 0)  5.81 us
    all_to_all x1, waiting for transfers between devices, gather_depth(): moved = lax.all_to_all(copies, 'depth', 0, 0)  5.65 us
    ppermute x1, starting transfers between devices, local(): lax.ppermute(hologram, 'tile', [(i + 1, i) for i in range(tile_count - 1)])  3.64 us
    ppermute x1, starting transfers between devices, local(): lax.ppermute(hologram, 'tile', [(i, i + 1) for i in range(tile_count - 1)])  1.92 us
    concatenate x1, other arithmetic, local(): jnp.concatenate([above[:, rows - halo:], hologram, below[:, :halo]], axis=1)  1.57 us
    broadcast_in_dim x1, local copies, waits for them, and re-layouts, local(): jnp.broadcast_to(prior_rows[:, :, None], prior_rows.shape + (LANE,))  1.49 us
  transfers between devices with their start and end apart: 3, of which 1 were waited for; matrix products, arithmetic and copies ran while one was open for 7% of the time, Pallas kernels for 0%

profile of v10, /device:TPU:4, one launch (start us, length us, event | category | flops | bytes accessed | tf_op | source)
XLA Modules:
  0.0 56.2 jit_solution(806193057099879432)
XLA Ops:
  0.6 1.9 %collective-permute-start = (bf16[2,64,4096]{2,1,0:T(8,128)(2,1)}, bf16[2,64,4096]{2,1,0:T(8,128)(2,1)S(1)}, u32[]{:S(2)}, u32[]{:S(2)}) collective-permute-start(bf16[2,64,4096]{2,1,0:T(8,128)(2,1)} %param.3), channel_id=1, source_target_pairs={{0,1},{1,2},{2,3},{4,5},{5,6},{6,7},{8,9},{9,10},{10,11},{12,13},{... | collective-permute-start | bytes 3145736 | tf_op jit(solution)/shard_map/ppermute | solution.py:233
  2.6 3.6 %collective-permute-start.1 = (bf16[2,64,4096]{2,1,0:T(8,128)(2,1)}, bf16[2,64,4096]{2,1,0:T(8,128)(2,1)S(1)}, u32[]{:S(2)}, u32[]{:S(2)}) collective-permute-start(bf16[2,64,4096]{2,1,0:T(8,128)(2,1)} %param.3), channel_id=1, source_target_pairs={{1,0},{2,1},{3,2},{5,4},{6,5},{7,6},{9,8},{10,9},{11,10},{13,12},{... | collective-permute-start | bytes 3145736 | tf_op jit(solution)/shard_map/ppermute | solution.py:234
  6.2 1.3 %fusion.6 = (f32[1,4,2,256]{3,2,1,0:T(2,128)S(1)}, f32[4,2,256]{2,1,0:T(2,128)}) fusion(bf16[4,2,64]{2,1,0:T(2,128)(2,1)} %param.4), kind=kLoop, calls=%fused_computation.14 | loop fusion | flops 2048 | bytes 17408
  7.5 0.7 %pad_maximum_fusion = f32[4,576]{1,0:T(4,128)S(1)} fusion(f32[4,64]{1,0:T(4,128)} %param.5, f32[4,512]{1,0:T(4,128)S(1)} %bitcast.9), kind=kLoop, calls=%fused_computation.11 | loop fusion | flops 2304 | bytes 18432 | tf_op jit(solution)/shard_map/concatenate | solution.py:228
  8.2 0.6 %broadcast_in_dim.4 = f32[8,4,576]{2,1,0:T(4,128)} broadcast(f32[4,576]{1,0:T(4,128)S(1)} %pad_maximum_fusion), dimensions={1,2} | broadcast | bytes 82944 | tf_op jit(solution)/shard_map/broadcast_in_dim | solution.py:210
  8.8 5.8 %all-to-all-start = ((f32[8,4,576]{2,1,0:T(4,128)}), f32[8,4,576]{2,1,0:T(4,128)S(1)}, u32[]{:S(2)}, u32[]{:S(2)}) async-start(f32[8,4,576]{2,1,0:T(4,128)} %broadcast_in_dim.4), calls=%async_computation | async-start | bytes 163840 | tf_op jit(solution)/shard_map/all_to_all | solution.py:211
  14.6 0.1 copy.7
  14.7 0.6 %broadcast_multiply_fusion.depth_ref = f32[32,1,1]{2,1,0:T(1,128)} fusion(f32[32,1,1]{2,1,0:T(1,128)S(1)} %copy.7), kind=kLoop, calls=%fused_computation.12 | loop fusion | flops 32 | bytes 256 | tf_op jit(solution)/shard_map/div | solution.py:254
  15.4 0.6 %pad_add_fusion.corner_ref = s32[2]{0:T(128)} fusion(s32[1]{0:T(128)} %bitcast.2, s32[1]{0:T(128)} %bitcast.1), kind=kLoop, calls=%fused_computation.15 | loop fusion | flops 2 | bytes 16 | tf_op jit(solution)/shard_map/stack | solution.py:249
  16.0 5.7 %all-to-all-done = f32[8,4,576]{2,1,0:T(4,128)S(1)} async-done(((f32[8,4,576]{2,1,0:T(4,128)}), f32[8,4,576]{2,1,0:T(4,128)S(1)}, u32[]{:S(2)}, u32[]{:S(2)}) %all-to-all-start) | async-done | bytes 73760 | tf_op jit(solution)/shard_map/all_to_all | solution.py:211
  21.7 0.0 copy-start.2
  21.7 0.0 copy-start.1
  21.7 0.0 collective-permute-done
  21.7 0.1 slice.12
  21.8 0.0 collective-permute-done.1
  21.8 0.1 slice.13
  21.9 1.1 %copy-done.1 = bf16[2,64,4096]{2,1,0:T(8,128)(2,1)S(1)} copy-done((bf16[2,64,4096]{2,1,0:T(8,128)(2,1)S(1)}, bf16[2,64,4096]{2,1,0:T(8,128)(2,1)}, u32[]{:S(2)}) %copy-start.1) | copy-done | bytes 1048600
  23.0 1.6 %fusion.5 = bf16[2,160,4224]{2,1,0:T(8,128)(2,1)S(1)} fusion(bf16[2,48,4096]{2,1,0:T(8,128)(2,1)S(1)} %slice.13, bf16[2,64,4096]{2,1,0:T(8,128)(2,1)S(1)} %copy-done.1, bf16[2,48,4096]{2,1,0:T(8,128)(2,1)S(1)} %slice.12), kind=kLoop, calls=%fused_computation.8 | loop fusion | flops 16220160 | bytes 5324800 | tf_op jit(solution)/shard_map/concatenate | solution.py:235
  24.5 1.4 %pad_dynamic-slice_fusion = bf16[2,264,768]{2,1,0:T(8,128)(2,1)} fusion(s32[]{:T(128)S(6)} %select_n.3, bf16[2,160,4224]{2,1,0:T(8,128)(2,1)S(1)} %fusion.5), kind=kLoop, calls=%fused_computation.3 | loop fusion | bytes 3514372 | tf_op jit(solution)/shard_map/dynamic_slice | solution.py:248
  25.9 0.4 copy-done
  26.3 8.1 %shard_map.58 = f32[4,64,4096]{2,1,0:T(8,128)} custom-call(f32[4,2,256]{2,1,0:T(2,128)} %get-tuple-element.12.taps_ref, bf16[320,4224]{1,0:T(8,128)(2,1)} %bitcast.7), custom_call_target="tpu_custom_call" | custom-call | flops 3254779904 | bytes 6897664 | tf_op jit(solution)/shard_map/pallas_call | solution.py:150
  34.5 0.1 pad.21
  34.5 1.5 %broadcast_in_dim.5.prior_ref = f32[32,80,128]{2,1,0:T(8,128)} broadcast(f32[32,80]{1,0:T(8,128)S(1)} %pad.21), dimensions={0,1} | broadcast | bytes 1320960 | tf_op jit(solution)/shard_map/broadcast_in_dim | solution.py:256
  36.0 20.2 %shard_map.59 = (f32[64,512]{1,0:T(8,128)}, f32[64,512]{1,0:T(8,128)}) custom-call(s32[2]{0:T(128)} %pad_add_fusion.corner_ref, f32[32,576]{1,0:T(8,128)} %copy-done.2, f32[32,80,128]{2,1,0:T(8,128)} %broadcast_in_dim.5.prior_ref, f32[32,1,1]{2,1,0:T(1,128)} %broadcast_multiply_fusion.depth_ref, bf16[528,768]{1,0:T(8,128)(2,1)} %bitcast.8), custom_call_target="tpu_custom_call" | custom-call | flops 7381975040 | bytes 1220608 | tf_op jit(solution)/shard_map/pallas_call | solution.py:195
  (7 shorter events, 0.1 us)
Async XLA Ops:
  0.6 21.1 %collective-permute-start = (bf16[2,64,4096]{2,1,0:T(8,128)(2,1)}, bf16[2,64,4096]{2,1,0:T(8,128)(2,1)S(1)}, u32[]{:S(2)}, u32[]{:S(2)}) collective-permute-start(bf16[2,64,4096]{2,1,0:T(8,128)(2,1)} %param.3), channel_id=1, source_target_pairs={{0,1},{1,2},{2,3},{4,5},{5,6},{6,7},{8,9},{9,10},{10,11},{12,13},{... | collective-permute-start | bytes 3145736 | tf_op jit(solution)/shard_map/ppermute | solution.py:233
  2.6 19.2 %collective-permute-start.1 = (bf16[2,64,4096]{2,1,0:T(8,128)(2,1)}, bf16[2,64,4096]{2,1,0:T(8,128)(2,1)S(1)}, u32[]{:S(2)}, u32[]{:S(2)}) collective-permute-start(bf16[2,64,4096]{2,1,0:T(8,128)(2,1)} %param.3), channel_id=1, source_target_pairs={{1,0},{2,1},{3,2},{5,4},{6,5},{7,6},{9,8},{10,9},{11,10},{13,12},{... | collective-permute-start | bytes 3145736 | tf_op jit(solution)/shard_map/ppermute | solution.py:234
  8.8 12.8 %all-to-all-start = ((f32[8,4,576]{2,1,0:T(4,128)}), f32[8,4,576]{2,1,0:T(4,128)S(1)}, u32[]{:S(2)}, u32[]{:S(2)}) async-start(f32[8,4,576]{2,1,0:T(4,128)} %broadcast_in_dim.4), calls=%async_computation | async-start | bytes 163840 | tf_op jit(solution)/shard_map/all_to_all | solution.py:211
  21.7 12.8 %copy-start.2 = (f32[32,576]{1,0:T(8,128)}, f32[32,576]{1,0:T(8,128)S(1)}, u32[]{:S(2)}) copy-start(f32[32,576]{1,0:T(8,128)S(1)} %reshape.36.taps_ref) | copy-start | bytes 221188
  21.7 1.3 %copy-start.1 = (bf16[2,64,4096]{2,1,0:T(8,128)(2,1)S(1)}, bf16[2,64,4096]{2,1,0:T(8,128)(2,1)}, u32[]{:S(2)}) copy-start(bf16[2,64,4096]{2,1,0:T(8,128)(2,1)} %param.3) | copy-start | bytes 3145732
  24.5 1.7 %copy-start = (bf16[2,160,4224]{2,1,0:T(8,128)(2,1)}, bf16[2,160,4224]{2,1,0:T(8,128)(2,1)S(1)}, u32[]{:S(2)}) copy-start(bf16[2,160,4224]{2,1,0:T(8,128)(2,1)S(1)} %fusion.5) | copy-start | bytes 8110084

commit v11 on v10

--- a/solution.py
+++ b/solution.py
@@ -166,7 +166,7 @@
 
 def joining(corner, taps, prior, depth_values, window, n_out, first_row, bounds, crop, out_shape):
     planes = taps.shape[0]
-    group = 16 if planes % 16 == 0 else planes
+    group = 32 if planes % 32 == 0 else planes
     _, window_rows, width = window.shape
     n_in = SPAN
     block_count = width // LANE - 1

time: 56.6 us -> 54.6 us (0.965)
  Pallas kernels: 28.3 us -> 26.3 us
    pallas_call x1, Pallas kernels: 20.2 us -> 18.2 us  [joining(): pl.pallas_call(body, grid_spec=grid_spec, out_shape=[jax.ShapeDtypeStruct...]
where the time goes in v11:
time: 54.6 us; the launch traced here: 54.2 us
  Pallas kernels  26.3 us (48%)
  starting transfers between devices  11.4 us (21%)
  waiting for transfers between devices  5.66 us (10%)
  local copies, waits for them, and re-layouts  5.29 us (10%)
  other arithmetic  4.84 us (9%)
  between operations  0.73 us (1%)
    pallas_call x1, Pallas kernels, joining(): pl.pallas_call(body, grid_spec=grid_spec, out_shape=[jax.ShapeDtypeStruct...  18.2 us
    pallas_call x1, Pallas kernels, propagate(): pl.pallas_call(body, grid=(planes,), in_specs=[pl.BlockSpec((1, 2, SPAN),...  8.14 us
    all_to_all x1, starting transfers between devices, gather_depth(): moved = lax.all_to_all(copies, 'depth', 0, 0)  5.81 us
    all_to_all x1, waiting for transfers between devices, gather_depth(): moved = lax.all_to_all(copies, 'depth', 0, 0)  5.65 us
    ppermute x1, starting transfers between devices, local(): lax.ppermute(hologram, 'tile', [(i + 1, i) for i in range(tile_count - 1)])  3.64 us
    ppermute x1, starting transfers between devices, local(): lax.ppermute(hologram, 'tile', [(i, i + 1) for i in range(tile_count - 1)])  1.92 us
    concatenate x1, other arithmetic, local(): jnp.concatenate([above[:, rows - halo:], hologram, below[:, :halo]], axis=1)  1.57 us
    broadcast_in_dim x1, local copies, waits for them, and re-layouts, local(): jnp.broadcast_to(prior_rows[:, :, None], prior_rows.shape + (LANE,))  1.49 us
  transfers between devices with their start and end apart: 3, of which 1 were waited for; matrix products, arithmetic and copies ran while one was open for 7% of the time, Pallas kernels for 0%

profile of v11, /device:TPU:4, one launch (start us, length us, event | category | flops | bytes accessed | tf_op | source)
XLA Modules:
  0.0 54.2 jit_solution(15339170162904886524)
XLA Ops:
  0.6 1.9 %collective-permute-start = (bf16[2,64,4096]{2,1,0:T(8,128)(2,1)}, bf16[2,64,4096]{2,1,0:T(8,128)(2,1)S(1)}, u32[]{:S(2)}, u32[]{:S(2)}) collective-permute-start(bf16[2,64,4096]{2,1,0:T(8,128)(2,1)} %param.3), channel_id=1, source_target_pairs={{0,1},{1,2},{2,3},{4,5},{5,6},{6,7},{8,9},{9,10},{10,11},{12,13},{... | collective-permute-start | bytes 3145736 | tf_op jit(solution)/shard_map/ppermute | solution.py:233
  2.6 3.6 %collective-permute-start.1 = (bf16[2,64,4096]{2,1,0:T(8,128)(2,1)}, bf16[2,64,4096]{2,1,0:T(8,128)(2,1)S(1)}, u32[]{:S(2)}, u32[]{:S(2)}) collective-permute-start(bf16[2,64,4096]{2,1,0:T(8,128)(2,1)} %param.3), channel_id=1, source_target_pairs={{1,0},{2,1},{3,2},{5,4},{6,5},{7,6},{9,8},{10,9},{11,10},{13,12},{... | collective-permute-start | bytes 3145736 | tf_op jit(solution)/shard_map/ppermute | solution.py:234
  6.2 1.3 %fusion.6 = (f32[1,4,2,256]{3,2,1,0:T(2,128)S(1)}, f32[4,2,256]{2,1,0:T(2,128)}) fusion(bf16[4,2,64]{2,1,0:T(2,128)(2,1)} %param.4), kind=kLoop, calls=%fused_computation.14 | loop fusion | flops 2048 | bytes 17408
  7.5 0.7 %pad_maximum_fusion = f32[4,576]{1,0:T(4,128)S(1)} fusion(f32[4,64]{1,0:T(4,128)} %param.5, f32[4,512]{1,0:T(4,128)S(1)} %bitcast.9), kind=kLoop, calls=%fused_computation.11 | loop fusion | flops 2304 | bytes 18432 | tf_op jit(solution)/shard_map/concatenate | solution.py:228
  8.2 0.6 %broadcast_in_dim.4 = f32[8,4,576]{2,1,0:T(4,128)} broadcast(f32[4,576]{1,0:T(4,128)S(1)} %pad_maximum_fusion), dimensions={1,2} | broadcast | bytes 82944 | tf_op jit(solution)/shard_map/broadcast_in_dim | solution.py:210
  8.8 5.8 %all-to-all-start = ((f32[8,4,576]{2,1,0:T(4,128)}), f32[8,4,576]{2,1,0:T(4,128)S(1)}, u32[]{:S(2)}, u32[]{:S(2)}) async-start(f32[8,4,576]{2,1,0:T(4,128)} %broadcast_in_dim.4), calls=%async_computation | async-start | bytes 163840 | tf_op jit(solution)/shard_map/all_to_all | solution.py:211
  14.6 0.1 copy.7
  14.7 0.6 %broadcast_multiply_fusion.depth_ref = f32[32,1,1]{2,1,0:T(1,128)} fusion(f32[32,1,1]{2,1,0:T(1,128)S(1)} %copy.7), kind=kLoop, calls=%fused_computation.12 | loop fusion | flops 32 | bytes 256 | tf_op jit(solution)/shard_map/div | solution.py:254
  15.4 0.6 %pad_add_fusion.corner_ref = s32[2]{0:T(128)} fusion(s32[1]{0:T(128)} %bitcast.2, s32[1]{0:T(128)} %bitcast.1), kind=kLoop, calls=%fused_computation.15 | loop fusion | flops 2 | bytes 16 | tf_op jit(solution)/shard_map/stack | solution.py:249
  16.0 5.7 %all-to-all-done = f32[8,4,576]{2,1,0:T(4,128)S(1)} async-done(((f32[8,4,576]{2,1,0:T(4,128)}), f32[8,4,576]{2,1,0:T(4,128)S(1)}, u32[]{:S(2)}, u32[]{:S(2)}) %all-to-all-start) | async-done | bytes 73760 | tf_op jit(solution)/shard_map/all_to_all | solution.py:211
  21.7 0.0 copy-start.2
  21.7 0.0 copy-start.1
  21.7 0.0 collective-permute-done
  21.7 0.1 slice.12
  21.8 0.0 collective-permute-done.1
  21.8 0.1 slice.13
  21.9 1.1 %copy-done.1 = bf16[2,64,4096]{2,1,0:T(8,128)(2,1)S(1)} copy-done((bf16[2,64,4096]{2,1,0:T(8,128)(2,1)S(1)}, bf16[2,64,4096]{2,1,0:T(8,128)(2,1)}, u32[]{:S(2)}) %copy-start.1) | copy-done | bytes 1048600
  23.0 1.6 %fusion.5 = bf16[2,160,4224]{2,1,0:T(8,128)(2,1)S(1)} fusion(bf16[2,48,4096]{2,1,0:T(8,128)(2,1)S(1)} %slice.13, bf16[2,64,4096]{2,1,0:T(8,128)(2,1)S(1)} %copy-done.1, bf16[2,48,4096]{2,1,0:T(8,128)(2,1)S(1)} %slice.12), kind=kLoop, calls=%fused_computation.8 | loop fusion | flops 16220160 | bytes 5324800 | tf_op jit(solution)/shard_map/concatenate | solution.py:235
  24.5 1.4 %pad_dynamic-slice_fusion = bf16[2,264,768]{2,1,0:T(8,128)(2,1)} fusion(s32[]{:T(128)S(6)} %select_n.3, bf16[2,160,4224]{2,1,0:T(8,128)(2,1)S(1)} %fusion.5), kind=kLoop, calls=%fused_computation.3 | loop fusion | bytes 3514372 | tf_op jit(solution)/shard_map/dynamic_slice | solution.py:248
  25.9 0.4 copy-done
  26.3 8.1 %shard_map.58 = f32[4,64,4096]{2,1,0:T(8,128)} custom-call(f32[4,2,256]{2,1,0:T(2,128)} %get-tuple-element.12.taps_ref, bf16[320,4224]{1,0:T(8,128)(2,1)} %bitcast.7), custom_call_target="tpu_custom_call" | custom-call | flops 3254779904 | bytes 6897664 | tf_op jit(solution)/shard_map/pallas_call | solution.py:150
  34.5 0.1 pad.21
  34.5 1.5 %broadcast_in_dim.5.prior_ref = f32[32,80,128]{2,1,0:T(8,128)} broadcast(f32[32,80]{1,0:T(8,128)S(1)} %pad.21), dimensions={0,1} | broadcast | bytes 1320960 | tf_op jit(solution)/shard_map/broadcast_in_dim | solution.py:256
  36.0 18.2 %shard_map.59 = (f32[64,512]{1,0:T(8,128)}, f32[64,512]{1,0:T(8,128)}) custom-call(s32[2]{0:T(128)} %pad_add_fusion.corner_ref, f32[32,576]{1,0:T(8,128)} %copy-done.2, f32[32,80,128]{2,1,0:T(8,128)} %broadcast_in_dim.5.prior_ref, f32[32,1,1]{2,1,0:T(1,128)} %broadcast_multiply_fusion.depth_ref, bf16[528,768]{1,0:T(8,128)(2,1)} %bitcast.8), custom_call_target="tpu_custom_call" | custom-call | flops 7381975040 | bytes 1220608 | tf_op jit(solution)/shard_map/pallas_call | solution.py:195
  (7 shorter events, 0.1 us)
Async XLA Ops:
  0.6 21.1 %collective-permute-start = (bf16[2,64,4096]{2,1,0:T(8,128)(2,1)}, bf16[2,64,4096]{2,1,0:T(8,128)(2,1)S(1)}, u32[]{:S(2)}, u32[]{:S(2)}) collective-permute-start(bf16[2,64,4096]{2,1,0:T(8,128)(2,1)} %param.3), channel_id=1, source_target_pairs={{0,1},{1,2},{2,3},{4,5},{5,6},{6,7},{8,9},{9,10},{10,11},{12,13},{... | collective-permute-start | bytes 3145736 | tf_op jit(solution)/shard_map/ppermute | solution.py:233
  2.6 19.2 %collective-permute-start.1 = (bf16[2,64,4096]{2,1,0:T(8,128)(2,1)}, bf16[2,64,4096]{2,1,0:T(8,128)(2,1)S(1)}, u32[]{:S(2)}, u32[]{:S(2)}) collective-permute-start(bf16[2,64,4096]{2,1,0:T(8,128)(2,1)} %param.3), channel_id=1, source_target_pairs={{1,0},{2,1},{3,2},{5,4},{6,5},{7,6},{9,8},{10,9},{11,10},{13,12},{... | collective-permute-start | bytes 3145736 | tf_op jit(solution)/shard_map/ppermute | solution.py:234
  8.8 12.8 %all-to-all-start = ((f32[8,4,576]{2,1,0:T(4,128)}), f32[8,4,576]{2,1,0:T(4,128)S(1)}, u32[]{:S(2)}, u32[]{:S(2)}) async-start(f32[8,4,576]{2,1,0:T(4,128)} %broadcast_in_dim.4), calls=%async_computation | async-start | bytes 163840 | tf_op jit(solution)/shard_map/all_to_all | solution.py:211
  21.7 12.8 %copy-start.2 = (f32[32,576]{1,0:T(8,128)}, f32[32,576]{1,0:T(8,128)S(1)}, u32[]{:S(2)}) copy-start(f32[32,576]{1,0:T(8,128)S(1)} %reshape.36.taps_ref) | copy-start | bytes 221188
  21.7 1.3 %copy-start.1 = (bf16[2,64,4096]{2,1,0:T(8,128)(2,1)S(1)}, bf16[2,64,4096]{2,1,0:T(8,128)(2,1)}, u32[]{:S(2)}) copy-start(bf16[2,64,4096]{2,1,0:T(8,128)(2,1)} %param.3) | copy-start | bytes 3145732
  24.5 1.7 %copy-start = (bf16[2,160,4224]{2,1,0:T(8,128)(2,1)}, bf16[2,160,4224]{2,1,0:T(8,128)(2,1)S(1)}, u32[]{:S(2)}) copy-start(bf16[2,160,4224]{2,1,0:T(8,128)(2,1)S(1)} %fusion.5) | copy-start | bytes 8110084

commit v12 on v11

--- a/solution.py
+++ b/solution.py
@@ -87,7 +87,7 @@
 
 
 def joining_kernel(
-    corner_ref, taps_ref, prior_ref, depth_ref, window_ref, joined_ref, mean_ref,
+    corner_ref, taps_ref, prior_ref, window_ref, joined_ref, mean_ref,
     total_ref, weighted_ref, placed_ref, *, n_out, n_in, block_count, bounds, crop, starts,
 ):
     step = pl.program_id(0)
@@ -122,7 +122,9 @@
         fresh = prior_ref[g][:, 0:1] * (1.0 + (grad_x * grad_x + grad_y * grad_y))
         total_ref[...] = total_ref[...] + fresh
         weighted_ref[...] = weighted_ref[...] + fresh * intensity
-        placed_ref[...] = placed_ref[...] + fresh * depth_ref[g]
+        plane = (step * len(skewed) + g).astype(jnp.float32)
+        depth_value = (plane + 0.5) / jnp.asarray(len(skewed) * pl.num_programs(0), jnp.float32)
+        placed_ref[...] = placed_ref[...] + fresh * depth_value
 
     @pl.when(step == pl.num_programs(0) - 1)
     def _():
@@ -164,7 +166,7 @@
     )(taps, stacked)
 
 
-def joining(corner, taps, prior, depth_values, window, n_out, first_row, bounds, crop, out_shape):
+def joining(corner, taps, prior, window, n_out, first_row, bounds, crop, out_shape):
     planes = taps.shape[0]
     group = 32 if planes % 32 == 0 else planes
     _, window_rows, width = window.shape
@@ -183,7 +185,6 @@
         in_specs=[
             pl.BlockSpec((group, taps.shape[1]), lambda p, c: (p, 0)),
             pl.BlockSpec((group, n_out, LANE), lambda p, c: (p, 0, 0)),
-            pl.BlockSpec((group, 1, 1), lambda p, c: (p, 0, 0)),
             pl.BlockSpec((2 * window_rows, width), lambda p, c: (0, 0)),
         ],
         out_specs=[
@@ -202,7 +203,7 @@
             transcendentals=0,
             bytes_accessed=stacked.size * 2 + 2 * n_out * out_cols * 4,
         ),
-    )(corner, taps, prior, depth_values, stacked)
+    )(corner, taps, prior, stacked)
 
 
 def gather_depth(block):
@@ -227,7 +228,6 @@
     taps = jnp.pad(kernel.astype(jnp.float32), ((0, 0), (0, 0), (0, SPAN - TAPS)))
     packed = jnp.concatenate([taps.reshape(local_planes, 2 * SPAN), depth_prior], axis=1)
     packed_all = gather_depth(packed)
-    plane_at = jnp.arange(planes_total)
 
     halo = 48
     above = lax.ppermute(hologram, "tile", [(i, i + 1) for i in range(tile_count - 1)])
@@ -251,10 +251,9 @@
     )
     prior_weight = jnp.exp(prior_all - jnp.max(prior_all, axis=0, keepdims=True))
     prior_rows = jnp.pad(prior_weight, ((0, 0), (lead_rows, lead_rows)), constant_values=1.0)
-    depth_values = ((plane_at.astype(jnp.float32) + 0.5) / planes_total)[:, None, None]
     joined, mean_depth = joining(
         corner, packed_all, jnp.broadcast_to(prior_rows[:, :, None], prior_rows.shape + (LANE,)),
-        depth_values, window, n_out, first,
+        window, n_out, first,
         (row_total, col_total), (lead_rows, LANE // 2), (rows, own_cols),
     )
     return (plane_stack, joined, mean_depth)

time: 54.6 us -> 54.6 us (level)
  waiting for transfers between devices: 5.66 us -> 6.43 us
  other arithmetic: 4.84 us -> 4.16 us
    all_to_all x1, waiting for transfers between devices: 5.65 us -> 6.42 us  [gather_depth(): moved = lax.all_to_all(copies, 'depth', 0, 0)]
    div x1 -> x0, other arithmetic: 0.62 us -> none  [local(): (plane_at.astype(jnp.float32) + 0.5) / planes_total]
  transfers between devices with their start and end apart: 3 -> 3, of which waited for: 1 -> 1; matrix products, arithmetic and copies ran while one was open for 7% -> 6% of each run, Pallas kernels for 0% -> 0%
where the time goes in v12:
time: 54.6 us; the launch traced here: 54.2 us
  Pallas kernels  26.3 us (48%)
  starting transfers between devices  11.4 us (21%)
  waiting for transfers between devices  6.43 us (12%)
  local copies, waits for them, and re-layouts  5.2 us (10%)
  other arithmetic  4.16 us (8%)
  between operations  0.73 us (1%)
    pallas_call x1, Pallas kernels, joining(): pl.pallas_call(body, grid_spec=grid_spec, out_shape=[jax.ShapeDtypeStruct...  18.2 us
    pallas_call x1, Pallas kernels, propagate(): pl.pallas_call(body, grid=(planes,), in_specs=[pl.BlockSpec((1, 2, SPAN),...  8.14 us
    all_to_all x1, waiting for transfers between devices, gather_depth(): moved = lax.all_to_all(copies, 'depth', 0, 0)  6.42 us
    all_to_all x1, starting transfers between devices, gather_depth(): moved = lax.all_to_all(copies, 'depth', 0, 0)  5.81 us
    ppermute x1, starting transfers between devices, local(): lax.ppermute(hologram, 'tile', [(i + 1, i) for i in range(tile_count - 1)])  3.64 us
    ppermute x1, starting transfers between devices, local(): lax.ppermute(hologram, 'tile', [(i, i + 1) for i in range(tile_count - 1)])  1.92 us
    concatenate x1, other arithmetic, local(): jnp.concatenate([above[:, rows - halo:], hologram, below[:, :halo]], axis=1)  1.57 us
    broadcast_in_dim x1, local copies, waits for them, and re-layouts, local(): jnp.broadcast_to(prior_rows[:, :, None], prior_rows.shape + (LANE,))  1.49 us
  transfers between devices with their start and end apart: 3, of which 1 were waited for; matrix products, arithmetic and copies ran while one was open for 6% of the time, Pallas kernels for 0%

profile of v12, /device:TPU:4, one launch (start us, length us, event | category | flops | bytes accessed | tf_op | source)
XLA Modules:
  0.0 54.2 jit_solution(7599325070543569541)
XLA Ops:
  0.6 1.9 %collective-permute-start = (bf16[2,64,4096]{2,1,0:T(8,128)(2,1)}, bf16[2,64,4096]{2,1,0:T(8,128)(2,1)S(1)}, u32[]{:S(2)}, u32[]{:S(2)}) collective-permute-start(bf16[2,64,4096]{2,1,0:T(8,128)(2,1)} %param.3), channel_id=1, source_target_pairs={{0,1},{1,2},{2,3},{4,5},{5,6},{6,7},{8,9},{9,10},{10,11},{12,13},{... | collective-permute-start | bytes 3145736 | tf_op jit(solution)/shard_map/ppermute | solution.py:233
  2.6 3.6 %collective-permute-start.1 = (bf16[2,64,4096]{2,1,0:T(8,128)(2,1)}, bf16[2,64,4096]{2,1,0:T(8,128)(2,1)S(1)}, u32[]{:S(2)}, u32[]{:S(2)}) collective-permute-start(bf16[2,64,4096]{2,1,0:T(8,128)(2,1)} %param.3), channel_id=1, source_target_pairs={{1,0},{2,1},{3,2},{5,4},{6,5},{7,6},{9,8},{10,9},{11,10},{13,12},{... | collective-permute-start | bytes 3145736 | tf_op jit(solution)/shard_map/ppermute | solution.py:234
  6.2 1.3 %fusion.6 = (f32[1,4,2,256]{3,2,1,0:T(2,128)S(1)}, f32[4,2,256]{2,1,0:T(2,128)}) fusion(bf16[4,2,64]{2,1,0:T(2,128)(2,1)} %param.4), kind=kLoop, calls=%fused_computation.13 | loop fusion | flops 2048 | bytes 17408
  7.5 0.7 %pad_maximum_fusion = f32[4,576]{1,0:T(4,128)S(1)} fusion(f32[4,64]{1,0:T(4,128)} %param.5, f32[4,512]{1,0:T(4,128)S(1)} %bitcast.9), kind=kLoop, calls=%fused_computation.11 | loop fusion | flops 2304 | bytes 18432 | tf_op jit(solution)/shard_map/concatenate | solution.py:229
  8.2 0.6 %broadcast_in_dim.4 = f32[8,4,576]{2,1,0:T(4,128)} broadcast(f32[4,576]{1,0:T(4,128)S(1)} %pad_maximum_fusion), dimensions={1,2} | broadcast | bytes 82944 | tf_op jit(solution)/shard_map/broadcast_in_dim | solution.py:211
  8.8 5.8 %all-to-all-start = ((f32[8,4,576]{2,1,0:T(4,128)}), f32[8,4,576]{2,1,0:T(4,128)S(1)}, u32[]{:S(2)}, u32[]{:S(2)}) async-start(f32[8,4,576]{2,1,0:T(4,128)} %broadcast_in_dim.4), calls=%async_computation | async-start | bytes 163840 | tf_op jit(solution)/shard_map/all_to_all | solution.py:212
  14.6 0.6 %pad_add_fusion.corner_ref = s32[2]{0:T(128)} fusion(s32[1]{0:T(128)} %bitcast.2, s32[1]{0:T(128)} %bitcast.1), kind=kLoop, calls=%fused_computation.14 | loop fusion | flops 2 | bytes 16 | tf_op jit(solution)/shard_map/stack | solution.py:249
  15.2 6.4 %all-to-all-done = f32[8,4,576]{2,1,0:T(4,128)S(1)} async-done(((f32[8,4,576]{2,1,0:T(4,128)}), f32[8,4,576]{2,1,0:T(4,128)S(1)}, u32[]{:S(2)}, u32[]{:S(2)}) %all-to-all-start) | async-done | bytes 73760 | tf_op jit(solution)/shard_map/all_to_all | solution.py:212
  21.7 0.0 copy-start.2
  21.7 0.0 copy-start.1
  21.7 0.0 collective-permute-done
  21.7 0.1 slice.12
  21.8 0.0 collective-permute-done.1
  21.8 0.1 slice.13
  21.9 1.1 %copy-done.1 = bf16[2,64,4096]{2,1,0:T(8,128)(2,1)S(1)} copy-done((bf16[2,64,4096]{2,1,0:T(8,128)(2,1)S(1)}, bf16[2,64,4096]{2,1,0:T(8,128)(2,1)}, u32[]{:S(2)}) %copy-start.1) | copy-done | bytes 1048600
  23.0 1.6 %fusion.5 = bf16[2,160,4224]{2,1,0:T(8,128)(2,1)S(1)} fusion(bf16[2,48,4096]{2,1,0:T(8,128)(2,1)S(1)} %slice.13, bf16[2,64,4096]{2,1,0:T(8,128)(2,1)S(1)} %copy-done.1, bf16[2,48,4096]{2,1,0:T(8,128)(2,1)S(1)} %slice.12), kind=kLoop, calls=%fused_computation.8 | loop fusion | flops 16220160 | bytes 5324800 | tf_op jit(solution)/shard_map/concatenate | solution.py:235
  24.5 0.0 copy-start
  24.5 1.4 %pad_dynamic-slice_fusion = bf16[2,264,768]{2,1,0:T(8,128)(2,1)} fusion(s32[]{:T(128)S(6)} %select_n.3, bf16[2,160,4224]{2,1,0:T(8,128)(2,1)S(1)} %fusion.5), kind=kLoop, calls=%fused_computation.3 | loop fusion | bytes 3514372 | tf_op jit(solution)/shard_map/dynamic_slice | solution.py:248
  25.9 0.4 copy-done
  26.3 8.1 %shard_map.58 = f32[4,64,4096]{2,1,0:T(8,128)} custom-call(f32[4,2,256]{2,1,0:T(2,128)} %get-tuple-element.12.taps_ref, bf16[320,4224]{1,0:T(8,128)(2,1)} %bitcast.7), custom_call_target="tpu_custom_call" | custom-call | flops 3254779904 | bytes 6897664 | tf_op jit(solution)/shard_map/pallas_call | solution.py:152
  34.4 0.0 copy-done.2
  34.5 0.1 pad.21
  34.5 1.5 %broadcast_in_dim.5.prior_ref = f32[32,80,128]{2,1,0:T(8,128)} broadcast(f32[32,80]{1,0:T(8,128)S(1)} %pad.21), dimensions={0,1} | broadcast | bytes 1320960 | tf_op jit(solution)/shard_map/broadcast_in_dim | solution.py:255
  36.0 18.2 %shard_map.59 = (f32[64,512]{1,0:T(8,128)}, f32[64,512]{1,0:T(8,128)}) custom-call(s32[2]{0:T(128)} %pad_add_fusion.corner_ref, f32[32,576]{1,0:T(8,128)} %copy-done.2, f32[32,80,128]{2,1,0:T(8,128)} %broadcast_in_dim.5.prior_ref, bf16[528,768]{1,0:T(8,128)(2,1)} %bitcast.8), custom_call_target="tpu_custom_call" | custom-call | flops 7381975040 | bytes 1220608 | tf_op jit(solution)/shard_map/pallas_call | solution.py:196
  (4 shorter events, 0.1 us)
Async XLA Ops:
  0.6 21.1 %collective-permute-start = (bf16[2,64,4096]{2,1,0:T(8,128)(2,1)}, bf16[2,64,4096]{2,1,0:T(8,128)(2,1)S(1)}, u32[]{:S(2)}, u32[]{:S(2)}) collective-permute-start(bf16[2,64,4096]{2,1,0:T(8,128)(2,1)} %param.3), channel_id=1, source_target_pairs={{0,1},{1,2},{2,3},{4,5},{5,6},{6,7},{8,9},{9,10},{10,11},{12,13},{... | collective-permute-start | bytes 3145736 | tf_op jit(solution)/shard_map/ppermute | solution.py:233
  2.6 19.2 %collective-permute-start.1 = (bf16[2,64,4096]{2,1,0:T(8,128)(2,1)}, bf16[2,64,4096]{2,1,0:T(8,128)(2,1)S(1)}, u32[]{:S(2)}, u32[]{:S(2)}) collective-permute-start(bf16[2,64,4096]{2,1,0:T(8,128)(2,1)} %param.3), channel_id=1, source_target_pairs={{1,0},{2,1},{3,2},{5,4},{6,5},{7,6},{9,8},{10,9},{11,10},{13,12},{... | collective-permute-start | bytes 3145736 | tf_op jit(solution)/shard_map/ppermute | solution.py:234
  8.8 12.8 %all-to-all-start = ((f32[8,4,576]{2,1,0:T(4,128)}), f32[8,4,576]{2,1,0:T(4,128)S(1)}, u32[]{:S(2)}, u32[]{:S(2)}) async-start(f32[8,4,576]{2,1,0:T(4,128)} %broadcast_in_dim.4), calls=%async_computation | async-start | bytes 163840 | tf_op jit(solution)/shard_map/all_to_all | solution.py:212
  21.7 12.8 %copy-start.2 = (f32[32,576]{1,0:T(8,128)}, f32[32,576]{1,0:T(8,128)S(1)}, u32[]{:S(2)}) copy-start(f32[32,576]{1,0:T(8,128)S(1)} %reshape.23.taps_ref) | copy-start | bytes 221188
  21.7 1.3 %copy-start.1 = (bf16[2,64,4096]{2,1,0:T(8,128)(2,1)S(1)}, bf16[2,64,4096]{2,1,0:T(8,128)(2,1)}, u32[]{:S(2)}) copy-start(bf16[2,64,4096]{2,1,0:T(8,128)(2,1)} %param.3) | copy-start | bytes 3145732
  24.5 1.7 %copy-start = (bf16[2,160,4224]{2,1,0:T(8,128)(2,1)}, bf16[2,160,4224]{2,1,0:T(8,128)(2,1)S(1)}, u32[]{:S(2)}) copy-start(bf16[2,160,4224]{2,1,0:T(8,128)(2,1)S(1)} %fusion.5) | copy-start | bytes 8110084

commit v13 on v11

--- a/solution.py
+++ b/solution.py
@@ -138,6 +138,7 @@
 
 def propagate(taps, window, n_out, first_row):
     planes = taps.shape[0]
+    pair = 2 if planes % 2 == 0 else 1
     _, window_rows, width = window.shape
     n_in = n_out + TAPS
     block_count = width // LANE - 1
@@ -149,12 +150,12 @@
     flops = 2 * planes * (2 * n_out * 2 * n_in * width + block_count * n_out * 4 * LANE * SPAN)
     return pl.pallas_call(
         body,
-        grid=(planes,),
+        grid=(planes // pair,),
         in_specs=[
-            pl.BlockSpec((1, 2, SPAN), lambda p: (p, 0, 0)),
+            pl.BlockSpec((pair, 2, SPAN), lambda p: (p, 0, 0)),
             pl.BlockSpec((2 * window_rows, width), lambda p: (0, 0)),
         ],
-        out_specs=pl.BlockSpec((1, n_out, block_count * LANE), lambda p: (p, 0, 0)),
+        out_specs=pl.BlockSpec((pair, n_out, block_count * LANE), lambda p: (p, 0, 0)),
         out_shape=jax.ShapeDtypeStruct((planes, n_out, block_count * LANE), jnp.float32),
         cost_estimate=pl.CostEstimate(
             flops=flops,

time: 54.6 us -> 54.5 us (level)
  transfers between devices with their start and end apart: 3 -> 3, of which waited for: 1 -> 1; matrix products, arithmetic and copies ran while one was open for 7% -> 8% of each run, Pallas kernels for 0% -> 0%
where the time goes in v13:
time: 54.5 us; the launch traced here: 54.1 us
  Pallas kernels  26.2 us (48%)
  starting transfers between devices  11.4 us (21%)
  waiting for transfers between devices  5.66 us (10%)
  local copies, waits for them, and re-layouts  5.29 us (10%)
  other arithmetic  4.84 us (9%)
  between operations  0.73 us (1%)
    pallas_call x1, Pallas kernels, joining(): pl.pallas_call(body, grid_spec=grid_spec, out_shape=[jax.ShapeDtypeStruct...  18.2 us
    pallas_call x1, Pallas kernels, propagate(): pl.pallas_call(body, grid=(planes // pair,), in_specs=[pl.BlockSpec((pair...  7.97 us
    all_to_all x1, starting transfers between devices, gather_depth(): moved = lax.all_to_all(copies, 'depth', 0, 0)  5.81 us
    all_to_all x1, waiting for transfers between devices, gather_depth(): moved = lax.all_to_all(copies, 'depth', 0, 0)  5.65 us
    ppermute x1, starting transfers between devices, local(): lax.ppermute(hologram, 'tile', [(i + 1, i) for i in range(tile_count - 1)])  3.64 us
    ppermute x1, starting transfers between devices, local(): lax.ppermute(hologram, 'tile', [(i, i + 1) for i in range(tile_count - 1)])  1.92 us
    concatenate x1, other arithmetic, local(): jnp.concatenate([above[:, rows - halo:], hologram, below[:, :halo]], axis=1)  1.57 us
    broadcast_in_dim x1, local copies, waits for them, and re-layouts, local(): jnp.broadcast_to(prior_rows[:, :, None], prior_rows.shape + (LANE,))  1.49 us
  transfers between devices with their start and end apart: 3, of which 1 were waited for; matrix products, arithmetic and copies ran while one was open for 8% of the time, Pallas kernels for 0%

profile of v13, /device:TPU:4, one launch (start us, length us, event | category | flops | bytes accessed | tf_op | source)
XLA Modules:
  0.0 54.1 jit_solution(127217689513294103)
XLA Ops:
  0.6 1.9 %collective-permute-start = (bf16[2,64,4096]{2,1,0:T(8,128)(2,1)}, bf16[2,64,4096]{2,1,0:T(8,128)(2,1)S(1)}, u32[]{:S(2)}, u32[]{:S(2)}) collective-permute-start(bf16[2,64,4096]{2,1,0:T(8,128)(2,1)} %param.3), channel_id=1, source_target_pairs={{0,1},{1,2},{2,3},{4,5},{5,6},{6,7},{8,9},{9,10},{10,11},{12,13},{... | collective-permute-start | bytes 3145736 | tf_op jit(solution)/shard_map/ppermute | solution.py:234
  2.6 3.6 %collective-permute-start.1 = (bf16[2,64,4096]{2,1,0:T(8,128)(2,1)}, bf16[2,64,4096]{2,1,0:T(8,128)(2,1)S(1)}, u32[]{:S(2)}, u32[]{:S(2)}) collective-permute-start(bf16[2,64,4096]{2,1,0:T(8,128)(2,1)} %param.3), channel_id=1, source_target_pairs={{1,0},{2,1},{3,2},{5,4},{6,5},{7,6},{9,8},{10,9},{11,10},{13,12},{... | collective-permute-start | bytes 3145736 | tf_op jit(solution)/shard_map/ppermute | solution.py:235
  6.2 1.3 %fusion.6 = (f32[1,4,2,256]{3,2,1,0:T(2,128)S(1)}, f32[4,2,256]{2,1,0:T(2,128)}) fusion(bf16[4,2,64]{2,1,0:T(2,128)(2,1)} %param.4), kind=kLoop, calls=%fused_computation.14 | loop fusion | flops 2048 | bytes 17408
  7.5 0.7 %pad_maximum_fusion = f32[4,576]{1,0:T(4,128)S(1)} fusion(f32[4,64]{1,0:T(4,128)} %param.5, f32[4,512]{1,0:T(4,128)S(1)} %bitcast.9), kind=kLoop, calls=%fused_computation.11 | loop fusion | flops 2304 | bytes 18432 | tf_op jit(solution)/shard_map/concatenate | solution.py:229
  8.2 0.6 %broadcast_in_dim.4 = f32[8,4,576]{2,1,0:T(4,128)} broadcast(f32[4,576]{1,0:T(4,128)S(1)} %pad_maximum_fusion), dimensions={1,2} | broadcast | bytes 82944 | tf_op jit(solution)/shard_map/broadcast_in_dim | solution.py:211
  8.8 5.8 %all-to-all-start = ((f32[8,4,576]{2,1,0:T(4,128)}), f32[8,4,576]{2,1,0:T(4,128)S(1)}, u32[]{:S(2)}, u32[]{:S(2)}) async-start(f32[8,4,576]{2,1,0:T(4,128)} %broadcast_in_dim.4), calls=%async_computation | async-start | bytes 163840 | tf_op jit(solution)/shard_map/all_to_all | solution.py:212
  14.6 0.1 copy.7
  14.7 0.6 %broadcast_multiply_fusion.depth_ref = f32[32,1,1]{2,1,0:T(1,128)} fusion(f32[32,1,1]{2,1,0:T(1,128)S(1)} %copy.7), kind=kLoop, calls=%fused_computation.12 | loop fusion | flops 32 | bytes 256 | tf_op jit(solution)/shard_map/div | solution.py:255
  15.4 0.6 %pad_add_fusion.corner_ref = s32[2]{0:T(128)} fusion(s32[1]{0:T(128)} %bitcast.2, s32[1]{0:T(128)} %bitcast.1), kind=kLoop, calls=%fused_computation.15 | loop fusion | flops 2 | bytes 16 | tf_op jit(solution)/shard_map/stack | solution.py:250
  16.0 5.7 %all-to-all-done = f32[8,4,576]{2,1,0:T(4,128)S(1)} async-done(((f32[8,4,576]{2,1,0:T(4,128)}), f32[8,4,576]{2,1,0:T(4,128)S(1)}, u32[]{:S(2)}, u32[]{:S(2)}) %all-to-all-start) | async-done | bytes 73760 | tf_op jit(solution)/shard_map/all_to_all | solution.py:212
  21.7 0.0 copy-start.1
  21.7 0.0 collective-permute-done
  21.7 0.1 slice.12
  21.8 0.0 collective-permute-done.1
  21.8 0.1 slice.13
  21.9 1.1 %copy-done.1 = bf16[2,64,4096]{2,1,0:T(8,128)(2,1)S(1)} copy-done((bf16[2,64,4096]{2,1,0:T(8,128)(2,1)S(1)}, bf16[2,64,4096]{2,1,0:T(8,128)(2,1)}, u32[]{:S(2)}) %copy-start.1) | copy-done | bytes 1048600
  23.0 1.6 %fusion.5 = bf16[2,160,4224]{2,1,0:T(8,128)(2,1)S(1)} fusion(bf16[2,48,4096]{2,1,0:T(8,128)(2,1)S(1)} %slice.13, bf16[2,64,4096]{2,1,0:T(8,128)(2,1)S(1)} %copy-done.1, bf16[2,48,4096]{2,1,0:T(8,128)(2,1)S(1)} %slice.12), kind=kLoop, calls=%fused_computation.8 | loop fusion | flops 16220160 | bytes 5324800 | tf_op jit(solution)/shard_map/concatenate | solution.py:236
  24.5 1.4 %pad_dynamic-slice_fusion = bf16[2,264,768]{2,1,0:T(8,128)(2,1)} fusion(s32[]{:T(128)S(6)} %select_n.3, bf16[2,160,4224]{2,1,0:T(8,128)(2,1)S(1)} %fusion.5), kind=kLoop, calls=%fused_computation.3 | loop fusion | bytes 3514372 | tf_op jit(solution)/shard_map/dynamic_slice | solution.py:249
  25.9 0.4 copy-done
  26.3 8.0 %shard_map.58 = f32[4,64,4096]{2,1,0:T(8,128)} custom-call(f32[4,2,256]{2,1,0:T(2,128)} %get-tuple-element.12.taps_ref, bf16[320,4224]{1,0:T(8,128)(2,1)} %bitcast.7), custom_call_target="tpu_custom_call" | custom-call | flops 3254779904 | bytes 6897664 | tf_op jit(solution)/shard_map/pallas_call | solution.py:151
  34.3 0.0 copy-done.2
  34.3 0.1 pad.21
  34.4 1.5 %broadcast_in_dim.5.prior_ref = f32[32,80,128]{2,1,0:T(8,128)} broadcast(f32[32,80]{1,0:T(8,128)S(1)} %pad.21), dimensions={0,1} | broadcast | bytes 1320960 | tf_op jit(solution)/shard_map/broadcast_in_dim | solution.py:257
  35.9 18.2 %shard_map.59 = (f32[64,512]{1,0:T(8,128)}, f32[64,512]{1,0:T(8,128)}) custom-call(s32[2]{0:T(128)} %pad_add_fusion.corner_ref, f32[32,576]{1,0:T(8,128)} %copy-done.2, f32[32,80,128]{2,1,0:T(8,128)} %broadcast_in_dim.5.prior_ref, f32[32,1,1]{2,1,0:T(1,128)} %broadcast_multiply_fusion.depth_ref, bf16[528,768]{1,0:T(8,128)(2,1)} %bitcast.8), custom_call_target="tpu_custom_call" | custom-call | flops 7381975040 | bytes 1220608 | tf_op jit(solution)/shard_map/pallas_call | solution.py:196
  (7 shorter events, 0.1 us)
Async XLA Ops:
  0.6 21.1 %collective-permute-start = (bf16[2,64,4096]{2,1,0:T(8,128)(2,1)}, bf16[2,64,4096]{2,1,0:T(8,128)(2,1)S(1)}, u32[]{:S(2)}, u32[]{:S(2)}) collective-permute-start(bf16[2,64,4096]{2,1,0:T(8,128)(2,1)} %param.3), channel_id=1, source_target_pairs={{0,1},{1,2},{2,3},{4,5},{5,6},{6,7},{8,9},{9,10},{10,11},{12,13},{... | collective-permute-start | bytes 3145736 | tf_op jit(solution)/shard_map/ppermute | solution.py:234
  2.6 19.2 %collective-permute-start.1 = (bf16[2,64,4096]{2,1,0:T(8,128)(2,1)}, bf16[2,64,4096]{2,1,0:T(8,128)(2,1)S(1)}, u32[]{:S(2)}, u32[]{:S(2)}) collective-permute-start(bf16[2,64,4096]{2,1,0:T(8,128)(2,1)} %param.3), channel_id=1, source_target_pairs={{1,0},{2,1},{3,2},{5,4},{6,5},{7,6},{9,8},{10,9},{11,10},{13,12},{... | collective-permute-start | bytes 3145736 | tf_op jit(solution)/shard_map/ppermute | solution.py:235
  8.8 12.8 %all-to-all-start = ((f32[8,4,576]{2,1,0:T(4,128)}), f32[8,4,576]{2,1,0:T(4,128)S(1)}, u32[]{:S(2)}, u32[]{:S(2)}) async-start(f32[8,4,576]{2,1,0:T(4,128)} %broadcast_in_dim.4), calls=%async_computation | async-start | bytes 163840 | tf_op jit(solution)/shard_map/all_to_all | solution.py:212
  21.7 12.6 %copy-start.2 = (f32[32,576]{1,0:T(8,128)}, f32[32,576]{1,0:T(8,128)S(1)}, u32[]{:S(2)}) copy-start(f32[32,576]{1,0:T(8,128)S(1)} %reshape.36.taps_ref) | copy-start | bytes 221188
  21.7 1.3 %copy-start.1 = (bf16[2,64,4096]{2,1,0:T(8,128)(2,1)S(1)}, bf16[2,64,4096]{2,1,0:T(8,128)(2,1)}, u32[]{:S(2)}) copy-start(bf16[2,64,4096]{2,1,0:T(8,128)(2,1)} %param.3) | copy-start | bytes 3145732
  24.5 1.7 %copy-start = (bf16[2,160,4224]{2,1,0:T(8,128)(2,1)}, bf16[2,160,4224]{2,1,0:T(8,128)(2,1)S(1)}, u32[]{:S(2)}) copy-start(bf16[2,160,4224]{2,1,0:T(8,128)(2,1)S(1)} %fusion.5) | copy-start | bytes 8110084
